TPU v7x, 256 devices: a whole 4x4x8 slice. The times are simulated.
256 devices in a mesh: dp: 16 (over z, core), seq: 16 (over y, x).
Axes of the slice: x: 4, y: 4, z: 8, core: 2. Of those that a mesh axis runs over, the one named last changes fastest.
Arguments:
- clean_frames: bfloat16 [16, 2048, 1024], P('dp', 'seq')
- noise_frames: bfloat16 [16, 2048, 1024], P('dp', 'seq'), may hold values from -6 to 6
- lengths: int32 [16], P('dp'), may hold values from 512 to 2048
- group_ids: int32 [16, 2048], P('dp'), may hold values from 0 to 255, never falling along the last dimension, each value on 1 to 25 neighbouring positions
- time_index: int32 [16], P('dp'), may hold values from 0 to 999
- modulation: float32 [1024], replicated, may hold values from -4 to 4
- teacher_qkv: bfloat16 [1024, 3072], replicated, may hold values from -0.1875 to 0.1875
- teacher_out: bfloat16 [1024, 1024], replicated, may hold values from -6 to 6
- student_in: bfloat16 [3, 1024, 1024], P(None, ('dp', 'seq')), may hold values from -0.1875 to 0.1875
- student_out: bfloat16 [1024, 1024], P(('dp', 'seq')), may hold values from -1 to 1
Outputs:
- grad_inputs: float32 [2, 1024, 1024], P(None, ('dp', 'seq'))
- mean_error: float32 [], replicated
Inputs may be any that keep to these rules, and one draw needn't show every extreme that they name: `group_ids`: group numbers never fall along a dialogue, and each group holds 1 to 25 frames.
All inputs are finite; a program needn't handle non-finite values.
Results may differ from a plain program's by a relative error of at most 0.015.
Values may be sent and summed in bfloat16 or wider, within the bound.
No kernel may reach another device: no remote copies, remote signals or barrier semaphores. Data moves between devices by JAX's collectives and lax.ppermute only.
A program may use at most 128 MiB of HBM per device.

v0:
```python
import jax
import jax.numpy as jnp
from jax import lax
from jax.sharding import PartitionSpec as P

HEADS = 16
HALO = 64
TSTEPS = 1000


EPSILON = 1e-06
NEGATIVE = -1e30


def with_halo(block, sides, width):
    for axis, dim in sides:
        count = lax.axis_size(axis)
        forward = [(i, i + 1) for i in range(count - 1)]
        backward = [(target, source) for source, target in forward]
        low = lax.ppermute(
            lax.slice_in_dim(block, block.shape[dim] - width, None, axis=dim), axis, forward
        )
        high = lax.ppermute(lax.slice_in_dim(block, 0, width, axis=dim), axis, backward)
        block = jnp.concatenate([low, block, high], axis=dim)
    return block


def from_behind(block, axis, distance):
    devices = range(lax.axis_size(axis))
    route = [(i - distance, i) for i in devices if i - distance in devices]
    return lax.ppermute(block, axis, route)


def normalize(clean_frames, noise_frames, time_index, modulation):
    flow_time = (time_index.astype(jnp.float32) + 0.5) / TSTEPS
    flow_time = flow_time[:, None, None]
    blended = (1.0 - flow_time) * noise_frames.astype(
        jnp.float32
    ) + flow_time * clean_frames.astype(jnp.float32)
    inv_rms = lax.rsqrt(jnp.mean(blended * blended, axis=-1, keepdims=True) + EPSILON)
    return (blended * inv_rms * (1.0 + flow_time * modulation)).astype(jnp.bfloat16)


def attend_block(queries, key_rows, values, key_bias):
    scores = jnp.dot(queries, key_rows.T, preferred_element_type=jnp.float32) * queries.shape[
        -1
    ] ** (-0.5)
    scores = scores + key_bias[None, :]
    row_max = jnp.max(scores, axis=-1, keepdims=True)
    exponent = jnp.exp(scores - row_max)
    probs_low = (exponent / jnp.sum(exponent, axis=-1, keepdims=True)).astype(jnp.bfloat16)
    return jnp.dot(probs_low, values, preferred_element_type=jnp.float32).astype(jnp.bfloat16)


def full_attention(queries, key_rows, values, key_bias):
    total_rows = queries.shape[0]
    block_rows = min(512, total_rows)
    blocked = queries.reshape(total_rows // block_rows, block_rows, queries.shape[1])
    result = lax.map(lambda piece: attend_block(piece, key_rows, values, key_bias), blocked)
    return result.reshape(total_rows, values.shape[1])


def teacher_heads(proj_one, bias_one):
    stacked = jnp.transpose(proj_one, (2, 1, 0, 3))
    result = lax.map(
        lambda element: full_attention(element[0], element[1], element[2], bias_one), stacked
    )
    return jnp.transpose(result, (1, 0, 2))


def build_allowed(query_group, query_pos, key_group, key_pos, lengths):
    same_group = key_group[:, None, :] == query_group[:, :, None]
    prev_group = key_group[:, None, :] == query_group[:, :, None] - 1
    live_key = (key_pos[None, :] < lengths[:, None]) & (key_pos[None, :] >= 0)
    itself = key_pos[None, :] == query_pos[:, None]
    return (same_group | prev_group) & (live_key[:, None, :] | itself[None])


def split_product(form, gradient, other, first):
    upper_part = gradient.astype(jnp.bfloat16)
    lower_part = (gradient - upper_part.astype(jnp.float32)).astype(jnp.bfloat16)
    if first:
        return jnp.einsum(form, upper_part, other, preferred_element_type=jnp.float32) + jnp.einsum(
            form, lower_part, other, preferred_element_type=jnp.float32
        )
    return jnp.einsum(form, other, upper_part, preferred_element_type=jnp.float32) + jnp.einsum(
        form, other, lower_part, preferred_element_type=jnp.float32
    )


def shards(
    clean_frames,
    noise_frames,
    lengths,
    group_ids,
    time_index,
    modulation,
    teacher_qkv,
    teacher_out,
    student_in,
    student_out,
):
    dialogs, shard_rows, model_width = clean_frames.shape
    head_dim = model_width // HEADS
    seq_count = lax.axis_size("seq")
    seq_index = lax.axis_index("seq")
    frames = shard_rows * seq_count
    window = shard_rows + 2 * HALO
    w_inputs, w_output = (
        lax.all_gather(student_in, ("dp", "seq"), axis=1, tiled=True),
        lax.all_gather(student_out, ("dp", "seq"), axis=0, tiled=True),
    )
    normed = normalize(clean_frames, noise_frames, time_index, modulation)
    flat_rows = normed.reshape(dialogs * shard_rows, model_width)
    frame_pos = jnp.arange(frames, dtype=jnp.int32)
    key_bias = jnp.where(frame_pos[None, :] < lengths[:, None], 0.0, NEGATIVE).astype(jnp.float32)
    teacher_proj = jnp.dot(flat_rows, teacher_qkv, preferred_element_type=jnp.float32).astype(
        jnp.bfloat16
    )
    teacher_proj = teacher_proj.reshape(dialogs, shard_rows, 3, HEADS, head_dim)
    by_heads = lax.all_to_all(teacher_proj, "seq", split_axis=3, concat_axis=1, tiled=True)
    head_out = lax.map(lambda element: teacher_heads(element[0], element[1]), (by_heads, key_bias))
    by_frames = lax.all_to_all(head_out, "seq", split_axis=1, concat_axis=2, tiled=True)
    teacher_vel = jnp.dot(
        by_frames.reshape(dialogs * shard_rows, model_width),
        teacher_out,
        preferred_element_type=jnp.float32,
    )
    offset = seq_index * shard_rows
    queries = jnp.dot(flat_rows, w_inputs[0], preferred_element_type=jnp.float32).astype(
        jnp.bfloat16
    )
    queries = queries.reshape(dialogs, shard_rows, HEADS, head_dim)
    key_local = jnp.dot(flat_rows, w_inputs[1], preferred_element_type=jnp.float32).astype(
        jnp.bfloat16
    )
    value_local = jnp.dot(flat_rows, w_inputs[2], preferred_element_type=jnp.float32).astype(
        jnp.bfloat16
    )
    both_local = jnp.concatenate((key_local, value_local), axis=-1).reshape(
        dialogs, shard_rows, 2 * model_width
    )
    both_window = with_halo(both_local, (("seq", 1),), HALO)
    key_rows = both_window[:, :, :model_width].reshape(dialogs, window, HEADS, head_dim)
    value_rows = both_window[:, :, model_width:].reshape(dialogs, window, HEADS, head_dim)
    group_pad = jnp.pad(group_ids, ((0, 0), (HALO, HALO)), constant_values=-10)
    key_group = lax.dynamic_slice_in_dim(group_pad, offset, window, 1)
    query_group = lax.dynamic_slice_in_dim(group_ids, offset, shard_rows, 1)
    query_pos = offset + jnp.arange(shard_rows, dtype=jnp.int32)
    key_pos = offset - HALO + jnp.arange(window, dtype=jnp.int32)
    allowed = build_allowed(query_group, query_pos, key_group, key_pos, lengths)
    scaling = head_dim ** (-0.5)
    scores = jnp.einsum("brhd,bwhd->bhrw", queries, key_rows, preferred_element_type=jnp.float32)
    scores = jnp.where(allowed[:, None], scores * scaling, NEGATIVE)
    row_max = jnp.max(scores, axis=-1, keepdims=True)
    exponent = jnp.exp(scores - row_max)
    probs = exponent / jnp.sum(exponent, axis=-1, keepdims=True)
    probs_low = probs.astype(jnp.bfloat16)
    student_mix = jnp.einsum(
        "bhrw,bwhd->brhd", probs_low, value_rows, preferred_element_type=jnp.float32
    ).astype(jnp.bfloat16)
    mix_flat = student_mix.reshape(dialogs * shard_rows, model_width)
    student_vel = jnp.dot(mix_flat, w_output, preferred_element_type=jnp.float32)
    query_valid = (query_pos[None, :] < lengths[:, None]).reshape(-1)
    difference = jnp.where(query_valid[:, None], student_vel - teacher_vel, 0.0)
    square_sum, frame_count = lax.psum(
        (jnp.sum(difference * difference), jnp.sum(query_valid.astype(jnp.float32))), ("dp", "seq")
    )
    mean_error = square_sum / (frame_count * model_width)
    grad_vel = (difference * lax.rsqrt(frame_count)).astype(jnp.bfloat16)
    grad_mix = jnp.dot(grad_vel, w_output.T, preferred_element_type=jnp.float32).astype(
        jnp.bfloat16
    )
    grad_mix = grad_mix.reshape(dialogs, shard_rows, HEADS, head_dim)
    grad_prob = jnp.einsum(
        "brhd,bwhd->bhrw", grad_mix, value_rows, preferred_element_type=jnp.float32
    )
    grad_score = probs * (grad_prob - jnp.sum(probs * grad_prob, axis=-1, keepdims=True)) * scaling
    grad_key = split_product("bhrw,brhd->bwhd", grad_score, queries, True)
    grad_value = jnp.einsum(
        "bhrw,brhd->bwhd", probs_low, grad_mix, preferred_element_type=jnp.float32
    )
    grad_both = jnp.concatenate(
        (
            grad_key.reshape(dialogs, window, model_width),
            grad_value.reshape(dialogs, window, model_width),
        ),
        axis=-1,
    )
    from_next = from_behind(grad_both[:, :HALO].astype(jnp.bfloat16), "seq", -1).astype(jnp.float32)
    from_prev = from_behind(
        grad_both[:, HALO + shard_rows :].astype(jnp.bfloat16), "seq", 1
    ).astype(jnp.float32)
    owned_rows = grad_both[:, HALO : HALO + shard_rows]
    owned_rows = owned_rows.at[:, :HALO].add(from_prev)
    owned_rows = owned_rows.at[:, shard_rows - HALO :].add(from_next)
    owned_flat = owned_rows.reshape(dialogs * shard_rows, 2 * model_width)
    grad_kv_weight = split_product("rf,rg->fg", owned_flat, flat_rows, False)
    grad_stack = jnp.stack((grad_kv_weight[:, :model_width], grad_kv_weight[:, model_width:]))
    grad_inputs = lax.psum_scatter(grad_stack, ("dp", "seq"), scatter_dimension=1, tiled=True)
    return (grad_inputs, mean_error)


def solution(mesh):
    in_specs = (
        P("dp", "seq", None),
        P("dp", "seq", None),
        P("dp"),
        P("dp", None),
        P("dp"),
        P(),
        P(),
        P(),
        P(None, ("dp", "seq"), None),
        P(("dp", "seq"), None),
    )
    out_specs = (P(None, ("dp", "seq"), None), P())
    return jax.shard_map(shards, mesh=mesh, in_specs=in_specs, out_specs=out_specs, check_vma=False)
```

profile of v0, /device:TPU:1, one launch (start us, length us, event | category | flops | bytes accessed | tf_op | source)
XLA Modules:
  0.0 737.3 jit_solution(1324006842698795777)
XLA Ops:
  8.0 1.4 copy.54
  10.0 1.2 multiply_reduce_fusion.2
  11.9 1.2 fusion.49
  13.1 3.8 convolution_convert_fusion
  16.9 1.1 copy.61
  18.0 2.1 copy.62
  20.1 7.6 %all-to-all-start = ((bf16[1,128,3,16,64]{1,4,2,0,3:T(8,128)(2,1)}), bf16[1,128,3,16,64]{1,4,2,0,3:T(8,128)(2,1)S(1)}, u32[]{:S(2)}, u32[]{:S(2)}) async-start(bf16[1,128,3,16,64]{1,4,2,0,3:T(8,128)(2,1)} %copy.62), calls=%async_computation | async-start | bytes 1572864 | tf_op jit(solution)/shard_map/all_to_all | solution.py:121
  28.5 12.5 %all-to-all-done = bf16[1,128,3,16,64]{1,4,2,0,3:T(8,128)(2,1)S(1)} async-done(((bf16[1,128,3,16,64]{1,4,2,0,3:T(8,128)(2,1)}), bf16[1,128,3,16,64]{1,4,2,0,3:T(8,128)(2,1)S(1)}, u32[]{:S(2)}, u32[]{:S(2)}) %all-to-all-start) | async-done | bytes 786464 | tf_op jit(solution)/shard_map/all_to_all | solution.py:121
  41.0 1.4 copy.63
  42.4 1.4 squeeze.43
  44.7 1.2 copy.72
  46.0 1.2 copy.65
  47.2 2.0 copy.66
  49.2 17.6 %while.29 = (s32[]{:T(128)}, bf16[4,512,64]{1,2,0:T(8,128)(2,1)}, bf16[4,512,64]{2,1,0:T(8,128)(2,1)S(1)}, bf16[2048,64]{1,0:T(8,128)(2,1)S(1)}, bf16[2048,64]{1,0:T(8,128)(2,1)}, /*index=5*/s32[]{:T(128)}, s32[]{:T(128)}) while((s32[]{:T(128)}, bf16[4,512,64]{1,2,0:T(8,128)(2,1)}, bf16[4,512,64]{2,1,0:T(8,128)(2,1)S(1)}, ...), condition=%wide.region_6.7_spmd.clone, body=%wide.region_3.6_spmd.clone.sunk | while | flops 281054208 | bytes 14657661 | solution.py:59
  50.6 0.9 fusion.101
  51.7 1.9 fusion.102
  56.0 1.9 fusion.102
  60.4 1.9 fusion.102
  63.8 0.9 fusion.101
  64.8 1.9 fusion.102
  66.7 2.0 copy.73
  68.7 3.3 reshape.409
  72.5 12.3 %reduce.11 = bf16[2048,64]{1,0:T(8,128)(2,1)} reduce(bf16[2048,1,1,64]{3,2,1,0:T(2,128)(2,1)S(1)} %bitcast.130, bf16[]{:T(256)} %broadcast.272), dimensions={1,2}, to_apply=%bitcast.85.reduce_sub_computation | reduce | bytes 524290
  84.8 2.1 reshape.412
  87.0 4.2 all-to-all-start.1
  92.1 6.6 all-to-all-done.1
  98.7 2.1 reshape.413
  100.9 1.7 copy.69
  102.6 1.0 copy.80
  104.4 16.5 %all-gather.6.cloned.1.call-done = bf16[256,4,1024]{2,1,0:T(4,128)(2,1)} async-done(((bf16[1,4,1024]{2,1,0:T(4,128)(2,1)}), bf16[256,4,1024]{2,1,0:T(4,128)(2,1)}) %all-gather.6.cloned.1.call-update) | async-done | bytes 2097168 | tf_op jit(solution)/shard_map/all_gather | solution.py:111
  120.9 4.0 reshape.408
  124.8 117.2 %all-gather.4.cloned.1.call-done = bf16[3,1024,1024]{2,0,1:T(4,128)(2,1)} async-done(((bf16[3,4,1024]{2,0,1:T(4,128)(2,1)}), bf16[3,1024,1024]{2,0,1:T(4,128)(2,1)}) %all-gather.4.cloned.1.call-update) | async-done | bytes 6291472 | tf_op jit(solution)/shard_map/all_gather | solution.py:110
  242.1 18.7 %fusion.62 = (bf16[1,1024,1024]{2,0,1:T(2,128)(2,1)S(1)}, bf16[1,1024,1024]{2,0,1:T(2,128)(2,1)S(1)}, bf16[1,1024,1024]{2,0,1:T(2,128)(2,1)S(1)}) fusion(bf16[3,1024,1024]{2,0,1:T(4,128)(2,1)} %all-gather.4.cloned.1.call-done), kind=kLoop, calls=%fused_computation.100 | loop fusion | bytes 12582912 | tf_op jit(solution)/shard_map/slice | solution.py:134
  263.2 1.3 collective-permute-start.1
  264.5 4.7 collective-permute-start
  270.9 2.2 collective-permute-done.1
  273.6 1.1 pad_maximum_fusion.2
  275.6 1.2 copy.60
  276.9 1.0 copy.59
  277.9 3.2 fusion.66
  281.1 2.3 convolution_convert_fusion.2
  284.3 1.1 multiply_reduce_fusion.1
  285.5 79.6 %all-reduce.2 = (f32[]{:T(128)}, f32[]{:T(128)}) all-reduce(f32[]{:T(128)} %get-tuple-element.134, f32[]{:T(128)} %get-tuple-element.156), channel_id=1, replica_groups=mesh['dp'=16,'seq'=16] {'dp','seq'}, use_global_device_ids=true, to_apply=%region_8.9 | all-reduce | flops 2 | bytes 16 | tf_op jit(solution)/shard_map/psum | solution.py:166
  365.8 3.1 convolution_convert_fusion.1
  368.9 1.1 copy.71
  370.8 1.8 fusion.68
  372.6 1.5 fusion.46
  374.1 16.1 %fusion.36 = f32[16,64,256]{2,1,0:T(8,128)} fusion(bf16[128,16,64]{0,2,1:T(8,128)(2,1)} %bitcast.144, f32[16,128,256]{2,1,0:T(8,128)} %fusion.68, f32[16,128,256]{2,1,0:T(8,128)} %get-tuple-element.155, f32[16,128]{1,0:T(8,128)S(1)} %get-tuple-element.154), kind=kOutput, calls=%fused_computation.65 | convolution fusion | flops 70781184 | bytes 5513216 | tf_op jit(solution)/shard_map/bhrw,brhd->bwhd/dot_general | solution.py:83
  390.2 16.0 %convolution_add_fusion.1 = f32[16,64,256]{2,1,0:T(8,128)} fusion(f32[16,64,256]{2,1,0:T(8,128)} %fusion.36, bf16[128,16,64]{0,2,1:T(8,128)(2,1)} %bitcast.145, f32[16,128,256]{2,1,0:T(8,128)} %fusion.68, f32[16,128,256]{2,1,0:T(8,128)} %get-tuple-element.155, f32[16,128]{1,0:T(8,128)S(1)} %get-tuple-element.154), kind=kOutput, calls=%fused_computation.43 | convolution fusion | flops 72616192 | bytes 6561792 | tf_op jit(solution)/shard_map/bhrw,brhd->bwhd/dot_general | solution.py:83
  406.2 1.4 fusion.16
  407.6 1.0 fusion.63
  408.6 2.0 collective-permute-start.2
  410.6 1.6 collective-permute-start.3
  412.5 8.6 %collective-permute-done.2 = bf16[1,64,2048]{1,2,0:T(8,128)(2,1)S(1)} collective-permute-done((bf16[1,64,2048]{1,2,0:T(8,128)(2,1)S(1)}, bf16[1,64,2048]{1,2,0:T(8,128)(2,1)S(1)}, u32[]{:S(2)}, u32[]{:S(2)}) %collective-permute-start.2) | collective-permute-done | bytes 262176 | tf_op jit(solution)/shard_map/ppermute | solution.py:31
  421.2 1.3 fusion.30
  422.5 7.6 %scatter-add.6 = f32[1,128,2048]{1,2,0:T(8,128)S(1)} dynamic-update-slice(f32[1,128,2048]{1,2,0:T(8,128)S(1)} %fusion.28, f32[1,64,2048]{1,2,0:T(8,128)} %fusion.30, s32[]{:T(128)} %constant.132.clone.1, s32[]{:T(128)} %constant.132.clone.1, s32[]{:T(128)} %constant.132.clone.1) | dynamic-update-slice | bytes 1048580 | tf_op jit(solution)/shard_map/scatter-add | solution.py:195
  430.1 2.3 fusion.31
  432.5 8.6 %scatter-add.9 = f32[128,2048]{0,1:T(8,128)S(1)} dynamic-update-slice(f32[128,2048]{0,1:T(8,128)S(1)} %bitcast.122, f32[64,2048]{0,1:T(8,128)} %fusion.31, s32[]{:T(128)} %constant.143.clone.1, s32[]{:T(128)} %constant.132.clone.1) | dynamic-update-slice | bytes 1048580 | tf_op jit(solution)/shard_map/scatter-add | solution.py:196
  441.1 1.3 fusion.51
  442.4 1.3 convolution_add_fusion
  443.7 1.7 slice_bitcast_fusion.1
  445.3 4.1 pad_maximum_fusion
  450.7 277.4 %all-reduce.5.cloned.1.call-done = f32[2,1024,1024]{2,1,0:T(8,128)} async-done(((f32[2,1024,1024]{2,1,0:T(8,128)}), f32[2,1024,1024]{2,1,0:T(8,128)}) %all-reduce.5.cloned.1.call-update) | async-done | bytes 8388624
  728.1 1.5 constant_dynamic-slice_fusion
  (65 shorter events, 20.4 us)
Async XLA Ops:
  7.2 276.7 %copy-start = (bf16[1024,1024]{1,0:T(8,128)(2,1)S(1)}, bf16[1024,1024]{1,0:T(8,128)(2,1)}, u32[]{:S(2)}) copy-start(bf16[1024,1024]{1,0:T(8,128)(2,1)} %param.23) | copy-start | bytes 6291460
  7.2 113.7 %all-gather.6.cloned.1.call-start = ((), (), s32[]{:S(2)}) async-start(), calls=%async_computation.3 | async-start | bytes 2105344 | tf_op jit(solution)/shard_map/all_gather | solution.py:111
  7.9 234.2 %all-gather.4.cloned.1.call-start = ((), (), s32[]{:S(2)}) async-start(), calls=%async_computation.2 | async-start | bytes 8421376 | tf_op jit(solution)/shard_map/all_gather | solution.py:110
  16.9 11.5 %copy-start.8 = (s32[1,2048]{1,0:T(1,128)S(1)}, s32[1,2048]{1,0:T(1,128)}, u32[]{:S(2)}) copy-start(s32[1,2048]{1,0:T(1,128)} %param.19) | copy-start | bytes 24580
  20.1 20.9 %all-to-all-start = ((bf16[1,128,3,16,64]{1,4,2,0,3:T(8,128)(2,1)}), bf16[1,128,3,16,64]{1,4,2,0,3:T(8,128)(2,1)S(1)}, u32[]{:S(2)}, u32[]{:S(2)}) async-start(bf16[1,128,3,16,64]{1,4,2,0,3:T(8,128)(2,1)} %copy.62), calls=%async_computation | async-start | bytes 1572864 | tf_op jit(solution)/shard_map/all_to_all | solution.py:121
  50.6 1.0 copy-start.7
  55.0 1.0 copy-start.7
  59.4 1.0 copy-start.7
  63.8 1.0 copy-start.7
  87.0 11.7 %all-to-all-start.1 = ((bf16[16,2,4096]{2,1,0:T(2,128)(2,1)}), bf16[16,2,4096]{2,1,0:T(2,128)(2,1)}, u32[]{:S(2)}, u32[]{:S(2)}) async-start(bf16[16,2,4096]{2,1,0:T(2,128)(2,1)} %reshape.412), calls=%async_computation.1 | async-start | bytes 524288 | tf_op jit(solution)/shard_map/all_to_all | solution.py:123
  91.2 637.0 %all-reduce.5.cloned.1.call-start = ((), (), s32[]{:S(2)}) async-start(), calls=%async_computation.4 | async-start | bytes 16777216
  263.2 9.8 %collective-permute-start.1 = (bf16[1,64,2048]{2,1,0:T(8,128)(2,1)}, bf16[1,64,2048]{2,1,0:T(8,128)(2,1)}, u32[]{:S(2)}, u32[]{:S(2)}) collective-permute-start(bf16[1,64,2048]{2,1,0:T(8,128)(2,1)} %get-tuple-element.153), channel_id=1, source_target_pairs={{1,0},{2,1},{3,2},{4,3},{5,4},{6,5},{7,6},{8,7},{9,8},{10,9},{11,1... | collective-permute-start | bytes 786440 | tf_op jit(solution)/shard_map/ppermute | solution.py:23
  264.5 9.1 %collective-permute-start = (bf16[1,64,2048]{2,1,0:T(8,128)(2,1)S(1)}, bf16[1,64,2048]{2,1,0:T(8,128)(2,1)}, u32[]{:S(2)}, u32[]{:S(2)}) collective-permute-start(bf16[1,64,2048]{2,1,0:T(8,128)(2,1)S(1)} %get-tuple-element.152), channel_id=1, source_target_pairs={{0,1},{1,2},{2,3},{3,4},{4,5},{5,6},{6,7},{7,8},{8,9},{9,10},{10,1... | collective-permute-start | bytes 786440 | tf_op jit(solution)/shard_map/ppermute | solution.py:20
  281.1 2.3 copy-start.1
  283.4 1.0 copy-start.5
  370.1 0.7 copy-start.6
  370.1 2.5 copy-start.9
  374.1 32.1 %copy-start.2 = (f32[16,64,256]{2,1,0:T(8,128)}, f32[16,64,256]{2,1,0:T(8,128)S(1)}, u32[]{:S(2)}) copy-start(f32[16,64,256]{2,1,0:T(8,128)S(1)} %fusion.46) | copy-start | bytes 3145732
  406.2 6.0 copy-start.4
  407.6 4.6 copy-start.3
  408.6 12.5 %collective-permute-start.2 = (bf16[1,64,2048]{1,2,0:T(8,128)(2,1)S(1)}, bf16[1,64,2048]{1,2,0:T(8,128)(2,1)S(1)}, u32[]{:S(2)}, u32[]{:S(2)}) collective-permute-start(bf16[1,64,2048]{1,2,0:T(8,128)(2,1)S(1)} %get-tuple-element.146), channel_id=1, source_target_pairs={{0,1},{1,2},{2,3},{3,4},{4,5},{5,6},{6,7},{7,8},{8,9},{9,10},{10,1... | collective-permute-start | bytes 786440 | tf_op jit(solution)/shard_map/ppermute | solution.py:31
  410.6 19.5 %collective-permute-start.3 = (bf16[1,64,2048]{1,2,0:T(8,128)(2,1)}, bf16[1,64,2048]{1,2,0:T(8,128)(2,1)}, u32[]{:S(2)}, u32[]{:S(2)}) collective-permute-start(bf16[1,64,2048]{1,2,0:T(8,128)(2,1)} %get-tuple-element.145), channel_id=1, source_target_pairs={{1,0},{2,1},{3,2},{4,3},{5,4},{6,5},{7,6},{8,7},{9,8},{10,9},{11,1... | collective-permute-start | bytes 786440 | tf_op jit(solution)/shard_map/ppermute | solution.py:31
Sparse Core Ops, SparseCore 0:
  11.7 109.1 all-gather.5
  125.1 116.9 all-gather.3
  449.6 278.5 all-reduce.4
where the time goes:
time: 740 us; the launch traced here: 737 us
  waiting for transfers between devices  442 us (60%)
  blocking collectives  79.6 us (11%)
  local copies, waits for them, and re-layouts  76.8 us (10%)
  matrix products  65.1 us (9%)
  other arithmetic  33.1 us (4%)
  starting transfers between devices  21.6 us (3%)
  between operations  18.5 us (2%)
    unnamed x4, waiting for transfers between devices  278 us
    all_gather x1, waiting for transfers between devices, shards(): lax.all_gather(student_in, ('dp', 'seq'), axis=1, tiled=True)  117 us
    psum x1, blocking collectives, shards(): lax.psum((jnp.sum(difference * difference), jnp.sum(query_valid.astype(jn...  79.6 us
    slice x1, local copies, waits for them, and re-layouts, shards(): w_inputs[1]  18.7 us
    unnamed x28, local copies, waits for them, and re-layouts  18.2 us
    all_gather x1, waiting for transfers between devices, shards(): lax.all_gather(student_out, ('dp', 'seq'), axis=0, tiled=True)  16.5 us
    dot_general x1, matrix products, split_product(): jnp.einsum(form, upper_part, other, preferred_element_type=jnp.float32)  16.1 us
    dot_general x1, matrix products, split_product(): jnp.einsum(form, lower_part, other, preferred_element_type=jnp.float32)  16 us
  transfers between devices with their start and end apart: 9, of which 8 were waited for; matrix products, arithmetic and copies ran while one was open for 11% of the time, Pallas kernels for 0%

commit v1 on v0

--- a/solution.py
+++ b/solution.py
@@ -86,6 +86,14 @@
     return jnp.einsum(form, other, upper_part, preferred_element_type=jnp.float32) + jnp.einsum(
         form, other, lower_part, preferred_element_type=jnp.float32
     )
+
+
+def total_of(value):
+    spread = jnp.broadcast_to(value, (lax.axis_size("seq"), 128))
+    spread = lax.all_to_all(spread, "seq", 0, 0, tiled=True).sum(0, keepdims=True)
+    spread = jnp.broadcast_to(spread, (lax.axis_size("dp"), 128))
+    spread = lax.all_to_all(spread, "dp", 0, 0, tiled=True).sum(0)
+    return spread[0]
 
 
 def shards(
@@ -106,10 +114,20 @@
     seq_index = lax.axis_index("seq")
     frames = shard_rows * seq_count
     window = shard_rows + 2 * HALO
-    w_inputs, w_output = (
-        lax.all_gather(student_in, ("dp", "seq"), axis=1, tiled=True),
-        lax.all_gather(student_out, ("dp", "seq"), axis=0, tiled=True),
-    )
+    rows_each = student_out.shape[0]
+    stacked = jnp.concatenate(
+        (student_in.reshape(3 * rows_each, model_width), student_out), axis=0
+    )
+    gathered = lax.all_gather(lax.all_gather(stacked, "seq", axis=0), "dp", axis=0)
+    gathered = gathered.reshape(-1, 4 * rows_each, model_width)
+    w_inputs = (
+        gathered[:, : 3 * rows_each]
+        .reshape(-1, 3, rows_each, model_width)
+        .transpose(1, 0, 2, 3)
+        .reshape(3, -1, model_width)
+    )
+    w_output = gathered[:, 3 * rows_each :].reshape(-1, model_width)
+    frame_count = jnp.sum(lax.all_gather(lengths, "dp", axis=0, tiled=True)).astype(jnp.float32)
     normed = normalize(clean_frames, noise_frames, time_index, modulation)
     flat_rows = normed.reshape(dialogs * shard_rows, model_width)
     frame_pos = jnp.arange(frames, dtype=jnp.int32)
@@ -163,9 +181,7 @@
     student_vel = jnp.dot(mix_flat, w_output, preferred_element_type=jnp.float32)
     query_valid = (query_pos[None, :] < lengths[:, None]).reshape(-1)
     difference = jnp.where(query_valid[:, None], student_vel - teacher_vel, 0.0)
-    square_sum, frame_count = lax.psum(
-        (jnp.sum(difference * difference), jnp.sum(query_valid.astype(jnp.float32))), ("dp", "seq")
-    )
+    square_sum = total_of(jnp.sum(difference * difference))
     mean_error = square_sum / (frame_count * model_width)
     grad_vel = (difference * lax.rsqrt(frame_count)).astype(jnp.bfloat16)
     grad_mix = jnp.dot(grad_vel, w_output.T, preferred_element_type=jnp.float32).astype(
@@ -194,10 +210,17 @@
     owned_rows = grad_both[:, HALO : HALO + shard_rows]
     owned_rows = owned_rows.at[:, :HALO].add(from_prev)
     owned_rows = owned_rows.at[:, shard_rows - HALO :].add(from_next)
-    owned_flat = owned_rows.reshape(dialogs * shard_rows, 2 * model_width)
-    grad_kv_weight = split_product("rf,rg->fg", owned_flat, flat_rows, False)
-    grad_stack = jnp.stack((grad_kv_weight[:, :model_width], grad_kv_weight[:, model_width:]))
-    grad_inputs = lax.psum_scatter(grad_stack, ("dp", "seq"), scatter_dimension=1, tiled=True)
+    by_head = owned_rows.reshape(shard_rows, 2, HEADS, head_dim).transpose(0, 2, 1, 3)
+    head_grads = lax.all_to_all(by_head, "seq", split_axis=1, concat_axis=0, tiled=True)
+    head_grads = head_grads.reshape(frames, 2 * head_dim)
+    normed_all = lax.all_gather(flat_rows, "seq", axis=0, tiled=True)
+    partial = split_product("rf,rg->fg", head_grads, normed_all, False)
+    dp_count = lax.axis_size("dp")
+    partial = partial.reshape(dp_count, seq_count, rows_each, 2 * head_dim)
+    partial = lax.all_to_all(partial, "dp", split_axis=0, concat_axis=0, tiled=True).sum(0)
+    mine = lax.all_to_all(partial, "seq", split_axis=0, concat_axis=0, tiled=True)
+    mine = mine.reshape(HEADS, rows_each, 2, head_dim).transpose(2, 1, 0, 3)
+    grad_inputs = mine.reshape(2, rows_each, model_width)
     return (grad_inputs, mean_error)
 
 

time: 740 us -> 359 us (0.49)
  waiting for transfers between devices: 442 us -> 45 us
  starting transfers between devices: 21.6 us -> 41.1 us
  blocking collectives: 79.6 us -> 64.3 us
  local copies, waits for them, and re-layouts: 76.8 us -> 87.7 us
    unnamed x4 -> x2, waiting for transfers between devices: 278 us -> 0.54 us
    all_gather x2, waiting for transfers between devices: 134 us -> 0.04 us  [the longest x1 0.02 us: shards(): lax.all_gather(lax.all_gather(stacked, 'seq', axis=0), 'dp', axis=0)]
    psum x1 -> x0, blocking collectives: 79.6 us -> none  [shards(): lax.psum((jnp.sum(difference * difference), jnp.sum(query_valid.astype(jn...]
    all_to_all x0 -> x4, waiting for transfers between devices: none -> 29.6 us  [the longest x1 17.3 us: shards(): lax.all_to_all(partial, 'dp', split_axis=0, concat_axis=0, tiled=True)]
    all_to_all x0 -> x4, starting transfers between devices: none -> 22 us  [the longest x1 8.33 us: shards(): lax.all_to_all(partial, 'dp', split_axis=0, concat_axis=0, tiled=True)]
    all_gather x0 -> x1, blocking collectives: none -> 21.8 us  [shards(): lax.all_gather(stacked, 'seq', axis=0)]
    unnamed x0 -> x1, blocking collectives: none -> 21.3 us
    all_to_all x0 -> x1, blocking collectives: none -> 21.2 us  [shards(): lax.all_to_all(by_head, 'seq', split_axis=1, concat_axis=0, tiled=True)]
  transfers between devices with their start and end apart: 9 -> 12, of which waited for: 8 -> 5; matrix products, arithmetic and copies ran while one was open for 11% -> 52% of each run, Pallas kernels for 0% -> 0%
where the time goes in v1:
time: 359 us; the launch traced here: 355 us
  local copies, waits for them, and re-layouts  87.7 us (24%)
  matrix products  67.7 us (19%)
  blocking collectives  64.3 us (18%)
  waiting for transfers between devices  45 us (13%)
  starting transfers between devices  41.1 us (11%)
  other arithmetic  30.8 us (9%)
  between operations  17.9 us (5%)
    all_gather x1, blocking collectives, shards(): lax.all_gather(stacked, 'seq', axis=0)  21.8 us
    unnamed x1, blocking collectives  21.3 us
    all_to_all x1, blocking collectives, shards(): lax.all_to_all(by_head, 'seq', split_axis=1, concat_axis=0, tiled=True)  21.2 us
    all_to_all x1, waiting for transfers between devices, shards(): lax.all_to_all(partial, 'dp', split_axis=0, concat_axis=0, tiled=True)  17.3 us
    dot_general x1, matrix products, split_product(): jnp.einsum(form, upper_part, other, preferred_element_type=jnp.float32)  15.6 us
    unnamed x33, local copies, waits for them, and re-layouts  15.5 us
    dot_general x1, matrix products, split_product(): jnp.einsum(form, lower_part, other, preferred_element_type=jnp.float32)  14.9 us
    unnamed x1, other arithmetic  12.4 us
  transfers between devices with their start and end apart: 12, of which 5 were waited for; matrix products, arithmetic and copies ran while one was open for 52% of the time, Pallas kernels for 0%

profile of v1, /device:TPU:1, one launch (start us, length us, event | category | flops | bytes accessed | tf_op | source)
XLA Modules:
  0.0 354.5 jit_solution(4930259637896913242)
XLA Ops:
  8.8 21.8 %all-gather.1 = bf16[256,1024]{1,0:T(8,128)(2,1)} all-gather(bf16[16,1024]{1,0:T(8,128)(2,1)S(1)} %pad_maximum_fusion.2), channel_id=3, replica_groups=mesh['dp'=16,'seq'=16] {'seq'}, dimensions={0}, use_global_device_ids=true | all-gather | bytes 557056 | tf_op jit(solution)/shard_map/all_gather | solution.py:121
  31.3 1.2 multiply_reduce_fusion.2
  33.2 1.2 multiply_convert_fusion.1
  34.4 3.9 %convolution_convert_fusion = bf16[128,3072]{1,0:T(8,128)(2,1)S(1)} fusion(bf16[1024,3072]{1,0:T(8,128)(2,1)} %param.22, bf16[1,128,1024]{2,1,0:T(8,128)(2,1)S(1)} %multiply_convert_fusion.1), kind=kOutput, calls=%fused_computation.23 | convolution fusion | flops 805699584 | bytes 7340032 | tf_op jit(solution)/shard_map/dot_general | solution.py:135
  38.3 1.2 copy.96
  39.5 2.1 copy.97
  41.6 4.7 %all-to-all-start = ((bf16[1,128,3,16,64]{1,4,2,0,3:T(8,128)(2,1)}), bf16[1,128,3,16,64]{1,4,2,0,3:T(8,128)(2,1)S(1)}, u32[]{:S(2)}, u32[]{:S(2)}) async-start(bf16[1,128,3,16,64]{1,4,2,0,3:T(8,128)(2,1)} %copy.97), calls=%async_computation | async-start | bytes 1572864 | tf_op jit(solution)/shard_map/all_to_all | solution.py:139
  47.9 8.9 %all-to-all-done = bf16[1,128,3,16,64]{1,4,2,0,3:T(8,128)(2,1)S(1)} async-done(((bf16[1,128,3,16,64]{1,4,2,0,3:T(8,128)(2,1)}), bf16[1,128,3,16,64]{1,4,2,0,3:T(8,128)(2,1)S(1)}, u32[]{:S(2)}, u32[]{:S(2)}) %all-to-all-start) | async-done | bytes 786464 | tf_op jit(solution)/shard_map/all_to_all | solution.py:139
  56.8 1.4 copy.98
  58.3 1.4 squeeze.46
  60.6 1.2 copy.113
  61.8 1.3 copy.100
  64.1 17.6 %while.29 = (s32[]{:T(128)}, bf16[4,512,64]{1,2,0:T(8,128)(2,1)}, bf16[4,512,64]{2,1,0:T(8,128)(2,1)S(1)}, bf16[2048,64]{1,0:T(8,128)(2,1)S(1)}, bf16[2048,64]{1,0:T(8,128)(2,1)}, /*index=5*/s32[]{:T(128)}, s32[]{:T(128)}) while((s32[]{:T(128)}, bf16[4,512,64]{1,2,0:T(8,128)(2,1)}, bf16[4,512,64]{2,1,0:T(8,128)(2,1)S(1)}, ...), condition=%wide.region_6.7_spmd.clone, body=%wide.region_3.6_spmd.clone.sunk | while | flops 281054208 | bytes 14658161 | solution.py:59
  66.6 1.9 fusion.101
  71.0 1.9 fusion.101
  75.4 1.9 fusion.101
  79.8 1.9 fusion.101
  81.7 2.0 copy.114
  83.7 3.3 reshape.458
  87.5 12.4 %reduce.14 = bf16[2048,64]{1,0:T(8,128)(2,1)} reduce(bf16[2048,1,1,64]{3,2,1,0:T(2,128)(2,1)S(1)} %bitcast.156, bf16[]{:T(256)} %broadcast.275), dimensions={1,2}, to_apply=%bitcast.107.reduce_sub_computation | reduce | bytes 524290
  99.9 2.2 reshape.459
  102.0 3.5 all-to-all-start.1
  106.9 21.3 %all-reduce.1 = s32[16]{0:T(128)S(1)} all-reduce(s32[16]{0:T(128)S(1)} %dynamic-update-slice.6), channel_id=1, replica_groups=mesh['dp'=16,'seq'=16] {'dp'}, use_global_device_ids=true, to_apply=%add.1 | all-reduce | flops 16 | bytes 128
  131.1 7.2 %copy.116 = bf16[256,12,1024]{2,0,1:T(8,128)(2,1)S(1)} copy(bf16[256,12,1024]{2,1,0:T(8,128)(2,1)} %bitcast.144) | data formatting | bytes 12582912
  138.3 3.4 fusion.64
  141.7 2.9 copy.93
  144.6 4.0 %squeeze.45 = bf16[1024,1024]{1,0:T(8,128)(2,1)} reshape(bf16[1,256,4,1024]{3,2,1,0:T(4,128)(2,1)} %copy.93) | data formatting | bytes 4194304 | tf_op jit(solution)/shard_map/squeeze | solution.py:155
  148.6 4.5 %copy.92 = bf16[1,256,4,1024]{3,2,1,0:T(4,128)(2,1)} copy(bf16[1,256,4,1024]{3,1,2,0:T(8,128)(2,1)} %get-tuple-element.142) | data formatting | bytes 4194304 | tf_op jit(solution)/shard_map/slice | solution.py:152
  153.1 4.0 %squeeze.44 = bf16[1024,1024]{1,0:T(8,128)(2,1)} reshape(bf16[1,256,4,1024]{3,2,1,0:T(4,128)(2,1)} %copy.92) | data formatting | bytes 4194304 | tf_op jit(solution)/shard_map/squeeze | solution.py:152
  157.2 2.2 convolution_convert_fusion.3
  160.7 4.0 %collective-permute-start = (bf16[1,64,2048]{2,1,0:T(8,128)(2,1)}, bf16[1,64,2048]{2,1,0:T(8,128)(2,1)}, u32[]{:S(2)}, u32[]{:S(2)}) collective-permute-start(bf16[1,64,2048]{2,1,0:T(8,128)(2,1)} %get-tuple-element.152), channel_id=1, source_target_pairs={{0,1},{1,2},{2,3},{3,4},{4,5},{5,6},{6,7},{7,8},{8,9},{9,10},{10,1... | collective-permute-start | bytes 786440 | tf_op jit(solution)/shard_map/ppermute | solution.py:20
  164.7 1.3 collective-permute-start.1
  166.0 3.0 copy.90
  169.0 4.4 %squeeze.43 = bf16[1024,1024]{1,0:T(8,128)(2,1)} reshape(bf16[1,256,4,1024]{3,2,1,0:T(4,128)(2,1)} %copy.90) | data formatting | bytes 4194304 | tf_op jit(solution)/shard_map/squeeze | solution.py:148
  173.4 2.0 convolution_convert_fusion.5
  176.3 4.6 %slice.137 = bf16[256,4,1024]{2,1,0:T(4,128)(2,1)} slice(bf16[256,16,1024]{2,1,0:T(8,128)(2,1)} %all-gather.8.cloned.1.call-done), slice={[0:256], [12:16], [0:1024]} | slice | bytes 4194304 | tf_op jit(solution)/shard_map/slice | solution.py:129
  180.9 4.0 %reshape.438 = bf16[1024,1024]{1,0:T(8,128)(2,1)} reshape(bf16[256,4,1024]{2,1,0:T(4,128)(2,1)} %slice.137) | data formatting | bytes 4194304 | tf_op jit(solution)/shard_map/reshape | solution.py:129
  187.3 3.2 fusion.68
  190.4 2.3 convolution_convert_fusion.2
  193.2 1.1 multiply_reduce_fusion.1
  195.4 1.8 fusion.70
  197.2 15.6 %fusion.38 = f32[16,64,256]{2,1,0:T(8,128)} fusion(bf16[128,16,64]{0,2,1:T(8,128)(2,1)S(1)} %bitcast.173, f32[16,128,256]{2,1,0:T(8,128)} %fusion.70, f32[16,128,256]{2,1,0:T(8,128)} %get-tuple-element.155, f32[16,128]{1,0:T(8,128)S(1)} %get-tuple-element.154), kind=kOutput, calls=%fused_computation.61 | convolution fusion | flops 70781184 | bytes 5513216 | tf_op jit(solution)/shard_map/bhrw,brhd->bwhd/dot_general | solution.py:83
  212.9 14.9 %convolution_add_fusion = f32[16,64,256]{2,1,0:T(8,128)S(1)} fusion(f32[16,64,256]{2,1,0:T(8,128)} %fusion.38, bf16[128,16,64]{0,2,1:T(8,128)(2,1)} %bitcast.172, f32[16,128,256]{2,1,0:T(8,128)} %fusion.70, f32[16,128,256]{2,1,0:T(8,128)} %get-tuple-element.155, f32[16,128]{1,0:T(8,128)S(1)} %get-tuple-element.154), kind=kOutput, calls=%fused_computation.37 | convolution fusion | flops 72616192 | bytes 6561792 | tf_op jit(solution)/shard_map/bhrw,brhd->bwhd/dot_general | solution.py:83
  227.8 2.1 fusion.48
  231.1 4.0 %collective-permute-start.2 = (bf16[1,64,2048]{1,2,0:T(8,128)(2,1)S(1)}, bf16[1,64,2048]{1,2,0:T(8,128)(2,1)S(1)}, u32[]{:S(2)}, u32[]{:S(2)}) collective-permute-start(bf16[1,64,2048]{1,2,0:T(8,128)(2,1)S(1)} %get-tuple-element.146), channel_id=1, source_target_pairs={{0,1},{1,2},{2,3},{3,4},{4,5},{5,6},{6,7},{7,8},{8,9},{9,10},{10,1... | collective-permute-start | bytes 786440 | tf_op jit(solution)/shard_map/ppermute | solution.py:31
  235.1 1.3 collective-permute-start.3
  236.4 1.3 fusion.29
  237.7 5.9 %collective-permute-done.2 = bf16[1,64,2048]{1,2,0:T(8,128)(2,1)S(1)} collective-permute-done((bf16[1,64,2048]{1,2,0:T(8,128)(2,1)S(1)}, bf16[1,64,2048]{1,2,0:T(8,128)(2,1)S(1)}, u32[]{:S(2)}, u32[]{:S(2)}) %collective-permute-start.2) | collective-permute-done | bytes 262176 | tf_op jit(solution)/shard_map/ppermute | solution.py:31
  243.6 1.4 fusion.31
  245.0 5.6 %scatter-add.6 = f32[1,128,2048]{1,2,0:T(8,128)} dynamic-update-slice(f32[1,128,2048]{1,2,0:T(8,128)} %fusion.29, f32[1,64,2048]{1,2,0:T(8,128)} %fusion.31, s32[]{:T(128)} %constant.131.clone.1, s32[]{:T(128)} %constant.131.clone.1, s32[]{:T(128)} %constant.131.clone.1) | dynamic-update-slice | bytes 1048580 | tf_op jit(solution)/shard_map/scatter-add | solution.py:211
  250.6 2.8 slice_add_fusion
  253.4 8.6 %scatter-add.9 = f32[1,128,2048]{1,2,0:T(8,128)S(1)} dynamic-update-slice(f32[1,128,2048]{1,2,0:T(8,128)S(1)} %copy-done.5, f32[1,64,2048]{1,2,0:T(8,128)} %slice_add_fusion, s32[]{:T(128)} %constant.131.clone.1, s32[]{:T(128)} %constant.142.clone.1, s32[]{:T(128)} %constant.131.clone.1) | dynamic-update-slice | bytes 1048580 | tf_op jit(solution)/shard_map/scatter-add | solution.py:212
  262.1 21.2 %all_to_all.67 = f32[128,16,2,64]{0,3,2,1:T(8,128)} all-to-all(f32[128,16,2,64]{0,3,2,1:T(8,128)S(1)} %copy.107), channel_id=1, replica_groups=mesh['dp'=16,'seq'=16] {'seq'}, dimensions={1} | all-to-all | bytes 2097152 | tf_op jit(solution)/shard_map/all_to_all | solution.py:214
  283.4 1.2 broadcast_in_dim.59
  284.6 3.5 all-to-all-start.5
  288.1 1.8 copy.108
  290.0 3.7 %fusion.16 = f32[1024,128]{1,0:T(8,128)S(1)} fusion(bf16[1,2048,1024]{2,1,0:T(8,128)(2,1)} %all-gather.6.cloned.1.call-done, f32[16,8,16,128]{3,2,1,0:T(8,128)S(1)} %bitcast.152), kind=kOutput, calls=%fused_computation.19 | convolution fusion | flops 537919488 | bytes 5767168 | tf_op jit(solution)/shard_map/rf,rg->fg/dot_general | solution.py:86
  293.7 2.3 fusion.25
  296.0 8.3 %all-to-all-start.3 = ((f32[16,16,4,128]{3,2,1,0:T(4,128)}), f32[16,16,4,128]{3,2,1,0:T(4,128)S(1)}, u32[]{:S(2)}, u32[]{:S(2)}) async-start(f32[16,16,4,128]{3,2,1,0:T(4,128)} %bitcast.164), calls=%async_computation.3 | async-start | bytes 1048576 | tf_op jit(solution)/shard_map/all_to_all | solution.py:220
  304.3 17.3 %all-to-all-done.3 = f32[16,16,4,128]{3,2,1,0:T(4,128)S(1)} async-done(((f32[16,16,4,128]{3,2,1,0:T(4,128)}), f32[16,16,4,128]{3,2,1,0:T(4,128)S(1)}, u32[]{:S(2)}, u32[]{:S(2)}) %all-to-all-start.3) | async-done | bytes 524320 | tf_op jit(solution)/shard_map/all_to_all | solution.py:220
  322.2 3.3 all-to-all-start.6
  326.3 5.9 %all-to-all-done.6 = f32[16,1,128]{2,1,0:T(1,128)S(1)} async-done(((f32[16,1,128]{2,1,0:T(1,128)}), f32[16,1,128]{2,1,0:T(1,128)S(1)}, u32[]{:S(2)}, u32[]{:S(2)}) %all-to-all-start.6) | async-done | bytes 8224 | tf_op jit(solution)/shard_map/all_to_all | solution.py:95
  332.2 6.9 %all-to-all-start.4 = ((f32[16,4,128]{2,1,0:T(4,128)}), f32[16,4,128]{2,1,0:T(4,128)S(1)}, u32[]{:S(2)}, u32[]{:S(2)}) async-start(f32[16,4,128]{2,1,0:T(4,128)} %reduce_sum.85), calls=%async_computation.4 | async-start | bytes 65536 | tf_op jit(solution)/shard_map/all_to_all | solution.py:221
  339.2 6.4 %all-to-all-done.4 = f32[16,4,128]{2,1,0:T(4,128)S(1)} async-done(((f32[16,4,128]{2,1,0:T(4,128)}), f32[16,4,128]{2,1,0:T(4,128)S(1)}, u32[]{:S(2)}, u32[]{:S(2)}) %all-to-all-start.4) | async-done | bytes 32800 | tf_op jit(solution)/shard_map/all_to_all | solution.py:221
  (97 shorter events, 28.6 us)
Async XLA Ops:
  7.2 186.0 %copy-start = (bf16[1024,1024]{1,0:T(8,128)(2,1)S(1)}, bf16[1024,1024]{1,0:T(8,128)(2,1)}, u32[]{:S(2)}) copy-start(bf16[1024,1024]{1,0:T(8,128)(2,1)} %param.23) | copy-start | bytes 6291460
  7.2 123.9 %all-gather.8.cloned.1.call-start = ((), (), s32[]{:S(2)}) async-start(), calls=%async_computation.8 | async-start | bytes 8912896 | tf_op jit(solution)/shard_map/all_gather | solution.py:121
  34.4 3.9 %copy-start.3 = (bf16[1,128,1024]{2,1,0:T(8,128)(2,1)}, bf16[1,128,1024]{2,1,0:T(8,128)(2,1)S(1)}, u32[]{:S(2)}) copy-start(bf16[1,128,1024]{2,1,0:T(8,128)(2,1)S(1)} %multiply_convert_fusion.1) | copy-start | bytes 786436
  39.5 8.3 %copy-start.10 = (s32[1,2048]{1,0:T(1,128)S(1)}, s32[1,2048]{1,0:T(1,128)}, u32[]{:S(2)}) copy-start(s32[1,2048]{1,0:T(1,128)} %param.19) | copy-start | bytes 24580
  41.6 15.2 %all-to-all-start = ((bf16[1,128,3,16,64]{1,4,2,0,3:T(8,128)(2,1)}), bf16[1,128,3,16,64]{1,4,2,0,3:T(8,128)(2,1)S(1)}, u32[]{:S(2)}, u32[]{:S(2)}) async-start(bf16[1,128,3,16,64]{1,4,2,0,3:T(8,128)(2,1)} %copy.97), calls=%async_computation | async-start | bytes 1572864 | tf_op jit(solution)/shard_map/all_to_all | solution.py:139
  46.4 243.6 %all-gather.6.cloned.1.call-start = ((), (), s32[]{:S(2)}) async-start(), calls=%async_computation.7 | async-start | bytes 4456448 | tf_op jit(solution)/shard_map/all_gather | solution.py:216
  65.6 1.0 copy-start.8
  69.9 1.0 copy-start.8
  74.3 1.1 copy-start.8
  78.7 1.1 copy-start.8
  83.7 21.9 %copy-start.11 = (u32[256]{0:T(256)S(1)}, u32[256]{0:T(256)}, u32[]{:S(2)}) copy-start(u32[256]{0:T(256)} %constant.155) | copy-start | bytes 3076
  102.0 27.7 %all-to-all-start.1 = ((bf16[16,2,4096]{2,1,0:T(2,128)(2,1)}), bf16[16,2,4096]{2,1,0:T(2,128)(2,1)S(1)}, u32[]{:S(2)}, u32[]{:S(2)}) async-start(bf16[16,2,4096]{2,1,0:T(2,128)(2,1)} %reshape.459), calls=%async_computation.1 | async-start | bytes 524288 | tf_op jit(solution)/shard_map/all_to_all | solution.py:141
  153.1 4.0 %copy-start.4 = (bf16[1,128,1024]{2,1,0:T(8,128)(2,1)S(1)}, bf16[1,128,1024]{2,1,0:T(8,128)(2,1)}, u32[]{:S(2)}) copy-start(bf16[1,128,1024]{2,1,0:T(8,128)(2,1)} %copy-done.3) | copy-start | bytes 786436
  157.2 2.2 copy-start.6
  159.4 6.6 %copy-start.7 = (bf16[1,256,4,1024]{3,1,2,0:T(8,128)(2,1)S(1)}, bf16[1,256,4,1024]{3,1,2,0:T(8,128)(2,1)}, u32[]{:S(2)}) copy-start(bf16[1,256,4,1024]{3,1,2,0:T(8,128)(2,1)} %get-tuple-element.144) | copy-start | bytes 6291460
  160.7 24.1 %collective-permute-start = (bf16[1,64,2048]{2,1,0:T(8,128)(2,1)}, bf16[1,64,2048]{2,1,0:T(8,128)(2,1)}, u32[]{:S(2)}, u32[]{:S(2)}) collective-permute-start(bf16[1,64,2048]{2,1,0:T(8,128)(2,1)} %get-tuple-element.152), channel_id=1, source_target_pairs={{0,1},{1,2},{2,3},{3,4},{4,5},{5,6},{6,7},{7,8},{8,9},{9,10},{10,1... | collective-permute-start | bytes 786440 | tf_op jit(solution)/shard_map/ppermute | solution.py:20
  164.7 20.1 %collective-permute-start.1 = (bf16[1,64,2048]{2,1,0:T(8,128)(2,1)}, bf16[1,64,2048]{2,1,0:T(8,128)(2,1)}, u32[]{:S(2)}, u32[]{:S(2)}) collective-permute-start(bf16[1,64,2048]{2,1,0:T(8,128)(2,1)} %get-tuple-element.153), channel_id=1, source_target_pairs={{1,0},{2,1},{3,2},{4,3},{5,4},{6,5},{7,6},{8,7},{9,8},{10,9},{11,1... | collective-permute-start | bytes 786440 | tf_op jit(solution)/shard_map/ppermute | solution.py:23
  190.4 2.3 copy-start.2
  195.2 2.0 copy-start.9
  231.1 12.5 %collective-permute-start.2 = (bf16[1,64,2048]{1,2,0:T(8,128)(2,1)S(1)}, bf16[1,64,2048]{1,2,0:T(8,128)(2,1)S(1)}, u32[]{:S(2)}, u32[]{:S(2)}) collective-permute-start(bf16[1,64,2048]{1,2,0:T(8,128)(2,1)S(1)} %get-tuple-element.146), channel_id=1, source_target_pairs={{0,1},{1,2},{2,3},{3,4},{4,5},{5,6},{6,7},{7,8},{8,9},{9,10},{10,1... | collective-permute-start | bytes 786440 | tf_op jit(solution)/shard_map/ppermute | solution.py:31
  235.1 15.5 %collective-permute-start.3 = (bf16[1,64,2048]{1,2,0:T(8,128)(2,1)}, bf16[1,64,2048]{1,2,0:T(8,128)(2,1)}, u32[]{:S(2)}, u32[]{:S(2)}) collective-permute-start(bf16[1,64,2048]{1,2,0:T(8,128)(2,1)} %get-tuple-element.145), channel_id=1, source_target_pairs={{1,0},{2,1},{3,2},{4,3},{5,4},{6,5},{7,6},{8,7},{9,8},{10,9},{11,1... | collective-permute-start | bytes 786440 | tf_op jit(solution)/shard_map/ppermute | solution.py:31
  250.6 2.8 copy-start.5
  284.6 11.4 %all-to-all-start.5 = ((f32[16,1,128]{2,1,0:T(1,128)}), f32[16,1,128]{2,1,0:T(1,128)S(1)}, u32[]{:S(2)}, u32[]{:S(2)}) async-start(f32[16,1,128]{2,1,0:T(1,128)} %broadcast_in_dim.59), calls=%async_computation.5 | async-start | bytes 16384 | tf_op jit(solution)/shard_map/all_to_all | solution.py:93
  290.0 3.7 %copy-start.1 = (bf16[1,2048,1024]{2,1,0:T(8,128)(2,1)S(1)}, bf16[1,2048,1024]{2,1,0:T(8,128)(2,1)}, u32[]{:S(2)}) copy-start(bf16[1,2048,1024]{2,1,0:T(8,128)(2,1)} %all-gather.6.cloned.1.call-done) | copy-start | bytes 12582916
  296.0 25.6 %all-to-all-start.3 = ((f32[16,16,4,128]{3,2,1,0:T(4,128)}), f32[16,16,4,128]{3,2,1,0:T(4,128)S(1)}, u32[]{:S(2)}, u32[]{:S(2)}) async-start(f32[16,16,4,128]{3,2,1,0:T(4,128)} %bitcast.164), calls=%async_computation.3 | async-start | bytes 1048576 | tf_op jit(solution)/shard_map/all_to_all | solution.py:220
  322.2 10.0 %all-to-all-start.6 = ((f32[16,1,128]{2,1,0:T(1,128)}), f32[16,1,128]{2,1,0:T(1,128)S(1)}, u32[]{:S(2)}, u32[]{:S(2)}) async-start(f32[16,1,128]{2,1,0:T(1,128)} %broadcast_in_dim.88), calls=%async_computation.6 | async-start | bytes 16384 | tf_op jit(solution)/shard_map/all_to_all | solution.py:95
  332.2 13.3 %all-to-all-start.4 = ((f32[16,4,128]{2,1,0:T(4,128)}), f32[16,4,128]{2,1,0:T(4,128)S(1)}, u32[]{:S(2)}, u32[]{:S(2)}) async-start(f32[16,4,128]{2,1,0:T(4,128)} %reduce_sum.85), calls=%async_computation.4 | async-start | bytes 65536 | tf_op jit(solution)/shard_map/all_to_all | solution.py:221
Sparse Core Ops, SparseCore 0:
  30.7 62.3 all-gather.7
  95.6 56.1 all-gather.5

commit v2 on v1

--- a/solution.py
+++ b/solution.py
@@ -86,14 +86,6 @@
     return jnp.einsum(form, other, upper_part, preferred_element_type=jnp.float32) + jnp.einsum(
         form, other, lower_part, preferred_element_type=jnp.float32
     )
-
-
-def total_of(value):
-    spread = jnp.broadcast_to(value, (lax.axis_size("seq"), 128))
-    spread = lax.all_to_all(spread, "seq", 0, 0, tiled=True).sum(0, keepdims=True)
-    spread = jnp.broadcast_to(spread, (lax.axis_size("dp"), 128))
-    spread = lax.all_to_all(spread, "dp", 0, 0, tiled=True).sum(0)
-    return spread[0]
 
 
 def shards(
@@ -115,19 +107,12 @@
     frames = shard_rows * seq_count
     window = shard_rows + 2 * HALO
     rows_each = student_out.shape[0]
-    stacked = jnp.concatenate(
-        (student_in.reshape(3 * rows_each, model_width), student_out), axis=0
-    )
-    gathered = lax.all_gather(lax.all_gather(stacked, "seq", axis=0), "dp", axis=0)
-    gathered = gathered.reshape(-1, 4 * rows_each, model_width)
-    w_inputs = (
-        gathered[:, : 3 * rows_each]
-        .reshape(-1, 3, rows_each, model_width)
-        .transpose(1, 0, 2, 3)
-        .reshape(3, -1, model_width)
-    )
-    w_output = gathered[:, 3 * rows_each :].reshape(-1, model_width)
-    frame_count = jnp.sum(lax.all_gather(lengths, "dp", axis=0, tiled=True)).astype(jnp.float32)
+    stacked = jnp.concatenate((student_in, student_out[None]), axis=0)
+    gathered = lax.all_gather(
+        lax.all_gather(stacked, "seq", axis=1, tiled=True), "dp", axis=1, tiled=True
+    )
+    w_inputs = gathered[:3]
+    w_output = gathered[3]
     normed = normalize(clean_frames, noise_frames, time_index, modulation)
     flat_rows = normed.reshape(dialogs * shard_rows, model_width)
     frame_pos = jnp.arange(frames, dtype=jnp.int32)
@@ -181,9 +166,9 @@
     student_vel = jnp.dot(mix_flat, w_output, preferred_element_type=jnp.float32)
     query_valid = (query_pos[None, :] < lengths[:, None]).reshape(-1)
     difference = jnp.where(query_valid[:, None], student_vel - teacher_vel, 0.0)
-    square_sum = total_of(jnp.sum(difference * difference))
-    mean_error = square_sum / (frame_count * model_width)
-    grad_vel = (difference * lax.rsqrt(frame_count)).astype(jnp.bfloat16)
+    square_local = jnp.sum(difference * difference)
+    count_local = jnp.sum(query_valid.astype(jnp.float32))
+    grad_vel = difference.astype(jnp.bfloat16)
     grad_mix = jnp.dot(grad_vel, w_output.T, preferred_element_type=jnp.float32).astype(
         jnp.bfloat16
     )
@@ -217,8 +202,16 @@
     partial = split_product("rf,rg->fg", head_grads, normed_all, False)
     dp_count = lax.axis_size("dp")
     partial = partial.reshape(dp_count, seq_count, rows_each, 2 * head_dim)
+    lane = jnp.arange(2 * head_dim)
+    scalars = jnp.where(lane == 0, square_local, jnp.where(lane == 1, count_local, 0.0))
+    scalars = jnp.broadcast_to(scalars, (dp_count, seq_count, 1, 2 * head_dim))
+    partial = jnp.concatenate((partial, scalars), axis=2)
     partial = lax.all_to_all(partial, "dp", split_axis=0, concat_axis=0, tiled=True).sum(0)
     mine = lax.all_to_all(partial, "seq", split_axis=0, concat_axis=0, tiled=True)
+    totals = mine[:, rows_each].sum(0)
+    square_sum, frame_count = totals[0], totals[1]
+    mean_error = square_sum / (frame_count * model_width)
+    mine = mine[:, :rows_each] * lax.rsqrt(frame_count)
     mine = mine.reshape(HEADS, rows_each, 2, head_dim).transpose(2, 1, 0, 3)
     grad_inputs = mine.reshape(2, rows_each, model_width)
     return (grad_inputs, mean_error)

time: 359 us -> 306 us (0.85)
  local copies, waits for them, and re-layouts: 87.7 us -> 50.1 us
  waiting for transfers between devices: 45 us -> 30.4 us
  starting transfers between devices: 41.1 us -> 28.4 us
  blocking collectives: 64.3 us -> 76 us
  matrix products: 67.7 us -> 72.6 us
    all_to_all x1 -> x2, blocking collectives: 21.2 us -> 56 us  [the longest x1 47 us: shards(): lax.all_to_all(partial, 'dp', split_axis=0, concat_axis=0, tiled=True)]
    unnamed x1 -> x0, blocking collectives: 21.3 us -> none
    all_to_all x4 -> x1, waiting for transfers between devices: 29.6 us -> 10.9 us  [shards(): lax.all_to_all(by_head, 'seq', split_axis=1, concat_axis=0, tiled=True)]
    slice x5 -> x2, local copies, waits for them, and re-layouts: 18.4 us -> 0.59 us  [the longest x1 0.58 us: shards(): square_sum, frame_count = (totals[0], totals[1])]
    all_to_all x4 -> x1, starting transfers between devices: 22 us -> 8.35 us  [shards(): lax.all_to_all(by_head, 'seq', split_axis=1, concat_axis=0, tiled=True)]
    squeeze x3 -> x0, local copies, waits for them, and re-layouts: 12.4 us -> none  [the longest x1 4.38 us: shards(): w_inputs[0]]
    all_to_all x1, waiting for transfers between devices: 0.01 us -> 6.56 us  [shards(): lax.all_to_all(head_out, 'seq', split_axis=1, concat_axis=2, tiled=True)]
    unnamed x33 -> x35, local copies, waits for them, and re-layouts: 15.5 us -> 9.66 us
  transfers between devices with their start and end apart: 12 -> 9, of which waited for: 5 -> 5; matrix products, arithmetic and copies ran while one was open for 52% -> 46% of each run, Pallas kernels for 0% -> 0%
where the time goes in v2:
time: 306 us; the launch traced here: 304 us
  blocking collectives  76 us (25%)
  matrix products  72.6 us (24%)
  local copies, waits for them, and re-layouts  50.1 us (16%)
  waiting for transfers between devices  30.4 us (10%)
  starting transfers between devices  28.4 us (9%)
  other arithmetic  28 us (9%)
  between operations  18.8 us (6%)
    all_to_all x1, blocking collectives, shards(): lax.all_to_all(partial, 'dp', split_axis=0, concat_axis=0, tiled=True)  47 us
    all_gather x1, blocking collectives, shards(): lax.all_gather(stacked, 'seq', axis=1, tiled=True)  20 us
    dot_general x1, matrix products, split_product(): jnp.einsum(form, upper_part, other, preferred_element_type=jnp.float32)  15.8 us
    dot_general x1, matrix products, split_product(): jnp.einsum(form, lower_part, other, preferred_element_type=jnp.float32)  15.1 us
    unnamed x1, other arithmetic  12.4 us
    all_to_all x1, waiting for transfers between devices, shards(): lax.all_to_all(by_head, 'seq', split_axis=1, concat_axis=0, tiled=True)  10.9 us
    unnamed x35, local copies, waits for them, and re-layouts  9.66 us
    all_to_all x1, blocking collectives, shards(): lax.all_to_all(partial, 'seq', split_axis=0, concat_axis=0, tiled=True)  9.1 us
  transfers between devices with their start and end apart: 9, of which 5 were waited for; matrix products, arithmetic and copies ran while one was open for 46% of the time, Pallas kernels for 0%

profile of v2, /device:TPU:1, one launch (start us, length us, event | category | flops | bytes accessed | tf_op | source)
XLA Modules:
  0.0 304.4 jit_solution(6594554172339820792)
XLA Ops:
  8.9 20.0 %all_gather.10 = bf16[4,64,1024]{2,0,1:T(4,128)(2,1)S(1)} all-gather(bf16[4,4,1024]{2,0,1:T(4,128)(2,1)S(1)} %pad_maximum_fusion.3), channel_id=1, replica_groups=mesh['dp'=16,'seq'=16] {'seq'}, dimensions={1}, use_global_device_ids=true | all-gather | bytes 557056 | tf_op jit(solution)/shard_map/all_gather | solution.py:112
  28.9 1.0 copy.87
  30.9 3.9 %convolution_convert_fusion = bf16[128,3072]{1,0:T(8,128)(2,1)S(1)} fusion(bf16[1024,3072]{1,0:T(8,128)(2,1)} %param.22, bf16[1,128,1024]{2,1,0:T(8,128)(2,1)S(1)} %multiply_convert_fusion), kind=kOutput, calls=%fused_computation.23 | convolution fusion | flops 805699584 | bytes 7340032 | tf_op jit(solution)/shard_map/dot_general | solution.py:120
  34.8 1.2 copy.91
  36.0 2.1 copy.92
  38.2 4.7 %all-to-all-start = ((bf16[1,128,3,16,64]{1,4,2,0,3:T(8,128)(2,1)}), bf16[1,128,3,16,64]{1,4,2,0,3:T(8,128)(2,1)S(1)}, u32[]{:S(2)}, u32[]{:S(2)}) async-start(bf16[1,128,3,16,64]{1,4,2,0,3:T(8,128)(2,1)} %copy.92), calls=%async_computation | async-start | bytes 1572864 | tf_op jit(solution)/shard_map/all_to_all | solution.py:124
  44.4 8.9 %all-to-all-done = bf16[1,128,3,16,64]{1,4,2,0,3:T(8,128)(2,1)S(1)} async-done(((bf16[1,128,3,16,64]{1,4,2,0,3:T(8,128)(2,1)}), bf16[1,128,3,16,64]{1,4,2,0,3:T(8,128)(2,1)S(1)}, u32[]{:S(2)}, u32[]{:S(2)}) %all-to-all-start) | async-done | bytes 786464 | tf_op jit(solution)/shard_map/all_to_all | solution.py:124
  53.3 1.4 copy.93
  54.7 1.4 squeeze.50
  57.1 1.2 copy.108
  58.3 1.3 copy.95
  59.6 1.0 copy.96
  60.6 17.6 %while.29 = (s32[]{:T(128)}, bf16[4,512,64]{1,2,0:T(8,128)(2,1)}, bf16[4,512,64]{2,1,0:T(8,128)(2,1)S(1)}, bf16[2048,64]{1,0:T(8,128)(2,1)S(1)}, bf16[2048,64]{1,0:T(8,128)(2,1)}, /*index=5*/s32[]{:T(128)}, s32[]{:T(128)}) while((s32[]{:T(128)}, bf16[4,512,64]{1,2,0:T(8,128)(2,1)}, bf16[4,512,64]{2,1,0:T(8,128)(2,1)S(1)}, ...), condition=%wide.region_6.7_spmd.clone, body=%wide.region_3.6_spmd.clone.sunk | while | flops 281054208 | bytes 14657661 | solution.py:59
  62.1 0.9 fusion.106
  63.1 1.9 fusion.107
  67.5 1.9 fusion.107
  70.8 0.9 fusion.106
  71.9 1.9 fusion.107
  75.3 0.9 fusion.106
  76.3 1.9 fusion.107
  78.2 2.0 copy.109
  80.2 3.3 %reshape.424 = bf16[1,2048,1,64]{3,2,0,1:T(2,128)(2,1)S(1)} reshape(bf16[4,512,64]{2,1,0:T(8,128)(2,1)} %copy.109) | data formatting | bytes 524288 | tf_op jit(solution)/shard_map/while/body/jit(dynamic_update_index_in_dim)/broadcast_in_dim | solution.py:125
  84.0 12.4 %reduce.12 = bf16[2048,64]{1,0:T(8,128)(2,1)} reduce(bf16[2048,1,1,64]{3,2,1,0:T(2,128)(2,1)S(1)} %bitcast.170, bf16[]{:T(256)} %broadcast.272), dimensions={1,2}, to_apply=%bitcast.127.reduce_sub_computation | reduce | bytes 524290
  96.3 2.2 reshape.425
  98.5 3.8 %all-to-all-start.1 = ((bf16[16,2,4096]{2,1,0:T(2,128)(2,1)}), bf16[16,2,4096]{2,1,0:T(2,128)(2,1)S(1)}, u32[]{:S(2)}, u32[]{:S(2)}) async-start(bf16[16,2,4096]{2,1,0:T(2,128)(2,1)} %reshape.425), calls=%async_computation.1 | async-start | bytes 524288 | tf_op jit(solution)/shard_map/all_to_all | solution.py:126
  103.0 6.6 %all-to-all-done.1 = bf16[16,2,4096]{2,1,0:T(2,128)(2,1)S(1)} async-done(((bf16[16,2,4096]{2,1,0:T(2,128)(2,1)}), bf16[16,2,4096]{2,1,0:T(2,128)(2,1)S(1)}, u32[]{:S(2)}, u32[]{:S(2)}) %all-to-all-start.1) | async-done | bytes 262176 | tf_op jit(solution)/shard_map/all_to_all | solution.py:126
  110.2 1.7 copy.99
  111.9 1.0 copy.113
  113.0 1.3 fusion.79
  114.3 2.0 fusion.38
  116.4 2.0 fusion.37
  119.2 1.3 collective-permute-start.1
  120.5 4.7 %collective-permute-start = (bf16[1,64,2048]{2,1,0:T(8,128)(2,1)S(1)}, bf16[1,64,2048]{2,1,0:T(8,128)(2,1)}, u32[]{:S(2)}, u32[]{:S(2)}) collective-permute-start(bf16[1,64,2048]{2,1,0:T(8,128)(2,1)S(1)} %get-tuple-element.151), channel_id=1, source_target_pairs={{0,1},{1,2},{2,3},{3,4},{4,5},{5,6},{6,7},{7,8},{8,9},{9,10},{10,1... | collective-permute-start | bytes 786440 | tf_op jit(solution)/shard_map/ppermute | solution.py:20
  125.2 2.0 fusion.36
  127.8 1.1 pad_maximum_fusion.1
  129.8 1.4 copy.90
  131.2 1.0 copy.89
  132.2 3.1 %fusion.78 = (f32[16,128]{1,0:T(8,128)S(1)}, f32[16,128,256]{2,1,0:T(8,128)}) fusion(pred[128,256]{1,0:T(8,128)(4,1)S(1)} %or_and_fusion, bf16[128,16,64]{0,2,1:T(8,128)(2,1)S(1)} %bitcast.184, bf16[256,16,64]{0,2,1:T(8,128)(2,1)} %bitcast.183), kind=kOutput, calls=%fused_computation.113 | convolution fusion | flops 69206272 | bytes 2924544 | tf_op jit(solution)/shard_map/sub | solution.py:159
  135.4 2.2 convolution_convert_fusion.1
  137.6 2.8 multiply_reduce_fusion.1
  140.4 2.5 fusion.35
  143.1 1.8 fusion.80
  144.9 15.8 %fusion.48 = f32[16,64,256]{2,1,0:T(8,128)} fusion(bf16[128,16,64]{0,2,1:T(8,128)(2,1)S(1)} %bitcast.186, f32[16,128,256]{2,1,0:T(8,128)} %fusion.80, f32[16,128,256]{2,1,0:T(8,128)} %get-tuple-element.156, f32[16,128]{1,0:T(8,128)S(1)} %get-tuple-element.155), kind=kOutput, calls=%fused_computation.71 | convolution fusion | flops 70781184 | bytes 5513216 | tf_op jit(solution)/shard_map/bhrw,brhd->bwhd/dot_general | solution.py:83
  160.7 15.1 %convolution_add_fusion = f32[16,64,256]{2,1,0:T(8,128)S(1)} fusion(f32[16,64,256]{2,1,0:T(8,128)} %fusion.48, bf16[128,16,64]{0,2,1:T(8,128)(2,1)} %bitcast.185, f32[16,128,256]{2,1,0:T(8,128)} %fusion.80, f32[16,128,256]{2,1,0:T(8,128)} %get-tuple-element.156, f32[16,128]{1,0:T(8,128)S(1)} %get-tuple-element.155), kind=kOutput, calls=%fused_computation.46 | convolution fusion | flops 72616192 | bytes 6561792 | tf_op jit(solution)/shard_map/bhrw,brhd->bwhd/dot_general | solution.py:83
  175.8 2.1 fusion.58
  178.1 1.0 fusion.74
  179.1 3.8 %collective-permute-start.2 = (bf16[1,64,2048]{1,2,0:T(8,128)(2,1)S(1)}, bf16[1,64,2048]{1,2,0:T(8,128)(2,1)S(1)}, u32[]{:S(2)}, u32[]{:S(2)}) collective-permute-start(bf16[1,64,2048]{1,2,0:T(8,128)(2,1)S(1)} %get-tuple-element.145), channel_id=1, source_target_pairs={{0,1},{1,2},{2,3},{3,4},{4,5},{5,6},{6,7},{7,8},{8,9},{9,10},{10,1... | collective-permute-start | bytes 786440 | tf_op jit(solution)/shard_map/ppermute | solution.py:31
  182.9 1.6 collective-permute-start.3
  184.5 1.3 fusion.39
  185.8 3.2 %collective-permute-done.2 = bf16[1,64,2048]{1,2,0:T(8,128)(2,1)S(1)} collective-permute-done((bf16[1,64,2048]{1,2,0:T(8,128)(2,1)S(1)}, bf16[1,64,2048]{1,2,0:T(8,128)(2,1)S(1)}, u32[]{:S(2)}, u32[]{:S(2)}) %collective-permute-start.2) | collective-permute-done | bytes 262176 | tf_op jit(solution)/shard_map/ppermute | solution.py:31
  189.0 1.4 fusion.41
  190.4 5.4 %scatter-add.6 = f32[1,128,2048]{1,2,0:T(8,128)} dynamic-update-slice(f32[1,128,2048]{1,2,0:T(8,128)} %fusion.39, f32[1,64,2048]{1,2,0:T(8,128)} %fusion.41, s32[]{:T(128)} %constant.134.clone.1, s32[]{:T(128)} %constant.134.clone.1, s32[]{:T(128)} %constant.134.clone.1) | dynamic-update-slice | bytes 1048580 | tf_op jit(solution)/shard_map/scatter-add | solution.py:196
  195.8 2.8 slice_add_fusion
  198.7 8.6 %scatter-add.9 = f32[1,128,2048]{1,2,0:T(8,128)S(1)} dynamic-update-slice(f32[1,128,2048]{1,2,0:T(8,128)S(1)} %copy-done.2, f32[1,64,2048]{1,2,0:T(8,128)} %slice_add_fusion, s32[]{:T(128)} %constant.134.clone.1, s32[]{:T(128)} %constant.145.clone.1, s32[]{:T(128)} %constant.134.clone.1) | dynamic-update-slice | bytes 1048580 | tf_op jit(solution)/shard_map/scatter-add | solution.py:197
  207.3 1.0 copy.102
  208.3 8.3 %all-to-all-start.2 = ((f32[128,16,2,64]{0,3,2,1:T(8,128)}), f32[128,16,2,64]{0,3,2,1:T(8,128)S(1)}, u32[]{:S(2)}, u32[]{:S(2)}) async-start(f32[128,16,2,64]{0,3,2,1:T(8,128)} %copy.102), calls=%async_computation.2 | async-start | bytes 2097152 | tf_op jit(solution)/shard_map/all_to_all | solution.py:199
  216.7 1.3 compare_select_fusion.1
  218.0 10.9 %all-to-all-done.2 = f32[128,16,2,64]{0,3,2,1:T(8,128)S(1)} async-done(((f32[128,16,2,64]{0,3,2,1:T(8,128)}), f32[128,16,2,64]{0,3,2,1:T(8,128)S(1)}, u32[]{:S(2)}, u32[]{:S(2)}) %all-to-all-start.2) | async-done | bytes 1048608 | tf_op jit(solution)/shard_map/all_to_all | solution.py:199
  228.9 1.0 copy-done.3
  229.9 1.8 copy.103
  231.7 3.7 %fusion.16 = f32[1024,128]{1,0:T(8,128)S(1)} fusion(bf16[1,2048,1024]{2,1,0:T(8,128)(2,1)} %all-gather.6.cloned.1.call-done, f32[16,8,16,128]{3,2,1,0:T(8,128)S(1)} %bitcast.166), kind=kOutput, calls=%fused_computation.19 | convolution fusion | flops 537919488 | bytes 5767168 | tf_op jit(solution)/shard_map/rf,rg->fg/dot_general | solution.py:86
  235.4 1.5 fusion.30
  237.0 47.0 %all_to_all.55 = f32[16,16,5,128]{3,1,2,0:T(8,128)S(1)} all-to-all(f32[16,16,5,128]{3,1,2,0:T(8,128)S(1)} %pad_maximum_fusion.2), channel_id=1, replica_groups=mesh['dp'=16,'seq'=16] {'dp'}, dimensions={0} | all-to-all | bytes 1310720 | tf_op jit(solution)/shard_map/all_to_all | solution.py:209
  284.1 9.1 %all_to_all.56 = f32[16,5,128]{2,1,0:T(8,128)S(1)} all-to-all(f32[16,5,128]{2,1,0:T(8,128)S(1)} %copy.111), channel_id=1, replica_groups=mesh['dp'=16,'seq'=16] {'seq'}, dimensions={0} | all-to-all | bytes 81920 | tf_op jit(solution)/shard_map/all_to_all | solution.py:210
  (88 shorter events, 17.1 us)
Async XLA Ops:
  7.2 105.9 %copy-start = (bf16[1024,1024]{1,0:T(8,128)(2,1)S(1)}, bf16[1024,1024]{1,0:T(8,128)(2,1)}, u32[]{:S(2)}) copy-start(bf16[1024,1024]{1,0:T(8,128)(2,1)} %param.23) | copy-start | bytes 6291460
  7.2 23.3 %copy-start.6 = (bf16[1,128,1024]{2,1,0:T(8,128)(2,1)S(1)}, bf16[1,128,1024]{2,1,0:T(8,128)(2,1)}, u32[]{:S(2)}) copy-start(bf16[1,128,1024]{2,1,0:T(8,128)(2,1)} %param.16) | copy-start | bytes 786436
  7.2 23.3 %copy-start.7 = (bf16[1,128,1024]{2,1,0:T(8,128)(2,1)S(1)}, bf16[1,128,1024]{2,1,0:T(8,128)(2,1)}, u32[]{:S(2)}) copy-start(bf16[1,128,1024]{2,1,0:T(8,128)(2,1)} %param.17) | copy-start | bytes 786436
  7.2 23.6 %copy-start.13 = (f32[1024]{0:T(1024)S(1)}, f32[1024]{0:T(1024)}, u32[]{:S(2)}) copy-start(f32[1024]{0:T(1024)} %param.21) | copy-start | bytes 12292
  7.2 107.1 %all-gather.4.cloned.1.call-start = ((), (), s32[]{:S(2)}) async-start(), calls=%async_computation.5 | async-start | bytes 8912896 | tf_op jit(solution)/shard_map/all_gather | solution.py:111
  30.9 3.9 %copy-start.4 = (bf16[1,128,1024]{2,1,0:T(8,128)(2,1)}, bf16[1,128,1024]{2,1,0:T(8,128)(2,1)S(1)}, u32[]{:S(2)}) copy-start(bf16[1,128,1024]{2,1,0:T(8,128)(2,1)S(1)} %multiply_convert_fusion) | copy-start | bytes 786436
  36.0 8.3 %copy-start.12 = (s32[1,2048]{1,0:T(1,128)S(1)}, s32[1,2048]{1,0:T(1,128)}, u32[]{:S(2)}) copy-start(s32[1,2048]{1,0:T(1,128)} %param.19) | copy-start | bytes 24580
  38.2 15.1 %all-to-all-start = ((bf16[1,128,3,16,64]{1,4,2,0,3:T(8,128)(2,1)}), bf16[1,128,3,16,64]{1,4,2,0,3:T(8,128)(2,1)S(1)}, u32[]{:S(2)}, u32[]{:S(2)}) async-start(bf16[1,128,3,16,64]{1,4,2,0,3:T(8,128)(2,1)} %copy.92), calls=%async_computation | async-start | bytes 1572864 | tf_op jit(solution)/shard_map/all_to_all | solution.py:124
  42.8 188.9 %all-gather.6.cloned.1.call-start = ((), (), s32[]{:S(2)}) async-start(), calls=%async_computation.6 | async-start | bytes 4456448 | tf_op jit(solution)/shard_map/all_gather | solution.py:201
  62.1 1.0 copy-start.8
  66.4 1.0 copy-start.8
  70.8 1.1 copy-start.8
  75.3 1.1 copy-start.8
  98.5 11.0 %all-to-all-start.1 = ((bf16[16,2,4096]{2,1,0:T(2,128)(2,1)}), bf16[16,2,4096]{2,1,0:T(2,128)(2,1)S(1)}, u32[]{:S(2)}, u32[]{:S(2)}) async-start(bf16[16,2,4096]{2,1,0:T(2,128)(2,1)} %reshape.425), calls=%async_computation.1 | async-start | bytes 524288 | tf_op jit(solution)/shard_map/all_to_all | solution.py:126
  111.9 2.4 copy-start.5
  119.2 8.2 %collective-permute-start.1 = (bf16[1,64,2048]{2,1,0:T(8,128)(2,1)}, bf16[1,64,2048]{2,1,0:T(8,128)(2,1)}, u32[]{:S(2)}, u32[]{:S(2)}) collective-permute-start(bf16[1,64,2048]{2,1,0:T(8,128)(2,1)} %get-tuple-element.152), channel_id=1, source_target_pairs={{1,0},{2,1},{3,2},{4,3},{5,4},{6,5},{7,6},{8,7},{9,8},{10,9},{11,1... | collective-permute-start | bytes 786440 | tf_op jit(solution)/shard_map/ppermute | solution.py:23
  120.5 7.3 %collective-permute-start = (bf16[1,64,2048]{2,1,0:T(8,128)(2,1)S(1)}, bf16[1,64,2048]{2,1,0:T(8,128)(2,1)}, u32[]{:S(2)}, u32[]{:S(2)}) collective-permute-start(bf16[1,64,2048]{2,1,0:T(8,128)(2,1)S(1)} %get-tuple-element.151), channel_id=1, source_target_pairs={{0,1},{1,2},{2,3},{3,4},{4,5},{5,6},{6,7},{7,8},{8,9},{9,10},{10,1... | collective-permute-start | bytes 786440 | tf_op jit(solution)/shard_map/ppermute | solution.py:20
  127.4 4.8 %copy-start.10 = (bf16[128,1024]{0,1:T(8,128)(2,1)}, bf16[128,1024]{0,1:T(8,128)(2,1)S(1)}, u32[]{:S(2)}) copy-start(bf16[128,1024]{0,1:T(8,128)(2,1)S(1)} %copy.88) | copy-start | bytes 786436
  135.4 2.2 copy-start.9
  142.9 2.0 copy-start.11
  179.1 9.9 %collective-permute-start.2 = (bf16[1,64,2048]{1,2,0:T(8,128)(2,1)S(1)}, bf16[1,64,2048]{1,2,0:T(8,128)(2,1)S(1)}, u32[]{:S(2)}, u32[]{:S(2)}) collective-permute-start(bf16[1,64,2048]{1,2,0:T(8,128)(2,1)S(1)} %get-tuple-element.145), channel_id=1, source_target_pairs={{0,1},{1,2},{2,3},{3,4},{4,5},{5,6},{6,7},{7,8},{8,9},{9,10},{10,1... | collective-permute-start | bytes 786440 | tf_op jit(solution)/shard_map/ppermute | solution.py:31
  182.9 12.9 %collective-permute-start.3 = (bf16[1,64,2048]{1,2,0:T(8,128)(2,1)}, bf16[1,64,2048]{1,2,0:T(8,128)(2,1)}, u32[]{:S(2)}, u32[]{:S(2)}) collective-permute-start(bf16[1,64,2048]{1,2,0:T(8,128)(2,1)} %get-tuple-element.144), channel_id=1, source_target_pairs={{1,0},{2,1},{3,2},{4,3},{5,4},{6,5},{7,6},{8,7},{9,8},{10,9},{11,1... | collective-permute-start | bytes 786440 | tf_op jit(solution)/shard_map/ppermute | solution.py:31
  195.8 2.8 copy-start.2
  208.3 20.5 %all-to-all-start.2 = ((f32[128,16,2,64]{0,3,2,1:T(8,128)}), f32[128,16,2,64]{0,3,2,1:T(8,128)S(1)}, u32[]{:S(2)}, u32[]{:S(2)}) async-start(f32[128,16,2,64]{0,3,2,1:T(8,128)} %copy.102), calls=%async_computation.2 | async-start | bytes 2097152 | tf_op jit(solution)/shard_map/all_to_all | solution.py:199
  228.9 1.0 copy-start.3
  231.7 3.7 %copy-start.1 = (bf16[1,2048,1024]{2,1,0:T(8,128)(2,1)S(1)}, bf16[1,2048,1024]{2,1,0:T(8,128)(2,1)}, u32[]{:S(2)}) copy-start(bf16[1,2048,1024]{2,1,0:T(8,128)(2,1)} %all-gather.6.cloned.1.call-done) | copy-start | bytes 12582916
Sparse Core Ops, SparseCore 0:
  30.0 62.3 all-gather.3
  94.8 58.1 all-gather.5

commit v3 on v2

--- a/solution.py
+++ b/solution.py
@@ -66,6 +66,13 @@
         lambda element: full_attention(element[0], element[1], element[2], bias_one), stacked
     )
     return jnp.transpose(result, (1, 0, 2))
+
+
+def teacher_direct(proj_one, bias_one):
+    def one_head(part):
+        return attend_block(part[:, 0], part[:, 1], part[:, 2], bias_one)
+
+    return jax.vmap(one_head, in_axes=2, out_axes=1)(proj_one)
 
 
 def build_allowed(query_group, query_pos, key_group, key_pos, lengths):
@@ -122,7 +129,7 @@
     )
     teacher_proj = teacher_proj.reshape(dialogs, shard_rows, 3, HEADS, head_dim)
     by_heads = lax.all_to_all(teacher_proj, "seq", split_axis=3, concat_axis=1, tiled=True)
-    head_out = lax.map(lambda element: teacher_heads(element[0], element[1]), (by_heads, key_bias))
+    head_out = jax.vmap(teacher_direct)(by_heads, key_bias)
     by_frames = lax.all_to_all(head_out, "seq", split_axis=1, concat_axis=2, tiled=True)
     teacher_vel = jnp.dot(
         by_frames.reshape(dialogs * shard_rows, model_width),
@@ -177,6 +184,7 @@
         "brhd,bwhd->bhrw", grad_mix, value_rows, preferred_element_type=jnp.float32
     )
     grad_score = probs * (grad_prob - jnp.sum(probs * grad_prob, axis=-1, keepdims=True)) * scaling
+    grad_score = lax.optimization_barrier(grad_score)
     grad_key = split_product("bhrw,brhd->bwhd", grad_score, queries, True)
     grad_value = jnp.einsum(
         "bhrw,brhd->bwhd", probs_low, grad_mix, preferred_element_type=jnp.float32
@@ -201,17 +209,26 @@
     normed_all = lax.all_gather(flat_rows, "seq", axis=0, tiled=True)
     partial = split_product("rf,rg->fg", head_grads, normed_all, False)
     dp_count = lax.axis_size("dp")
-    partial = partial.reshape(dp_count, seq_count, rows_each, 2 * head_dim)
+    partial = partial.reshape(dp_count, -1)
     lane = jnp.arange(2 * head_dim)
     scalars = jnp.where(lane == 0, square_local, jnp.where(lane == 1, count_local, 0.0))
-    scalars = jnp.broadcast_to(scalars, (dp_count, seq_count, 1, 2 * head_dim))
-    partial = jnp.concatenate((partial, scalars), axis=2)
+    partial = jnp.concatenate(
+        (partial, jnp.broadcast_to(scalars, (dp_count, 2 * head_dim))), axis=1
+    )
     partial = lax.all_to_all(partial, "dp", split_axis=0, concat_axis=0, tiled=True).sum(0)
+    block = rows_each * 2 * head_dim
+    partial = jnp.concatenate(
+        (
+            partial[: seq_count * block].reshape(seq_count, block),
+            jnp.broadcast_to(partial[seq_count * block :], (seq_count, 2 * head_dim)),
+        ),
+        axis=1,
+    )
     mine = lax.all_to_all(partial, "seq", split_axis=0, concat_axis=0, tiled=True)
-    totals = mine[:, rows_each].sum(0)
+    totals = mine[:, block:].sum(0)
     square_sum, frame_count = totals[0], totals[1]
     mean_error = square_sum / (frame_count * model_width)
-    mine = mine[:, :rows_each] * lax.rsqrt(frame_count)
+    mine = mine[:, :block] * lax.rsqrt(frame_count)
     mine = mine.reshape(HEADS, rows_each, 2, head_dim).transpose(2, 1, 0, 3)
     grad_inputs = mine.reshape(2, rows_each, model_width)
     return (grad_inputs, mean_error)

time: 306 us -> 253 us (0.83)
  matrix products: 72.6 us -> 43.1 us
  waiting for transfers between devices: 30.4 us -> 50.2 us
  blocking collectives: 76 us -> 58.7 us
  local copies, waits for them, and re-layouts: 50.1 us -> 33.7 us
  starting transfers between devices: 28.4 us -> 23.4 us
  other arithmetic: 28 us -> 23.2 us
    all_to_all x1, blocking collectives: 47 us -> 29.6 us  [shards(): lax.all_to_all(partial, 'dp', split_axis=0, concat_axis=0, tiled=True)]
    dot_general x1, matrix products: 15.8 us -> 0.29 us  [split_product(): jnp.einsum(form, upper_part, other, preferred_element_type=jnp.float32)]
    ppermute x2, waiting for transfers between devices: 3.2 us -> 16.4 us  [from_behind(): return lax.ppermute(block, axis, route)]
    dot_general x1, matrix products: 15.1 us -> 2.84 us  [split_product(): jnp.einsum(form, lower_part, other, preferred_element_type=jnp.float32)]
    sub x0 -> x1, matrix products: none -> 6.48 us  [shards(): grad_prob - jnp.sum(probs * grad_prob, axis=-1, keepdims=True)]
    broadcast_in_dim x3 -> x0, local copies, waits for them, and re-layouts: 5.27 us -> none  [the longest x2 5.26 us: shards(): lax.map(lambda element: teacher_heads(element[0], element[1]), (by_heads,...]
    ppermute x1, waiting for transfers between devices: 0.01 us -> 5.09 us  [with_halo(): lax.ppermute(lax.slice_in_dim(block, 0, width, axis=dim), axis, backward)]
    dot_general x4 -> x1, matrix products: 7.51 us -> 4.08 us  [attend_block(): jnp.dot(probs_low, values, preferred_element_type=jnp.float32)]
  transfers between devices with their start and end apart: 9 -> 9, of which waited for: 5 -> 5; matrix products, arithmetic and copies ran while one was open for 46% -> 35% of each run, Pallas kernels for 0% -> 0%
where the time goes in v3:
time: 253 us; the launch traced here: 251 us
  blocking collectives  58.7 us (23%)
  waiting for transfers between devices  50.2 us (20%)
  matrix products  43.1 us (17%)
  local copies, waits for them, and re-layouts  33.7 us (13%)
  starting transfers between devices  23.4 us (9%)
  other arithmetic  23.2 us (9%)
  between operations  19.1 us (8%)
    all_to_all x1, blocking collectives, shards(): lax.all_to_all(partial, 'dp', split_axis=0, concat_axis=0, tiled=True)  29.6 us
    all_gather x1, blocking collectives, shards(): lax.all_gather(stacked, 'seq', axis=1, tiled=True)  20 us
    ppermute x2, waiting for transfers between devices, from_behind(): return lax.ppermute(block, axis, route)  16.4 us
    all_to_all x1, waiting for transfers between devices, shards(): lax.all_to_all(by_head, 'seq', split_axis=1, concat_axis=0, tiled=True)  12.5 us
    unnamed x1, other arithmetic  12.3 us
    all_to_all x1, blocking collectives, shards(): lax.all_to_all(partial, 'seq', split_axis=0, concat_axis=0, tiled=True)  9.11 us
    all_to_all x1, waiting for transfers between devices, shards(): lax.all_to_all(teacher_proj, 'seq', split_axis=3, concat_axis=1, tiled=True)  8.89 us
    all_to_all x1, starting transfers between devices, shards(): lax.all_to_all(by_head, 'seq', split_axis=1, concat_axis=0, tiled=True)  7.84 us
  transfers between devices with their start and end apart: 9, of which 5 were waited for; matrix products, arithmetic and copies ran while one was open for 35% of the time, Pallas kernels for 0%

profile of v3, /device:TPU:1, one launch (start us, length us, event | category | flops | bytes accessed | tf_op | source)
XLA Modules:
  0.0 251.4 jit_solution(8563299708727312885)
XLA Ops:
  7.3 0.9 copy.48
  8.2 0.7 copy.49
  8.9 20.0 %all_gather.10 = bf16[4,64,1024]{2,0,1:T(4,128)(2,1)S(1)} all-gather(bf16[4,4,1024]{2,0,1:T(4,128)(2,1)S(1)} %pad_maximum_fusion.4), channel_id=1, replica_groups=mesh['dp'=16,'seq'=16] {'seq'}, dimensions={1}, use_global_device_ids=true | all-gather | bytes 557056 | tf_op jit(solution)/shard_map/all_gather | solution.py:119
  28.9 1.0 copy.50
  30.6 0.2 multiply_reduce_fusion.2
  31.0 3.9 %convolution_convert_fusion = bf16[128,3072]{1,0:T(8,128)(2,1)S(1)} fusion(bf16[1024,3072]{1,0:T(8,128)(2,1)} %param.20, bf16[1,128,1024]{2,1,0:T(8,128)(2,1)S(1)} %multiply_convert_fusion), kind=kOutput, calls=%fused_computation.12 | convolution fusion | flops 805699584 | bytes 7340032 | tf_op jit(solution)/shard_map/dot_general | solution.py:127
  34.8 1.2 copy.54
  36.1 2.1 copy.55
  38.2 4.7 %all-to-all-start = ((bf16[1,128,3,16,64]{1,4,2,0,3:T(8,128)(2,1)}), bf16[1,128,3,16,64]{1,4,2,0,3:T(8,128)(2,1)S(1)}, u32[]{:S(2)}, u32[]{:S(2)}) async-start(bf16[1,128,3,16,64]{1,4,2,0,3:T(8,128)(2,1)} %copy.55), calls=%async_computation | async-start | bytes 1572864 | tf_op jit(solution)/shard_map/all_to_all | solution.py:131
  42.9 0.7 all-gather.6.cloned.1.call-update
  44.4 8.9 %all-to-all-done = bf16[1,128,3,16,64]{1,4,2,0,3:T(8,128)(2,1)S(1)} async-done(((bf16[1,128,3,16,64]{1,4,2,0,3:T(8,128)(2,1)}), bf16[1,128,3,16,64]{1,4,2,0,3:T(8,128)(2,1)S(1)}, u32[]{:S(2)}, u32[]{:S(2)}) %all-to-all-start) | async-done | bytes 786464 | tf_op jit(solution)/shard_map/all_to_all | solution.py:131
  53.4 2.6 %fusion.2 = (f32[2048]{0:T(1024)S(1)}, f32[2048,2048]{0,1:T(8,128)S(1)}) fusion(f32[2048]{0:T(1024)S(1)} %fusion.57, bf16[1,2048,3,1,64]{1,4,2,3,0:T(8,128)(2,1)S(1)} %copy_bitcast_fusion), kind=kOutput, calls=%fused_computation.5 | convolution fusion | flops 549451776 | bytes 17317888 | tf_op jit(solution)/shard_map/vmap(vmap())/dot_general | solution.py:45
  56.1 4.8 %fusion.3 = f32[2048]{0:T(1024)S(1)} fusion(f32[2048,2048]{0,1:T(8,128)S(1)} %get-tuple-element.39, f32[2048]{0:T(1024)S(1)} %get-tuple-element.38, f32[2048]{0:T(1024)S(1)} %fusion.57), kind=kLoop, calls=%fused_computation.6 | loop fusion | flops 16775168 | bytes 16801792 | tf_op jit(solution)/shard_map/vmap(vmap())/reduce_sum | solution.py:51
  60.8 4.1 %fusion.10 = bf16[1,2048,1,64]{1,3,2,0:T(8,128)(2,1)S(1)} fusion(f32[2048,2048]{0,1:T(8,128)S(1)} %get-tuple-element.39, f32[2048]{0:T(1024)S(1)} %fusion.3, f32[2048]{0:T(1024)S(1)} %get-tuple-element.38, f32[2048]{0:T(1024)S(1)} %fusion.57, bf16[1,2048,3,1,64]{1,4,2,3,0:T(8,128)(2,1)S(1)} %copy_bitcast_fusion), kind=kOutput, calls=%fused_computation.19 | convolution fusion | flops 557973504 | bytes 17326080 | tf_op jit(solution)/shard_map/vmap(vmap())/dot_general | solution.py:52
  64.9 0.7 copy.57
  65.7 0.5 broadcast.261
  66.2 12.3 %reduce.16 = bf16[2048,64]{1,0:T(8,128)(2,1)} reduce(bf16[2048,1,1,64]{3,2,1,0:T(2,128)(2,1)S(1)} %bitcast.171, bf16[]{:T(256)} %broadcast.261), dimensions={1,2}, to_apply=%bitcast.131.reduce_sub_computation | reduce | bytes 524290
  78.5 2.2 reshape.461
  80.7 3.8 %all-to-all-start.1 = ((bf16[16,2,4096]{2,1,0:T(2,128)(2,1)}), bf16[16,2,4096]{2,1,0:T(2,128)(2,1)S(1)}, u32[]{:S(2)}, u32[]{:S(2)}) async-start(bf16[16,2,4096]{2,1,0:T(2,128)(2,1)} %reshape.461), calls=%async_computation.1 | async-start | bytes 524288 | tf_op jit(solution)/shard_map/all_to_all | solution.py:133
  84.4 0.6 convert_reduce_fusion
  85.2 6.6 %all-to-all-done.1 = bf16[16,2,4096]{2,1,0:T(2,128)(2,1)S(1)} async-done(((bf16[16,2,4096]{2,1,0:T(2,128)(2,1)}), bf16[16,2,4096]{2,1,0:T(2,128)(2,1)S(1)}, u32[]{:S(2)}, u32[]{:S(2)}) %all-to-all-start.1) | async-done | bytes 262176 | tf_op jit(solution)/shard_map/all_to_all | solution.py:133
  91.7 0.6 reshape.462
  92.4 1.7 copy.58
  94.1 1.0 copy.66
  95.2 1.3 fusion.66
  96.5 2.0 fusion.28
  98.6 2.0 fusion.29
  100.7 2.2 collective-permute-start
  102.9 1.3 collective-permute-start.1
  104.2 2.1 fusion.27
  106.5 5.1 %collective-permute-done.1 = bf16[1,64,2048]{2,1,0:T(8,128)(2,1)S(1)} collective-permute-done((bf16[1,64,2048]{2,1,0:T(8,128)(2,1)S(1)}, bf16[1,64,2048]{2,1,0:T(8,128)(2,1)S(1)}, u32[]{:S(2)}, u32[]{:S(2)}) %collective-permute-start.1) | collective-permute-done | bytes 262176 | tf_op jit(solution)/shard_map/ppermute | solution.py:23
  111.8 0.2 copy.52
  112.0 0.2 copy.53
  112.2 2.1 fusion.65
  114.3 2.2 convolution_convert_fusion.1
  116.5 2.7 %multiply_reduce_fusion.1 = (f32[]{:T(128)}, bf16[128,1024]{1,0:T(8,128)(2,1)S(1)}) fusion(f32[128,1024]{1,0:T(8,128)S(1)} %copy-done.8, bf16[128,1024]{0,1:T(8,128)(2,1)S(1)} %bitcast.190, bf16[4,1024,1024]{2,1,0:T(8,128)(2,1)} %all-gather.4.cloned.1.call-done, pred[128]{0:T(512)(128)(4,1)S(1)} %get-tuple-element.27), kind=kOutput, calls=%fused_computation.64 | convolution fusion | flops 269090816 | bytes 3145860 | tf_op jit(solution)/shard_map/dot_general | solution.py:173
  119.3 2.4 fusion.26
  121.9 6.5 %multiply_bitcast_fusion = f32[1,16,128,256]{3,2,1,0:T(8,128)S(1)} fusion(bf16[128,16,64]{0,2,1:T(8,128)(2,1)S(1)} %bitcast.183, bf16[256,16,64]{0,2,1:T(8,128)(2,1)S(1)} %bitcast.181, f32[16,128,256]{2,1,0:T(8,128)} %get-tuple-element.41, f32[16,128]{1,0:T(8,128)S(1)} %get-tuple-element.40), kind=kOutput, calls=%fused_computation.29 | convolution fusion | flops 137365760 | bytes 4988928 | tf_op jit(solution)/shard_map/sub | solution.py:186
  128.4 1.3 copy-done.3
  129.7 0.3 fusion.36
  130.0 2.8 %convolution_add_fusion = f32[16,64,256]{2,1,0:T(8,128)S(1)} fusion(f32[16,64,256]{2,1,0:T(8,128)S(1)} %fusion.36, bf16[128,16,64]{0,2,1:T(8,128)(2,1)S(1)} %bitcast.176, f32[1,16,128,256]{3,2,1,0:T(8,128)} %copy-done.3), kind=kOutput, calls=%fused_computation.37 | convolution fusion | flops 69468160 | bytes 4456448 | tf_op jit(solution)/shard_map/bhrw,brhd->bwhd/dot_general | solution.py:90
  133.0 0.8 fusion.44
  133.9 1.0 fusion.61
  134.9 2.2 collective-permute-start.2
  137.2 1.3 collective-permute-start.3
  138.5 0.3 fusion.32
  138.8 16.4 %collective-permute-done.2 = bf16[1,64,2048]{1,2,0:T(8,128)(2,1)S(1)} collective-permute-done((bf16[1,64,2048]{1,2,0:T(8,128)(2,1)S(1)}, bf16[1,64,2048]{1,2,0:T(8,128)(2,1)S(1)}, u32[]{:S(2)}, u32[]{:S(2)}) %collective-permute-start.2) | collective-permute-done | bytes 262176 | tf_op jit(solution)/shard_map/ppermute | solution.py:31
  155.3 1.3 fusion.34
  156.6 7.6 %scatter-add.6 = f32[1,128,2048]{1,2,0:T(8,128)S(1)} dynamic-update-slice(f32[1,128,2048]{1,2,0:T(8,128)S(1)} %fusion.32, f32[1,64,2048]{1,2,0:T(8,128)} %fusion.34, s32[]{:T(128)} %constant.92.clone.1, s32[]{:T(128)} %constant.92.clone.1, s32[]{:T(128)} %constant.92.clone.1) | dynamic-update-slice | bytes 1048580 | tf_op jit(solution)/shard_map/scatter-add | solution.py:204
  164.2 1.4 slice_add_fusion
  165.6 6.1 %scatter-add.9 = f32[1,128,2048]{1,2,0:T(8,128)S(1)} dynamic-update-slice(f32[1,128,2048]{1,2,0:T(8,128)S(1)} %scatter-add.6, f32[1,64,2048]{1,2,0:T(8,128)S(1)} %slice_add_fusion, s32[]{:T(128)} %constant.92.clone.1, s32[]{:T(128)} %constant.102.clone.1, s32[]{:T(128)} %constant.92.clone.1) | dynamic-update-slice | bytes 1048580 | tf_op jit(solution)/shard_map/scatter-add | solution.py:205
  171.7 1.0 copy.61
  172.7 7.8 %all-to-all-start.2 = ((f32[128,16,2,64]{0,3,2,1:T(8,128)}), f32[128,16,2,64]{0,3,2,1:T(8,128)S(1)}, u32[]{:S(2)}, u32[]{:S(2)}) async-start(f32[128,16,2,64]{0,3,2,1:T(8,128)} %copy.61), calls=%async_computation.2 | async-start | bytes 2097152 | tf_op jit(solution)/shard_map/all_to_all | solution.py:207
  180.6 1.3 compare_select_fusion.1
  181.9 12.5 %all-to-all-done.2 = f32[128,16,2,64]{0,3,2,1:T(8,128)S(1)} async-done(((f32[128,16,2,64]{0,3,2,1:T(8,128)}), f32[128,16,2,64]{0,3,2,1:T(8,128)S(1)}, u32[]{:S(2)}, u32[]{:S(2)}) %all-to-all-start.2) | async-done | bytes 1048608 | tf_op jit(solution)/shard_map/all_to_all | solution.py:207
  194.4 0.6 copy.62
  195.0 3.7 %fusion.5 = f32[1024,128]{1,0:T(8,128)S(1)} fusion(bf16[1,2048,1024]{2,1,0:T(8,128)(2,1)} %all-gather.6.cloned.1.call-done, f32[16,8,16,128]{3,2,1,0:T(8,128)S(1)} %bitcast.168), kind=kOutput, calls=%fused_computation.8 | convolution fusion | flops 537919488 | bytes 5767168 | tf_op jit(solution)/shard_map/rf,rg->fg/dot_general | solution.py:93
  198.7 1.5 fusion.21
  200.4 0.4 all_to_all.59
  200.8 29.6 %all_to_all.69 = f32[16,1,8320]{2,1,0:T(1,128)S(1)} all-to-all(f32[16,1,8320]{2,1,0:T(1,128)S(1)} %all_to_all.59), channel_id=1, replica_groups=mesh['dp'=16,'seq'=16] {'dp'}, dimensions={0} | all-to-all | bytes 1064960 | tf_op jit(solution)/shard_map/all_to_all | solution.py:218
  230.4 0.3 reduce_sum.78
  230.9 9.1 %all_to_all.70 = f32[16,1,640]{2,1,0:T(1,128)S(1)} all-to-all(f32[16,1,640]{2,1,0:T(1,128)S(1)} %all_to_all.61), channel_id=1, replica_groups=mesh['dp'=16,'seq'=16] {'seq'}, dimensions={0} | all-to-all | bytes 81920 | tf_op jit(solution)/shard_map/all_to_all | solution.py:227
  240.0 0.6 fusion.64
  242.1 0.7 reshape.457
  (64 shorter events, 2.0 us)
Async XLA Ops:
  7.2 88.0 %copy-start = (bf16[1024,1024]{1,0:T(8,128)(2,1)S(1)}, bf16[1024,1024]{1,0:T(8,128)(2,1)}, u32[]{:S(2)}) copy-start(bf16[1024,1024]{1,0:T(8,128)(2,1)} %param.21) | copy-start | bytes 6291460
  7.2 23.4 %copy-start.6 = (bf16[1,128,1024]{2,1,0:T(8,128)(2,1)S(1)}, bf16[1,128,1024]{2,1,0:T(8,128)(2,1)}, u32[]{:S(2)}) copy-start(bf16[1,128,1024]{2,1,0:T(8,128)(2,1)} %param.14) | copy-start | bytes 786436
  7.2 23.4 %copy-start.7 = (bf16[1,128,1024]{2,1,0:T(8,128)(2,1)S(1)}, bf16[1,128,1024]{2,1,0:T(8,128)(2,1)}, u32[]{:S(2)}) copy-start(bf16[1,128,1024]{2,1,0:T(8,128)(2,1)} %param.15) | copy-start | bytes 786436
  7.2 23.6 %copy-start.10 = (f32[1024]{0:T(1024)S(1)}, f32[1024]{0:T(1024)}, u32[]{:S(2)}) copy-start(f32[1024]{0:T(1024)} %param.19) | copy-start | bytes 12292
  7.2 89.3 %all-gather.4.cloned.1.call-start = ((), (), s32[]{:S(2)}) async-start(), calls=%async_computation.5 | async-start | bytes 8912896 | tf_op jit(solution)/shard_map/all_gather | solution.py:118
  30.9 3.9 %copy-start.4 = (bf16[1,128,1024]{2,1,0:T(8,128)(2,1)}, bf16[1,128,1024]{2,1,0:T(8,128)(2,1)S(1)}, u32[]{:S(2)}) copy-start(bf16[1,128,1024]{2,1,0:T(8,128)(2,1)S(1)} %multiply_convert_fusion) | copy-start | bytes 786436
  36.1 8.2 %copy-start.9 = (s32[1,2048]{1,0:T(1,128)S(1)}, s32[1,2048]{1,0:T(1,128)}, u32[]{:S(2)}) copy-start(s32[1,2048]{1,0:T(1,128)} %param.17) | copy-start | bytes 24580
  38.2 15.1 %all-to-all-start = ((bf16[1,128,3,16,64]{1,4,2,0,3:T(8,128)(2,1)}), bf16[1,128,3,16,64]{1,4,2,0,3:T(8,128)(2,1)S(1)}, u32[]{:S(2)}, u32[]{:S(2)}) async-start(bf16[1,128,3,16,64]{1,4,2,0,3:T(8,128)(2,1)} %copy.55), calls=%async_computation | async-start | bytes 1572864 | tf_op jit(solution)/shard_map/all_to_all | solution.py:131
  42.9 152.2 %all-gather.6.cloned.1.call-start = ((), (), s32[]{:S(2)}) async-start(), calls=%async_computation.6 | async-start | bytes 4456448 | tf_op jit(solution)/shard_map/all_gather | solution.py:209
  80.7 11.0 %all-to-all-start.1 = ((bf16[16,2,4096]{2,1,0:T(2,128)(2,1)}), bf16[16,2,4096]{2,1,0:T(2,128)(2,1)S(1)}, u32[]{:S(2)}, u32[]{:S(2)}) async-start(bf16[16,2,4096]{2,1,0:T(2,128)(2,1)} %reshape.461), calls=%async_computation.1 | async-start | bytes 524288 | tf_op jit(solution)/shard_map/all_to_all | solution.py:133
  94.1 2.4 copy-start.5
  100.7 5.8 %collective-permute-start = (bf16[1,64,2048]{2,1,0:T(8,128)(2,1)S(1)}, bf16[1,64,2048]{2,1,0:T(8,128)(2,1)S(1)}, u32[]{:S(2)}, u32[]{:S(2)}) collective-permute-start(bf16[1,64,2048]{2,1,0:T(8,128)(2,1)S(1)} %get-tuple-element.34), channel_id=1, source_target_pairs={{0,1},{1,2},{2,3},{3,4},{4,5},{5,6},{6,7},{7,8},{8,9},{9,10},{10,1... | collective-permute-start | bytes 786440 | tf_op jit(solution)/shard_map/ppermute | solution.py:20
  102.9 8.7 %collective-permute-start.1 = (bf16[1,64,2048]{2,1,0:T(8,128)(2,1)S(1)}, bf16[1,64,2048]{2,1,0:T(8,128)(2,1)S(1)}, u32[]{:S(2)}, u32[]{:S(2)}) collective-permute-start(bf16[1,64,2048]{2,1,0:T(8,128)(2,1)S(1)} %get-tuple-element.35), channel_id=1, source_target_pairs={{1,0},{2,1},{3,2},{4,3},{5,4},{6,5},{7,6},{8,7},{9,8},{10,9},{11,1... | collective-permute-start | bytes 786440 | tf_op jit(solution)/shard_map/ppermute | solution.py:23
  114.3 2.2 copy-start.8
  128.4 1.3 copy-start.3
  130.0 3.0 %copy-start.11 = (f32[16,128,256]{2,1,0:T(8,128)S(1)}, f32[16,128,256]{2,1,0:T(8,128)}, u32[]{:S(2)}) copy-start(f32[16,128,256]{2,1,0:T(8,128)} %get-tuple-element.41) | copy-start | bytes 6291460
  134.9 20.3 %collective-permute-start.2 = (bf16[1,64,2048]{1,2,0:T(8,128)(2,1)S(1)}, bf16[1,64,2048]{1,2,0:T(8,128)(2,1)S(1)}, u32[]{:S(2)}, u32[]{:S(2)}) collective-permute-start(bf16[1,64,2048]{1,2,0:T(8,128)(2,1)S(1)} %get-tuple-element.31), channel_id=1, source_target_pairs={{0,1},{1,2},{2,3},{3,4},{4,5},{5,6},{6,7},{7,8},{8,9},{9,10},{10,1... | collective-permute-start | bytes 786440 | tf_op jit(solution)/shard_map/ppermute | solution.py:31
  137.2 27.0 %collective-permute-start.3 = (bf16[1,64,2048]{1,2,0:T(8,128)(2,1)}, bf16[1,64,2048]{1,2,0:T(8,128)(2,1)}, u32[]{:S(2)}, u32[]{:S(2)}) collective-permute-start(bf16[1,64,2048]{1,2,0:T(8,128)(2,1)} %get-tuple-element.30), channel_id=1, source_target_pairs={{1,0},{2,1},{3,2},{4,3},{5,4},{6,5},{7,6},{8,7},{9,8},{10,9},{11,1... | collective-permute-start | bytes 786440 | tf_op jit(solution)/shard_map/ppermute | solution.py:31
  172.7 21.7 %all-to-all-start.2 = ((f32[128,16,2,64]{0,3,2,1:T(8,128)}), f32[128,16,2,64]{0,3,2,1:T(8,128)S(1)}, u32[]{:S(2)}, u32[]{:S(2)}) async-start(f32[128,16,2,64]{0,3,2,1:T(8,128)} %copy.61), calls=%async_computation.2 | async-start | bytes 2097152 | tf_op jit(solution)/shard_map/all_to_all | solution.py:207
  195.0 3.7 %copy-start.2 = (bf16[1,2048,1024]{2,1,0:T(8,128)(2,1)S(1)}, bf16[1,2048,1024]{2,1,0:T(8,128)(2,1)}, u32[]{:S(2)}) copy-start(bf16[1,2048,1024]{2,1,0:T(8,128)(2,1)} %all-gather.6.cloned.1.call-done) | copy-start | bytes 12582916
  200.2 43.2 %copy-start.1 = (bf16[1024,1024]{1,0:T(8,128)(2,1)S(1)}, bf16[1024,1024]{1,0:T(8,128)(2,1)}, u32[]{:S(2)}) copy-start(bf16[1024,1024]{1,0:T(8,128)(2,1)} %param.21) | copy-start | bytes 6291460
Sparse Core Ops, SparseCore 0:
  30.0 62.3 all-gather.3
  94.8 60.3 all-gather.5

commit v4 on v3

--- a/solution.py
+++ b/solution.py
@@ -130,12 +130,15 @@
     teacher_proj = teacher_proj.reshape(dialogs, shard_rows, 3, HEADS, head_dim)
     by_heads = lax.all_to_all(teacher_proj, "seq", split_axis=3, concat_axis=1, tiled=True)
     head_out = jax.vmap(teacher_direct)(by_heads, key_bias)
-    by_frames = lax.all_to_all(head_out, "seq", split_axis=1, concat_axis=2, tiled=True)
-    teacher_vel = jnp.dot(
-        by_frames.reshape(dialogs * shard_rows, model_width),
-        teacher_out,
+    heads_here = head_out.shape[2]
+    head_out = head_out.reshape(dialogs, seq_count, shard_rows, heads_here, head_dim)
+    by_frames = lax.all_to_all(head_out, "seq", split_axis=1, concat_axis=1, tiled=True)
+    teacher_vel = jnp.einsum(
+        "bsfhd,shdn->bfn",
+        by_frames,
+        teacher_out.reshape(seq_count, heads_here, head_dim, model_width),
         preferred_element_type=jnp.float32,
-    )
+    ).reshape(dialogs * shard_rows, model_width)
     offset = seq_index * shard_rows
     queries = jnp.dot(flat_rows, w_inputs[0], preferred_element_type=jnp.float32).astype(
         jnp.bfloat16
@@ -201,8 +204,12 @@
         grad_both[:, HALO + shard_rows :].astype(jnp.bfloat16), "seq", 1
     ).astype(jnp.float32)
     owned_rows = grad_both[:, HALO : HALO + shard_rows]
-    owned_rows = owned_rows.at[:, :HALO].add(from_prev)
-    owned_rows = owned_rows.at[:, shard_rows - HALO :].add(from_next)
+    if shard_rows >= 2 * HALO:
+        middle = jnp.zeros((dialogs, shard_rows - 2 * HALO, 2 * model_width), jnp.float32)
+        owned_rows = owned_rows + jnp.concatenate((from_prev, middle, from_next), axis=1)
+    else:
+        owned_rows = owned_rows.at[:, :HALO].add(from_prev)
+        owned_rows = owned_rows.at[:, shard_rows - HALO :].add(from_next)
     by_head = owned_rows.reshape(shard_rows, 2, HEADS, head_dim).transpose(0, 2, 1, 3)
     head_grads = lax.all_to_all(by_head, "seq", split_axis=1, concat_axis=0, tiled=True)
     head_grads = head_grads.reshape(frames, 2 * head_dim)

time: 253 us -> 237 us (0.937)
  waiting for transfers between devices: 50.2 us -> 73.5 us
  local copies, waits for them, and re-layouts: 33.7 us -> 13.2 us
  other arithmetic: 23.2 us -> 8.19 us
    all_gather x1, waiting for transfers between devices: 0.01 us -> 15.2 us  [shards(): lax.all_gather(lax.all_gather(stacked, 'seq', axis=1, tiled=True), 'dp',...]
    scatter-add x2 -> x0, local copies, waits for them, and re-layouts: 13.7 us -> none  [the longest x1 7.62 us: shards(): owned_rows = owned_rows.at[:, :HALO].add(from_prev)]
    unnamed x1 -> x0, other arithmetic: 12.3 us -> none
    ppermute x2, waiting for transfers between devices: 16.4 us -> 22 us  [from_behind(): return lax.ppermute(block, axis, route)]
    unnamed x30 -> x25, local copies, waits for them, and re-layouts: 6.78 us -> 2.44 us
  transfers between devices with their start and end apart: 9 -> 9, of which waited for: 5 -> 8; matrix products, arithmetic and copies ran while one was open for 35% -> 22% of each run, Pallas kernels for 0% -> 0%
where the time goes in v4:
time: 237 us; the launch traced here: 236 us
  waiting for transfers between devices  73.5 us (31%)
  blocking collectives  56.8 us (24%)
  matrix products  42.4 us (18%)
  starting transfers between devices  23.3 us (10%)
  between operations  19 us (8%)
  local copies, waits for them, and re-layouts  13.2 us (6%)
  other arithmetic  8.19 us (3%)
    all_to_all x1, blocking collectives, shards(): lax.all_to_all(partial, 'dp', split_axis=0, concat_axis=0, tiled=True)  27.8 us
    ppermute x2, waiting for transfers between devices, from_behind(): return lax.ppermute(block, axis, route)  22 us
    all_gather x1, blocking collectives, shards(): lax.all_gather(stacked, 'seq', axis=1, tiled=True)  20 us
    all_gather x1, waiting for transfers between devices, shards(): lax.all_gather(lax.all_gather(stacked, 'seq', axis=1, tiled=True), 'dp',...  15.2 us
    all_to_all x1, waiting for transfers between devices, shards(): lax.all_to_all(by_head, 'seq', split_axis=1, concat_axis=0, tiled=True)  13.9 us
    all_to_all x1, blocking collectives, shards(): lax.all_to_all(partial, 'seq', split_axis=0, concat_axis=0, tiled=True)  9 us
    all_to_all x1, waiting for transfers between devices, shards(): lax.all_to_all(teacher_proj, 'seq', split_axis=3, concat_axis=1, tiled=True)  8.89 us
    all_to_all x1, waiting for transfers between devices, shards(): lax.all_to_all(head_out, 'seq', split_axis=1, concat_axis=1, tiled=True)  6.6 us
  transfers between devices with their start and end apart: 9, of which 8 were waited for; matrix products, arithmetic and copies ran while one was open for 22% of the time, Pallas kernels for 0%

profile of v4, /device:TPU:1, one launch (start us, length us, event | category | flops | bytes accessed | tf_op | source)
XLA Modules:
  0.0 236.4 jit_solution(15649149949863776320)
XLA Ops:
  7.3 0.9 copy.49
  8.2 0.7 copy.50
  8.9 20.0 %all_gather.10 = bf16[4,64,1024]{2,0,1:T(4,128)(2,1)S(1)} all-gather(bf16[4,4,1024]{2,0,1:T(4,128)(2,1)S(1)} %pad_maximum_fusion.4), channel_id=1, replica_groups=mesh['dp'=16,'seq'=16] {'seq'}, dimensions={1}, use_global_device_ids=true | all-gather | bytes 557056 | tf_op jit(solution)/shard_map/all_gather | solution.py:119
  28.9 1.0 copy.51
  30.5 0.2 multiply_reduce_fusion.2
  30.8 0.1 multiply_convert_fusion
  30.9 3.9 %convolution_convert_fusion = bf16[128,3072]{1,0:T(8,128)(2,1)S(1)} fusion(bf16[1024,3072]{1,0:T(8,128)(2,1)} %param.16, bf16[1,128,1024]{2,1,0:T(8,128)(2,1)S(1)} %multiply_convert_fusion), kind=kOutput, calls=%fused_computation.12 | convolution fusion | flops 805699584 | bytes 7340032 | tf_op jit(solution)/shard_map/dot_general | solution.py:127
  34.8 1.2 copy.55
  36.0 2.1 copy.56
  38.2 4.7 %all-to-all-start = ((bf16[1,128,3,16,64]{1,4,2,0,3:T(8,128)(2,1)}), bf16[1,128,3,16,64]{1,4,2,0,3:T(8,128)(2,1)S(1)}, u32[]{:S(2)}, u32[]{:S(2)}) async-start(bf16[1,128,3,16,64]{1,4,2,0,3:T(8,128)(2,1)} %copy.56), calls=%async_computation | async-start | bytes 1572864 | tf_op jit(solution)/shard_map/all_to_all | solution.py:131
  42.9 0.7 all-gather.6.cloned.1.call-update
  44.4 8.9 %all-to-all-done = bf16[1,128,3,16,64]{1,4,2,0,3:T(8,128)(2,1)S(1)} async-done(((bf16[1,128,3,16,64]{1,4,2,0,3:T(8,128)(2,1)}), bf16[1,128,3,16,64]{1,4,2,0,3:T(8,128)(2,1)S(1)}, u32[]{:S(2)}, u32[]{:S(2)}) %all-to-all-start) | async-done | bytes 786464 | tf_op jit(solution)/shard_map/all_to_all | solution.py:131
  53.3 0.1 copy_bitcast_fusion
  53.5 2.6 %fusion.2 = (f32[2048]{0:T(1024)S(1)}, f32[2048,2048]{0,1:T(8,128)S(1)}) fusion(f32[2048]{0:T(1024)S(1)} %fusion.57, bf16[1,2048,3,1,64]{1,4,2,3,0:T(8,128)(2,1)S(1)} %copy_bitcast_fusion), kind=kOutput, calls=%fused_computation.5 | convolution fusion | flops 549451776 | bytes 17317888 | tf_op jit(solution)/shard_map/vmap(vmap())/dot_general | solution.py:45
  56.1 4.6 %fusion.3 = f32[2048]{0:T(1024)S(1)} fusion(f32[2048,2048]{0,1:T(8,128)S(1)} %get-tuple-element.15, f32[2048]{0:T(1024)S(1)} %get-tuple-element.14, f32[2048]{0:T(1024)S(1)} %fusion.57), kind=kLoop, calls=%fused_computation.6 | loop fusion | flops 16775168 | bytes 16801792 | tf_op jit(solution)/shard_map/vmap(vmap())/reduce_sum | solution.py:51
  60.7 4.1 %fusion.29 = bf16[8,8,16,128]{3,1,2,0:T(8,128)(2,1)S(1)} fusion(f32[2048,2048]{0,1:T(8,128)S(1)} %get-tuple-element.15, f32[2048]{0:T(1024)S(1)} %fusion.3, f32[2048]{0:T(1024)S(1)} %get-tuple-element.14, f32[2048]{0:T(1024)S(1)} %fusion.57, bf16[1,2048,3,1,64]{1,4,2,3,0:T(8,128)(2,1)S(1)} %copy_bitcast_fusion), kind=kOutput, calls=%fused_computation.44 | convolution fusion | flops 557973504 | bytes 17326080 | tf_op jit(solution)/shard_map/vmap(vmap())/dot_general | solution.py:52
  64.8 0.8 copy.58
  65.6 3.7 %all-to-all-start.1 = ((bf16[1,16,128,1,64]{2,4,3,0,1:T(8,128)(2,1)}), bf16[1,16,128,1,64]{2,4,3,0,1:T(8,128)(2,1)S(1)}, u32[]{:S(2)}, u32[]{:S(2)}) async-start(bf16[1,16,128,1,64]{2,4,3,0,1:T(8,128)(2,1)} %copy.58), calls=%async_computation.1 | async-start | bytes 524288 | tf_op jit(solution)/shard_map/all_to_all | solution.py:135
  69.3 0.6 convert_reduce_fusion
  69.9 0.1 or_and_fusion
  70.0 6.6 %all-to-all-done.1 = bf16[1,16,128,1,64]{2,4,3,0,1:T(8,128)(2,1)S(1)} async-done(((bf16[1,16,128,1,64]{2,4,3,0,1:T(8,128)(2,1)}), bf16[1,16,128,1,64]{2,4,3,0,1:T(8,128)(2,1)S(1)}, u32[]{:S(2)}, u32[]{:S(2)}) %all-to-all-start.1) | async-done | bytes 262176 | tf_op jit(solution)/shard_map/all_to_all | solution.py:135
  76.6 0.5 convolution_bitcast_fusion
  77.1 15.2 %all-gather.4.cloned.1.call-done = bf16[4,1024,1024]{2,1,0:T(8,128)(2,1)} async-done(((bf16[4,64,1024]{2,1,0:T(8,128)(2,1)}), bf16[4,1024,1024]{2,1,0:T(8,128)(2,1)}) %all-gather.4.cloned.1.call-update) | async-done | bytes 8388624 | tf_op jit(solution)/shard_map/all_gather | solution.py:118
  92.3 2.0 fusion.27
  94.3 2.0 fusion.28
  96.5 3.1 %collective-permute-start = (bf16[1,64,2048]{2,1,0:T(8,128)(2,1)S(1)}, bf16[1,64,2048]{2,1,0:T(8,128)(2,1)S(1)}, u32[]{:S(2)}, u32[]{:S(2)}) collective-permute-start(bf16[1,64,2048]{2,1,0:T(8,128)(2,1)S(1)} %get-tuple-element.10), channel_id=1, source_target_pairs={{0,1},{1,2},{2,3},{3,4},{4,5},{5,6},{6,7},{7,8},{8,9},{9,10},{10,1... | collective-permute-start | bytes 786440 | tf_op jit(solution)/shard_map/ppermute | solution.py:20
  99.6 1.3 collective-permute-start.1
  100.9 2.0 fusion.26
  102.9 0.2 copy.52
  103.1 1.8 collective-permute-done
  104.9 4.3 %collective-permute-done.1 = bf16[1,64,2048]{2,1,0:T(8,128)(2,1)S(1)} collective-permute-done((bf16[1,64,2048]{2,1,0:T(8,128)(2,1)S(1)}, bf16[1,64,2048]{2,1,0:T(8,128)(2,1)S(1)}, u32[]{:S(2)}, u32[]{:S(2)}) %collective-permute-start.1) | collective-permute-done | bytes 262176 | tf_op jit(solution)/shard_map/ppermute | solution.py:23
  109.4 0.2 copy.53
  109.6 0.2 copy.54
  109.9 2.1 fusion.65
  111.9 2.2 convolution_convert_fusion.1
  114.1 2.8 %multiply_reduce_fusion.1 = (f32[]{:T(128)}, bf16[128,1024]{1,0:T(8,128)(2,1)S(1)}) fusion(f32[128,1024]{1,0:T(8,128)S(1)} %convolution_bitcast_fusion, bf16[128,1024]{0,1:T(8,128)(2,1)S(1)} %bitcast.182, bf16[4,1024,1024]{2,1,0:T(8,128)(2,1)} %all-gather.4.cloned.1.call-done, pred[128]{0:T(512)(128)(4,1)S(1)} %get-tuple-element.3), kind=kOutput, calls=%fused_computation.61 | convolution fusion | flops 269090816 | bytes 3145860 | tf_op jit(solution)/shard_map/dot_general | solution.py:176
  116.9 2.4 %fusion.25 = bf16[128,1024]{1,0:T(8,128)(2,1)S(1)} fusion(bf16[4,1024,1024]{2,1,0:T(8,128)(2,1)} %all-gather.4.cloned.1.call-done, bf16[128,1024]{1,0:T(8,128)(2,1)S(1)} %get-tuple-element.19), kind=kOutput, calls=%fused_computation.39 | convolution fusion | flops 268566528 | bytes 2621440 | tf_op jit(solution)/shard_map/dot_general | solution.py:182
  119.3 0.2 copy.59
  119.5 6.5 %multiply_bitcast_fusion = f32[1,16,128,256]{3,2,1,0:T(8,128)S(1)} fusion(bf16[128,16,64]{0,2,1:T(8,128)(2,1)S(1)} %bitcast.175, bf16[256,16,64]{0,2,1:T(8,128)(2,1)S(1)} %bitcast.173, f32[16,128,256]{2,1,0:T(8,128)} %get-tuple-element.17, f32[16,128]{1,0:T(8,128)S(1)} %get-tuple-element.16), kind=kOutput, calls=%fused_computation.26 | convolution fusion | flops 137365760 | bytes 4988928 | tf_op jit(solution)/shard_map/sub | solution.py:189
  126.0 1.4 copy-done.3
  127.3 0.3 fusion.35
  127.6 3.1 %convolution_add_fusion = f32[16,64,256]{2,1,0:T(8,128)S(1)} fusion(f32[16,64,256]{2,1,0:T(8,128)S(1)} %fusion.35, bf16[128,16,64]{0,2,1:T(8,128)(2,1)S(1)} %bitcast.170, f32[1,16,128,256]{3,2,1,0:T(8,128)} %copy-done.3), kind=kOutput, calls=%fused_computation.34 | convolution fusion | flops 69468160 | bytes 4456448 | tf_op jit(solution)/shard_map/bhrw,brhd->bwhd/dot_general | solution.py:90
  130.8 0.8 fusion.43
  131.6 0.1 fusion.10
  131.7 0.2 fusion.61
  132.0 3.1 %collective-permute-start.2 = (bf16[1,64,2048]{1,2,0:T(8,128)(2,1)S(1)}, bf16[1,64,2048]{1,2,0:T(8,128)(2,1)S(1)}, u32[]{:S(2)}, u32[]{:S(2)}) collective-permute-start(bf16[1,64,2048]{1,2,0:T(8,128)(2,1)S(1)} %get-tuple-element.6), channel_id=1, source_target_pairs={{0,1},{1,2},{2,3},{3,4},{4,5},{5,6},{6,7},{7,8},{8,9},{9,10},{10,1... | collective-permute-start | bytes 786440 | tf_op jit(solution)/shard_map/ppermute | solution.py:31
  135.0 1.3 collective-permute-start.3
  136.3 19.8 %collective-permute-done.2 = bf16[1,64,2048]{1,2,0:T(8,128)(2,1)S(1)} collective-permute-done((bf16[1,64,2048]{1,2,0:T(8,128)(2,1)S(1)}, bf16[1,64,2048]{1,2,0:T(8,128)(2,1)S(1)}, u32[]{:S(2)}, u32[]{:S(2)}) %collective-permute-start.2) | collective-permute-done | bytes 262176 | tf_op jit(solution)/shard_map/ppermute | solution.py:31
  156.2 2.2 collective-permute-done.3
  158.4 0.5 fusion.33
  158.9 1.0 copy.60
  159.9 6.1 %all-to-all-start.2 = ((f32[128,16,2,64]{0,3,2,1:T(8,128)}), f32[128,16,2,64]{0,3,2,1:T(8,128)S(1)}, u32[]{:S(2)}, u32[]{:S(2)}) async-start(f32[128,16,2,64]{0,3,2,1:T(8,128)} %copy.60), calls=%async_computation.2 | async-start | bytes 2097152 | tf_op jit(solution)/shard_map/all_to_all | solution.py:214
  166.0 1.3 compare_select_fusion.1
  167.3 13.9 %all-to-all-done.2 = f32[128,16,2,64]{0,3,2,1:T(8,128)S(1)} async-done(((f32[128,16,2,64]{0,3,2,1:T(8,128)}), f32[128,16,2,64]{0,3,2,1:T(8,128)S(1)}, u32[]{:S(2)}, u32[]{:S(2)}) %all-to-all-start.2) | async-done | bytes 1048608 | tf_op jit(solution)/shard_map/all_to_all | solution.py:214
  181.3 0.6 copy.61
  181.9 3.7 %fusion.5 = f32[1024,128]{1,0:T(8,128)S(1)} fusion(bf16[1,2048,1024]{2,1,0:T(8,128)(2,1)} %all-gather.6.cloned.1.call-done, f32[16,8,16,128]{3,2,1,0:T(8,128)S(1)} %bitcast.161), kind=kOutput, calls=%fused_computation.8 | convolution fusion | flops 537919488 | bytes 5767168 | tf_op jit(solution)/shard_map/rf,rg->fg/dot_general | solution.py:93
  185.6 1.5 fusion.20
  187.3 0.4 all_to_all.49
  187.7 27.8 %all_to_all.59 = f32[16,1,8320]{2,1,0:T(1,128)S(1)} all-to-all(f32[16,1,8320]{2,1,0:T(1,128)S(1)} %all_to_all.49), channel_id=1, replica_groups=mesh['dp'=16,'seq'=16] {'dp'}, dimensions={0} | all-to-all | bytes 1064960 | tf_op jit(solution)/shard_map/all_to_all | solution.py:225
  215.5 0.3 reduce_sum.78
  215.9 9.0 %all_to_all.60 = f32[16,1,640]{2,1,0:T(1,128)S(1)} all-to-all(f32[16,1,640]{2,1,0:T(1,128)S(1)} %all_to_all.51), channel_id=1, replica_groups=mesh['dp'=16,'seq'=16] {'seq'}, dimensions={0} | all-to-all | bytes 81920 | tf_op jit(solution)/shard_map/all_to_all | solution.py:234
  225.0 0.6 fusion.64
  226.9 0.1 reshape.404
  227.0 0.7 reshape.405
  (52 shorter events, 1.0 us)
Async XLA Ops:
  7.2 69.5 %copy-start = (bf16[1024,1024]{1,0:T(8,128)(2,1)S(1)}, bf16[1024,1024]{1,0:T(8,128)(2,1)}, u32[]{:S(2)}) copy-start(bf16[1024,1024]{1,0:T(8,128)(2,1)} %param.17) | copy-start | bytes 6291460
  7.2 23.3 %copy-start.6 = (bf16[1,128,1024]{2,1,0:T(8,128)(2,1)S(1)}, bf16[1,128,1024]{2,1,0:T(8,128)(2,1)}, u32[]{:S(2)}) copy-start(bf16[1,128,1024]{2,1,0:T(8,128)(2,1)} %param.10) | copy-start | bytes 786436
  7.2 23.3 %copy-start.7 = (bf16[1,128,1024]{2,1,0:T(8,128)(2,1)S(1)}, bf16[1,128,1024]{2,1,0:T(8,128)(2,1)}, u32[]{:S(2)}) copy-start(bf16[1,128,1024]{2,1,0:T(8,128)(2,1)} %param.11) | copy-start | bytes 786436
  7.2 23.6 %copy-start.9 = (f32[1024]{0:T(1024)S(1)}, f32[1024]{0:T(1024)}, u32[]{:S(2)}) copy-start(f32[1024]{0:T(1024)} %param.15) | copy-start | bytes 12292
  7.2 85.1 %all-gather.4.cloned.1.call-start = ((), (), s32[]{:S(2)}) async-start(), calls=%async_computation.5 | async-start | bytes 8912896 | tf_op jit(solution)/shard_map/all_gather | solution.py:118
  30.9 3.9 %copy-start.4 = (bf16[1,128,1024]{2,1,0:T(8,128)(2,1)}, bf16[1,128,1024]{2,1,0:T(8,128)(2,1)S(1)}, u32[]{:S(2)}) copy-start(bf16[1,128,1024]{2,1,0:T(8,128)(2,1)S(1)} %multiply_convert_fusion) | copy-start | bytes 786436
  36.0 8.3 %copy-start.8 = (s32[1,2048]{1,0:T(1,128)S(1)}, s32[1,2048]{1,0:T(1,128)}, u32[]{:S(2)}) copy-start(s32[1,2048]{1,0:T(1,128)} %param.13) | copy-start | bytes 24580
  38.2 15.1 %all-to-all-start = ((bf16[1,128,3,16,64]{1,4,2,0,3:T(8,128)(2,1)}), bf16[1,128,3,16,64]{1,4,2,0,3:T(8,128)(2,1)S(1)}, u32[]{:S(2)}, u32[]{:S(2)}) async-start(bf16[1,128,3,16,64]{1,4,2,0,3:T(8,128)(2,1)} %copy.56), calls=%async_computation | async-start | bytes 1572864 | tf_op jit(solution)/shard_map/all_to_all | solution.py:131
  42.9 139.0 %all-gather.6.cloned.1.call-start = ((), (), s32[]{:S(2)}) async-start(), calls=%async_computation.6 | async-start | bytes 4456448 | tf_op jit(solution)/shard_map/all_gather | solution.py:216
  64.8 27.5 %copy-start.5 = (bf16[1,128,1024]{2,1,0:T(8,128)(2,1)S(1)}, bf16[1,128,1024]{2,1,0:T(8,128)(2,1)}, u32[]{:S(2)}) copy-start(bf16[1,128,1024]{2,1,0:T(8,128)(2,1)} %copy-done.4) | copy-start | bytes 786436
  65.6 11.0 %all-to-all-start.1 = ((bf16[1,16,128,1,64]{2,4,3,0,1:T(8,128)(2,1)}), bf16[1,16,128,1,64]{2,4,3,0,1:T(8,128)(2,1)S(1)}, u32[]{:S(2)}, u32[]{:S(2)}) async-start(bf16[1,16,128,1,64]{2,4,3,0,1:T(8,128)(2,1)} %copy.58), calls=%async_computation.1 | async-start | bytes 524288 | tf_op jit(solution)/shard_map/all_to_all | solution.py:135
  96.5 8.5 %collective-permute-start = (bf16[1,64,2048]{2,1,0:T(8,128)(2,1)S(1)}, bf16[1,64,2048]{2,1,0:T(8,128)(2,1)S(1)}, u32[]{:S(2)}, u32[]{:S(2)}) collective-permute-start(bf16[1,64,2048]{2,1,0:T(8,128)(2,1)S(1)} %get-tuple-element.10), channel_id=1, source_target_pairs={{0,1},{1,2},{2,3},{3,4},{4,5},{5,6},{6,7},{7,8},{8,9},{9,10},{10,1... | collective-permute-start | bytes 786440 | tf_op jit(solution)/shard_map/ppermute | solution.py:20
  99.6 9.7 %collective-permute-start.1 = (bf16[1,64,2048]{2,1,0:T(8,128)(2,1)S(1)}, bf16[1,64,2048]{2,1,0:T(8,128)(2,1)S(1)}, u32[]{:S(2)}, u32[]{:S(2)}) collective-permute-start(bf16[1,64,2048]{2,1,0:T(8,128)(2,1)S(1)} %get-tuple-element.11), channel_id=1, source_target_pairs={{1,0},{2,1},{3,2},{4,3},{5,4},{6,5},{7,6},{8,7},{9,8},{10,9},{11,1... | collective-permute-start | bytes 786440 | tf_op jit(solution)/shard_map/ppermute | solution.py:23
  126.0 1.4 copy-start.3
  127.6 3.2 %copy-start.10 = (f32[16,128,256]{2,1,0:T(8,128)S(1)}, f32[16,128,256]{2,1,0:T(8,128)}, u32[]{:S(2)}) copy-start(f32[16,128,256]{2,1,0:T(8,128)} %get-tuple-element.17) | copy-start | bytes 6291460
  132.0 24.2 %collective-permute-start.2 = (bf16[1,64,2048]{1,2,0:T(8,128)(2,1)S(1)}, bf16[1,64,2048]{1,2,0:T(8,128)(2,1)S(1)}, u32[]{:S(2)}, u32[]{:S(2)}) collective-permute-start(bf16[1,64,2048]{1,2,0:T(8,128)(2,1)S(1)} %get-tuple-element.6), channel_id=1, source_target_pairs={{0,1},{1,2},{2,3},{3,4},{4,5},{5,6},{6,7},{7,8},{8,9},{9,10},{10,1... | collective-permute-start | bytes 786440 | tf_op jit(solution)/shard_map/ppermute | solution.py:31
  135.0 23.3 %collective-permute-start.3 = (bf16[1,64,2048]{1,2,0:T(8,128)(2,1)S(1)}, bf16[1,64,2048]{1,2,0:T(8,128)(2,1)S(1)}, u32[]{:S(2)}, u32[]{:S(2)}) collective-permute-start(bf16[1,64,2048]{1,2,0:T(8,128)(2,1)S(1)} %get-tuple-element.7), channel_id=1, source_target_pairs={{1,0},{2,1},{3,2},{4,3},{5,4},{6,5},{7,6},{8,7},{9,8},{10,9},{11,1... | collective-permute-start | bytes 786440 | tf_op jit(solution)/shard_map/ppermute | solution.py:31
  159.9 21.3 %all-to-all-start.2 = ((f32[128,16,2,64]{0,3,2,1:T(8,128)}), f32[128,16,2,64]{0,3,2,1:T(8,128)S(1)}, u32[]{:S(2)}, u32[]{:S(2)}) async-start(f32[128,16,2,64]{0,3,2,1:T(8,128)} %copy.60), calls=%async_computation.2 | async-start | bytes 2097152 | tf_op jit(solution)/shard_map/all_to_all | solution.py:214
  181.9 3.7 %copy-start.2 = (bf16[1,2048,1024]{2,1,0:T(8,128)(2,1)S(1)}, bf16[1,2048,1024]{2,1,0:T(8,128)(2,1)}, u32[]{:S(2)}) copy-start(bf16[1,2048,1024]{2,1,0:T(8,128)(2,1)} %all-gather.6.cloned.1.call-done) | copy-start | bytes 12582916
  187.1 41.3 %copy-start.1 = (bf16[1024,1024]{1,0:T(8,128)(2,1)S(1)}, bf16[1024,1024]{1,0:T(8,128)(2,1)}, u32[]{:S(2)}) copy-start(bf16[1024,1024]{1,0:T(8,128)(2,1)} %param.17) | copy-start | bytes 6291460
Sparse Core Ops, SparseCore 0:
  30.0 62.2 all-gather.3
  94.7 61.6 all-gather.5

commit v5 on v4

--- a/solution.py
+++ b/solution.py
@@ -115,13 +115,21 @@
     window = shard_rows + 2 * HALO
     rows_each = student_out.shape[0]
     stacked = jnp.concatenate((student_in, student_out[None]), axis=0)
-    gathered = lax.all_gather(
-        lax.all_gather(stacked, "seq", axis=1, tiled=True), "dp", axis=1, tiled=True
-    )
+    seq_count = lax.axis_size("seq")
+    spread = jnp.broadcast_to(stacked[None], (seq_count,) + stacked.shape)
+    spread = lax.all_to_all(spread, "seq", split_axis=0, concat_axis=2, tiled=True)
+    gathered = lax.all_gather(spread.reshape(stacked.shape[0], -1, model_width), "dp", axis=1, tiled=True)
     w_inputs = gathered[:3]
     w_output = gathered[3]
     normed = normalize(clean_frames, noise_frames, time_index, modulation)
     flat_rows = normed.reshape(dialogs * shard_rows, model_width)
+    normed_all = lax.all_to_all(
+        jnp.broadcast_to(flat_rows[None], (seq_count,) + flat_rows.shape),
+        "seq",
+        split_axis=0,
+        concat_axis=0,
+        tiled=True,
+    ).reshape(-1, model_width)
     frame_pos = jnp.arange(frames, dtype=jnp.int32)
     key_bias = jnp.where(frame_pos[None, :] < lengths[:, None], 0.0, NEGATIVE).astype(jnp.float32)
     teacher_proj = jnp.dot(flat_rows, teacher_qkv, preferred_element_type=jnp.float32).astype(
@@ -213,29 +221,21 @@
     by_head = owned_rows.reshape(shard_rows, 2, HEADS, head_dim).transpose(0, 2, 1, 3)
     head_grads = lax.all_to_all(by_head, "seq", split_axis=1, concat_axis=0, tiled=True)
     head_grads = head_grads.reshape(frames, 2 * head_dim)
-    normed_all = lax.all_gather(flat_rows, "seq", axis=0, tiled=True)
     partial = split_product("rf,rg->fg", head_grads, normed_all, False)
     dp_count = lax.axis_size("dp")
-    partial = partial.reshape(dp_count, -1)
+    block = rows_each * 2 * head_dim
+    partial = partial.reshape(dp_count * seq_count, block)
     lane = jnp.arange(2 * head_dim)
     scalars = jnp.where(lane == 0, square_local, jnp.where(lane == 1, count_local, 0.0))
     partial = jnp.concatenate(
-        (partial, jnp.broadcast_to(scalars, (dp_count, 2 * head_dim))), axis=1
-    )
-    partial = lax.all_to_all(partial, "dp", split_axis=0, concat_axis=0, tiled=True).sum(0)
-    block = rows_each * 2 * head_dim
-    partial = jnp.concatenate(
-        (
-            partial[: seq_count * block].reshape(seq_count, block),
-            jnp.broadcast_to(partial[seq_count * block :], (seq_count, 2 * head_dim)),
-        ),
-        axis=1,
-    )
-    mine = lax.all_to_all(partial, "seq", split_axis=0, concat_axis=0, tiled=True)
-    totals = mine[:, block:].sum(0)
+        (partial, jnp.broadcast_to(scalars, (dp_count * seq_count, 2 * head_dim))), axis=1
+    )
+    mine = lax.all_to_all(partial, ("dp", "seq"), split_axis=0, concat_axis=0, tiled=True)
+    mine = mine.reshape(dp_count, seq_count, block + 2 * head_dim)
+    totals = mine[:, :, block:].sum((0, 1))
     square_sum, frame_count = totals[0], totals[1]
     mean_error = square_sum / (frame_count * model_width)
-    mine = mine[:, :block] * lax.rsqrt(frame_count)
+    mine = mine[:, :, :block].sum(0) * lax.rsqrt(frame_count)
     mine = mine.reshape(HEADS, rows_each, 2, head_dim).transpose(2, 1, 0, 3)
     grad_inputs = mine.reshape(2, rows_each, model_width)
     return (grad_inputs, mean_error)

time: 237 us -> 306 us (1.29)
  local copies, waits for them, and re-layouts: 13.2 us -> 39.8 us
  waiting for transfers between devices: 73.5 us -> 99.1 us
  blocking collectives: 56.8 us -> 76.4 us
    all_to_all x2 -> x3, blocking collectives: 36.8 us -> 76.4 us  [the longest x1 34.3 us: shards(): lax.all_to_all(partial, ('dp', 'seq'), split_axis=0, concat_axis=0, tiled...]
    all_to_all x1, waiting for transfers between devices: 13.9 us -> 53.5 us  [shards(): lax.all_to_all(jnp.broadcast_to(flat_rows[None], (seq_count,) + flat_rows...]
    slice x2 -> x1, local copies, waits for them, and re-layouts: 0.01 us -> 25.6 us  [shards(): w_inputs[1]]
    all_gather x1 -> x0, blocking collectives: 20 us -> none  [shards(): lax.all_gather(stacked, 'seq', axis=1, tiled=True)]
    ppermute x2, waiting for transfers between devices: 22 us -> 12.2 us  [from_behind(): return lax.ppermute(block, axis, route)]
    all_gather x2 -> x1, waiting for transfers between devices: 15.2 us -> 8.76 us  [shards(): lax.all_gather(spread.reshape(stacked.shape[0], -1, model_width), 'dp', a...]
  transfers between devices with their start and end apart: 9 -> 8, of which waited for: 8 -> 8; matrix products, arithmetic and copies ran while one was open for 22% -> 8% of each run, Pallas kernels for 0% -> 0%
where the time goes in v5:
time: 306 us; the launch traced here: 305 us
  waiting for transfers between devices  99.1 us (32%)
  blocking collectives  76.4 us (25%)
  matrix products  40 us (13%)
  local copies, waits for them, and re-layouts  39.8 us (13%)
  starting transfers between devices  21 us (7%)
  between operations  19 us (6%)
  other arithmetic  10.1 us (3%)
    all_to_all x1, waiting for transfers between devices, shards(): lax.all_to_all(jnp.broadcast_to(flat_rows[None], (seq_count,) + flat_rows...  53.5 us
    all_to_all x1, blocking collectives, shards(): lax.all_to_all(partial, ('dp', 'seq'), split_axis=0, concat_axis=0, tiled...  34.3 us
    slice x1, local copies, waits for them, and re-layouts, shards(): w_inputs[1]  25.6 us
    all_to_all x1, blocking collectives, shards(): lax.all_to_all(by_head, 'seq', split_axis=1, concat_axis=0, tiled=True)  24.2 us
    all_to_all x1, blocking collectives, shards(): lax.all_to_all(spread, 'seq', split_axis=0, concat_axis=2, tiled=True)  17.9 us
    ppermute x2, waiting for transfers between devices, from_behind(): return lax.ppermute(block, axis, route)  12.2 us
    all_to_all x1, waiting for transfers between devices, shards(): lax.all_to_all(teacher_proj, 'seq', split_axis=3, concat_axis=1, tiled=True)  11.6 us
    all_gather x1, waiting for transfers between devices, shards(): lax.all_gather(spread.reshape(stacked.shape[0], -1, model_width), 'dp', a...  8.76 us
  transfers between devices with their start and end apart: 8, of which 8 were waited for; matrix products, arithmetic and copies ran while one was open for 8% of the time, Pallas kernels for 0%

profile of v5, /device:TPU:1, one launch (start us, length us, event | category | flops | bytes accessed | tf_op | source)
XLA Modules:
  0.0 305.2 jit_solution(2860278963798234609)
XLA Ops:
  7.3 0.9 pad_maximum_fusion.3
  8.2 0.2 broadcast_in_dim.54
  8.4 17.9 %all_to_all.67 = bf16[16,4,4,1024]{3,1,2,0:T(4,128)(2,1)} all-to-all(bf16[16,4,4,1024]{3,1,2,0:T(4,128)(2,1)S(1)} %broadcast_in_dim.54), channel_id=1, replica_groups=mesh['dp'=16,'seq'=16] {'seq'}, dimensions={0} | all-to-all | bytes 1048576 | tf_op jit(solution)/shard_map/all_to_all | solution.py:120
  27.0 0.2 multiply_reduce_fusion.2
  27.2 0.1 fusion.41
  27.4 3.8 %convolution_convert_fusion = bf16[128,3072]{1,0:T(8,128)(2,1)S(1)} fusion(bf16[128,1024]{1,0:T(8,128)(2,1)S(1)} %fusion.41, bf16[1024,3072]{1,0:T(8,128)(2,1)} %param.16), kind=kOutput, calls=%fused_computation.8 | convolution fusion | flops 805699584 | bytes 7340032 | tf_op jit(solution)/shard_map/dot_general | solution.py:135
  31.2 1.2 copy.48
  32.4 2.1 copy.49
  34.5 3.6 %all-to-all-start.2 = ((bf16[1,128,3,16,64]{1,4,2,0,3:T(8,128)(2,1)}), bf16[1,128,3,16,64]{1,4,2,0,3:T(8,128)(2,1)S(1)}, u32[]{:S(2)}, u32[]{:S(2)}) async-start(bf16[1,128,3,16,64]{1,4,2,0,3:T(8,128)(2,1)} %copy.49), calls=%async_computation.2 | async-start | bytes 1572864 | tf_op jit(solution)/shard_map/all_to_all | solution.py:139
  38.9 11.6 %all-to-all-done.2 = bf16[1,128,3,16,64]{1,4,2,0,3:T(8,128)(2,1)S(1)} async-done(((bf16[1,128,3,16,64]{1,4,2,0,3:T(8,128)(2,1)}), bf16[1,128,3,16,64]{1,4,2,0,3:T(8,128)(2,1)S(1)}, u32[]{:S(2)}, u32[]{:S(2)}) %all-to-all-start.2) | async-done | bytes 786464 | tf_op jit(solution)/shard_map/all_to_all | solution.py:139
  50.6 2.6 fusion.2
  53.2 4.6 %fusion.3 = f32[2048]{0:T(1024)S(1)} fusion(f32[2048,2048]{0,1:T(8,128)S(1)} %get-tuple-element.21, f32[2048]{0:T(1024)S(1)} %get-tuple-element.20, f32[2048]{0:T(1024)S(1)} %fusion.47), kind=kLoop, calls=%fused_computation.6 | loop fusion | flops 16775168 | bytes 16801792 | tf_op jit(solution)/shard_map/vmap(vmap())/reduce_sum | solution.py:51
  57.8 4.1 %fusion.18 = bf16[8,8,16,128]{3,1,2,0:T(8,128)(2,1)S(1)} fusion(f32[2048,2048]{0,1:T(8,128)S(1)} %get-tuple-element.21, f32[2048]{0:T(1024)S(1)} %fusion.3, f32[2048]{0:T(1024)S(1)} %get-tuple-element.20, f32[2048]{0:T(1024)S(1)} %fusion.47, bf16[1,2048,3,1,64]{1,4,2,3,0:T(8,128)(2,1)S(1)} %copy_bitcast_fusion.15), kind=kOutput, calls=%fused_computation.38 | convolution fusion | flops 557973504 | bytes 17326080 | tf_op jit(solution)/shard_map/vmap(vmap())/dot_general | solution.py:52
  61.9 0.8 copy.51
  62.7 3.7 %all-to-all-start.3 = ((bf16[1,16,128,1,64]{2,4,3,0,1:T(8,128)(2,1)}), bf16[1,16,128,1,64]{2,4,3,0,1:T(8,128)(2,1)S(1)}, u32[]{:S(2)}, u32[]{:S(2)}) async-start(bf16[1,16,128,1,64]{2,4,3,0,1:T(8,128)(2,1)} %copy.51), calls=%async_computation.3 | async-start | bytes 524288 | tf_op jit(solution)/shard_map/all_to_all | solution.py:143
  66.5 0.6 convert_reduce_fusion
  67.2 6.8 %all-to-all-done.3 = bf16[1,16,128,1,64]{2,4,3,0,1:T(8,128)(2,1)S(1)} async-done(((bf16[1,16,128,1,64]{2,4,3,0,1:T(8,128)(2,1)}), bf16[1,16,128,1,64]{2,4,3,0,1:T(8,128)(2,1)S(1)}, u32[]{:S(2)}, u32[]{:S(2)}) %all-to-all-start.3) | async-done | bytes 262176 | tf_op jit(solution)/shard_map/all_to_all | solution.py:143
  74.0 0.5 convolution_bitcast_fusion
  74.5 8.8 %all-gather.2.cloned.1.call-done = bf16[4,1024,1024]{2,0,1:T(4,128)(2,1)} async-done(((bf16[4,64,1024]{2,0,1:T(4,128)(2,1)}), bf16[4,1024,1024]{2,0,1:T(4,128)(2,1)}) %all-gather.2.cloned.1.call-update) | async-done | bytes 8388624 | tf_op jit(solution)/shard_map/all_gather | solution.py:121
  83.2 25.6 %fusion.51 = (bf16[1,1024,1024]{2,0,1:T(2,128)(2,1)S(1)}, bf16[1,1024,1024]{2,0,1:T(2,128)(2,1)S(1)}, bf16[1,1024,1024]{2,0,1:T(2,128)(2,1)S(1)}, bf16[1,1024,1024]{2,0,1:T(2,128)(2,1)}) fusion(bf16[4,1024,1024]{2,0,1:T(4,128)(2,1)} %all-gather.2.cloned.1.call-done), kind=kLoop, calls=%fused_computation.100 | loop fusion | bytes 16777216 | tf_op jit(solution)/shard_map/slice | solution.py:155
  108.8 0.8 fusion.16
  109.6 0.8 fusion.17
  110.5 3.1 %collective-permute-start = (bf16[1,64,2048]{2,1,0:T(8,128)(2,1)S(1)}, bf16[1,64,2048]{2,1,0:T(8,128)(2,1)S(1)}, u32[]{:S(2)}, u32[]{:S(2)}) collective-permute-start(bf16[1,64,2048]{2,1,0:T(8,128)(2,1)S(1)} %get-tuple-element.16), channel_id=1, source_target_pairs={{0,1},{1,2},{2,3},{3,4},{4,5},{5,6},{6,7},{7,8},{8,9},{9,10},{10,1... | collective-permute-start | bytes 786440 | tf_op jit(solution)/shard_map/ppermute | solution.py:20
  113.6 1.3 collective-permute-start.1
  114.9 0.8 fusion.15
  115.7 0.2 copy.42
  115.9 3.1 %collective-permute-done = bf16[1,64,2048]{2,1,0:T(8,128)(2,1)S(1)} collective-permute-done((bf16[1,64,2048]{2,1,0:T(8,128)(2,1)S(1)}, bf16[1,64,2048]{2,1,0:T(8,128)(2,1)S(1)}, u32[]{:S(2)}, u32[]{:S(2)}) %collective-permute-start) | collective-permute-done | bytes 262176 | tf_op jit(solution)/shard_map/ppermute | solution.py:20
  119.0 0.7 copy-done.10
  119.7 3.3 %collective-permute-done.1 = bf16[1,64,2048]{2,1,0:T(8,128)(2,1)} collective-permute-done((bf16[1,64,2048]{2,1,0:T(8,128)(2,1)S(1)}, bf16[1,64,2048]{2,1,0:T(8,128)(2,1)}, u32[]{:S(2)}, u32[]{:S(2)}) %collective-permute-start.1) | collective-permute-done | bytes 262176 | tf_op jit(solution)/shard_map/ppermute | solution.py:23
  122.9 1.1 pad_maximum_fusion.1
  124.1 0.2 copy.45
  124.4 0.2 copy.46
  124.6 2.1 fusion.56
  126.7 2.3 convolution_convert_fusion.2
  129.0 0.5 copy-done.3
  129.5 1.5 multiply_reduce_fusion.1
  131.0 0.9 convolution_convert_fusion.1
  131.9 0.2 copy.52
  132.1 0.7 copy-done.9
  132.8 2.1 fusion.36
  134.9 6.9 %multiply_bitcast_fusion = f32[1,16,128,256]{3,2,1,0:T(8,128)S(1)} fusion(bf16[128,16,64]{0,2,1:T(8,128)(2,1)} %bitcast.174, bf16[256,16,64]{0,2,1:T(8,128)(2,1)} %bitcast.170, f32[16,128,256]{2,1,0:T(8,128)} %get-tuple-element.23, f32[16,128]{1,0:T(8,128)S(1)} %get-tuple-element.22), kind=kOutput, calls=%fused_computation.22 | convolution fusion | flops 137365760 | bytes 4988928 | tf_op jit(solution)/shard_map/sub | solution.py:197
  141.8 1.4 copy-done.2
  143.2 1.3 fusion.24
  144.5 2.6 convolution_add_fusion
  147.2 0.2 fusion.52
  147.4 3.1 %collective-permute-start.2 = (bf16[1,64,2048]{1,2,0:T(8,128)(2,1)S(1)}, bf16[1,64,2048]{1,2,0:T(8,128)(2,1)S(1)}, u32[]{:S(2)}, u32[]{:S(2)}) collective-permute-start(bf16[1,64,2048]{1,2,0:T(8,128)(2,1)S(1)} %get-tuple-element.12), channel_id=1, source_target_pairs={{0,1},{1,2},{2,3},{3,4},{4,5},{5,6},{6,7},{7,8},{8,9},{9,10},{10,1... | collective-permute-start | bytes 786440 | tf_op jit(solution)/shard_map/ppermute | solution.py:31
  150.6 1.5 collective-permute-start.3
  152.1 8.3 %collective-permute-done.2 = bf16[1,64,2048]{1,2,0:T(8,128)(2,1)S(1)} collective-permute-done((bf16[1,64,2048]{1,2,0:T(8,128)(2,1)S(1)}, bf16[1,64,2048]{1,2,0:T(8,128)(2,1)S(1)}, u32[]{:S(2)}, u32[]{:S(2)}) %collective-permute-start.2) | collective-permute-done | bytes 262176 | tf_op jit(solution)/shard_map/ppermute | solution.py:31
  160.4 3.9 %collective-permute-done.3 = bf16[1,64,2048]{1,2,0:T(8,128)(2,1)S(1)} collective-permute-done((bf16[1,64,2048]{1,2,0:T(8,128)(2,1)S(1)}, bf16[1,64,2048]{1,2,0:T(8,128)(2,1)S(1)}, u32[]{:S(2)}, u32[]{:S(2)}) %collective-permute-start.3) | collective-permute-done | bytes 262176 | tf_op jit(solution)/shard_map/ppermute | solution.py:31
  164.3 0.5 fusion.22
  164.8 24.2 %all_to_all.68 = f32[128,16,2,64]{0,3,2,1:T(8,128)S(1)} all-to-all(f32[128,16,2,64]{0,3,2,1:T(8,128)S(1)} %copy.53), channel_id=1, replica_groups=mesh['dp'=16,'seq'=16] {'seq'}, dimensions={1} | all-to-all | bytes 2097152 | tf_op jit(solution)/shard_map/all_to_all | solution.py:222
  189.0 2.5 broadcast_in_dim.52
  191.6 4.5 %all-to-all-start = ((bf16[16,128,1024]{2,1,0:T(8,128)(2,1)}), bf16[16,128,1024]{2,1,0:T(8,128)(2,1)}, u32[]{:S(2)}, u32[]{:S(2)}) async-start(bf16[16,128,1024]{2,1,0:T(8,128)(2,1)} %broadcast_in_dim.52), calls=%async_computation | async-start | bytes 8388608 | tf_op jit(solution)/shard_map/all_to_all | solution.py:126
  196.1 1.3 compare_select_fusion.1
  197.4 0.3 fusion.23
  197.7 0.3 copy.54
  198.1 0.3 copy.55
  198.4 53.5 %all-to-all-done = bf16[16,128,1024]{2,1,0:T(8,128)(2,1)} async-done(((bf16[16,128,1024]{2,1,0:T(8,128)(2,1)}), bf16[16,128,1024]{2,1,0:T(8,128)(2,1)}, u32[]{:S(2)}, u32[]{:S(2)}) %all-to-all-start) | async-done | bytes 4194336 | tf_op jit(solution)/shard_map/all_to_all | solution.py:126
  251.9 3.5 %fusion.31 = f32[1024,128]{1,0:T(8,128)S(1)} fusion(bf16[2048,1024]{1,0:T(8,128)(2,1)} %bitcast.3, bf16[16,8,16,128]{3,2,1,0:T(8,128)(2,1)S(1)} %bitcast.171), kind=kOutput, calls=%fused_computation.56 | convolution fusion | flops 536870912 | bytes 5242880 | tf_op jit(solution)/shard_map/rf,rg->fg/dot_general | solution.py:93
  255.3 3.5 %convolution_add_fusion.1 = f32[1024,128]{1,0:T(8,128)S(1)} fusion(f32[1024,128]{1,0:T(8,128)S(1)} %fusion.31, bf16[2048,1024]{1,0:T(8,128)(2,1)} %bitcast.3, bf16[16,8,16,128]{3,2,1,0:T(8,128)(2,1)S(1)} %bitcast.167), kind=kOutput, calls=%fused_computation.29 | convolution fusion | flops 537001984 | bytes 5767168 | tf_op jit(solution)/shard_map/rf,rg->fg/dot_general | solution.py:93
  259.0 0.5 all_to_all.59
  259.4 34.3 %all_to_all.69 = f32[256,1,640]{2,1,0:T(1,128)S(1)} all-to-all(f32[256,1,640]{2,1,0:T(1,128)S(1)} %all_to_all.59), channel_id=1, replica_groups=mesh['dp'=16,'seq'=16] {'dp','seq'}, dimensions={0} | all-to-all | bytes 1310720 | tf_op jit(solution)/shard_map/all_to_all | solution.py:233
  293.8 0.6 fusion.55
  295.9 0.7 reshape.410
  (49 shorter events, 1.2 us)
Async XLA Ops:
  7.2 66.8 %copy-start = (bf16[1024,1024]{1,0:T(8,128)(2,1)S(1)}, bf16[1024,1024]{1,0:T(8,128)(2,1)}, u32[]{:S(2)}) copy-start(bf16[1024,1024]{1,0:T(8,128)(2,1)} %param.17) | copy-start | bytes 6291460
  7.2 19.8 %copy-start.6 = (bf16[1,128,1024]{2,1,0:T(8,128)(2,1)S(1)}, bf16[1,128,1024]{2,1,0:T(8,128)(2,1)}, u32[]{:S(2)}) copy-start(bf16[1,128,1024]{2,1,0:T(8,128)(2,1)} %param.10) | copy-start | bytes 786436
  7.2 19.8 %copy-start.7 = (bf16[1,128,1024]{2,1,0:T(8,128)(2,1)S(1)}, bf16[1,128,1024]{2,1,0:T(8,128)(2,1)}, u32[]{:S(2)}) copy-start(bf16[1,128,1024]{2,1,0:T(8,128)(2,1)} %param.11) | copy-start | bytes 786436
  7.2 20.0 %copy-start.12 = (f32[1024]{0:T(1024)S(1)}, f32[1024]{0:T(1024)}, u32[]{:S(2)}) copy-start(f32[1024]{0:T(1024)} %param.15) | copy-start | bytes 12292
  7.2 76.0 %all-gather.2.cloned.1.call-start = ((), (), s32[]{:S(2)}) async-start(), calls=%async_computation.6 | async-start | bytes 8912896 | tf_op jit(solution)/shard_map/all_gather | solution.py:121
  31.2 7.6 %copy-start.11 = (s32[1,2048]{1,0:T(1,128)S(1)}, s32[1,2048]{1,0:T(1,128)}, u32[]{:S(2)}) copy-start(s32[1,2048]{1,0:T(1,128)} %param.13) | copy-start | bytes 24580
  34.5 16.0 %all-to-all-start.2 = ((bf16[1,128,3,16,64]{1,4,2,0,3:T(8,128)(2,1)}), bf16[1,128,3,16,64]{1,4,2,0,3:T(8,128)(2,1)S(1)}, u32[]{:S(2)}, u32[]{:S(2)}) async-start(bf16[1,128,3,16,64]{1,4,2,0,3:T(8,128)(2,1)} %copy.49), calls=%async_computation.2 | async-start | bytes 1572864 | tf_op jit(solution)/shard_map/all_to_all | solution.py:139
  62.7 11.3 %all-to-all-start.3 = ((bf16[1,16,128,1,64]{2,4,3,0,1:T(8,128)(2,1)}), bf16[1,16,128,1,64]{2,4,3,0,1:T(8,128)(2,1)S(1)}, u32[]{:S(2)}, u32[]{:S(2)}) async-start(bf16[1,16,128,1,64]{2,4,3,0,1:T(8,128)(2,1)} %copy.51), calls=%async_computation.3 | async-start | bytes 524288 | tf_op jit(solution)/shard_map/all_to_all | solution.py:143
  110.5 8.5 %collective-permute-start = (bf16[1,64,2048]{2,1,0:T(8,128)(2,1)S(1)}, bf16[1,64,2048]{2,1,0:T(8,128)(2,1)S(1)}, u32[]{:S(2)}, u32[]{:S(2)}) collective-permute-start(bf16[1,64,2048]{2,1,0:T(8,128)(2,1)S(1)} %get-tuple-element.16), channel_id=1, source_target_pairs={{0,1},{1,2},{2,3},{3,4},{4,5},{5,6},{6,7},{7,8},{8,9},{9,10},{10,1... | collective-permute-start | bytes 786440 | tf_op jit(solution)/shard_map/ppermute | solution.py:20
  113.6 9.3 %collective-permute-start.1 = (bf16[1,64,2048]{2,1,0:T(8,128)(2,1)S(1)}, bf16[1,64,2048]{2,1,0:T(8,128)(2,1)}, u32[]{:S(2)}, u32[]{:S(2)}) collective-permute-start(bf16[1,64,2048]{2,1,0:T(8,128)(2,1)S(1)} %get-tuple-element.17), channel_id=1, source_target_pairs={{1,0},{2,1},{3,2},{4,3},{5,4},{6,5},{7,6},{8,7},{9,8},{10,9},{11,1... | collective-permute-start | bytes 786440 | tf_op jit(solution)/shard_map/ppermute | solution.py:23
  115.9 8.7 %copy-start.4 = (bf16[128,1024]{0,1:T(8,128)(2,1)}, bf16[128,1024]{0,1:T(8,128)(2,1)S(1)}, u32[]{:S(2)}) copy-start(bf16[128,1024]{0,1:T(8,128)(2,1)S(1)} %copy.42) | copy-start | bytes 786436
  119.0 0.7 copy-start.10
  124.6 4.4 %copy-start.8 = (bf16[1,256,1024]{1,2,0:T(8,128)(2,1)}, bf16[1,256,1024]{1,2,0:T(8,128)(2,1)S(1)}, u32[]{:S(2)}) copy-start(bf16[1,256,1024]{1,2,0:T(8,128)(2,1)S(1)} %copy.46) | copy-start | bytes 1572868
  126.7 2.8 copy-start.3
  132.0 0.7 copy-start.9
  141.8 1.4 copy-start.2
  143.2 1.3 copy-start.5
  147.4 13.0 %collective-permute-start.2 = (bf16[1,64,2048]{1,2,0:T(8,128)(2,1)S(1)}, bf16[1,64,2048]{1,2,0:T(8,128)(2,1)S(1)}, u32[]{:S(2)}, u32[]{:S(2)}) collective-permute-start(bf16[1,64,2048]{1,2,0:T(8,128)(2,1)S(1)} %get-tuple-element.12), channel_id=1, source_target_pairs={{0,1},{1,2},{2,3},{3,4},{4,5},{5,6},{6,7},{7,8},{8,9},{9,10},{10,1... | collective-permute-start | bytes 786440 | tf_op jit(solution)/shard_map/ppermute | solution.py:31
  150.6 13.7 %collective-permute-start.3 = (bf16[1,64,2048]{1,2,0:T(8,128)(2,1)S(1)}, bf16[1,64,2048]{1,2,0:T(8,128)(2,1)S(1)}, u32[]{:S(2)}, u32[]{:S(2)}) collective-permute-start(bf16[1,64,2048]{1,2,0:T(8,128)(2,1)S(1)} %get-tuple-element.13), channel_id=1, source_target_pairs={{1,0},{2,1},{3,2},{4,3},{5,4},{6,5},{7,6},{8,7},{9,8},{10,9},{11,1... | collective-permute-start | bytes 786440 | tf_op jit(solution)/shard_map/ppermute | solution.py:31
  191.6 60.3 %all-to-all-start = ((bf16[16,128,1024]{2,1,0:T(8,128)(2,1)}), bf16[16,128,1024]{2,1,0:T(8,128)(2,1)}, u32[]{:S(2)}, u32[]{:S(2)}) async-start(bf16[16,128,1024]{2,1,0:T(8,128)(2,1)} %broadcast_in_dim.52), calls=%async_computation | async-start | bytes 8388608 | tf_op jit(solution)/shard_map/all_to_all | solution.py:126
  259.0 38.3 %copy-start.1 = (bf16[1024,1024]{1,0:T(8,128)(2,1)S(1)}, bf16[1024,1024]{1,0:T(8,128)(2,1)}, u32[]{:S(2)}) copy-start(bf16[1024,1024]{1,0:T(8,128)(2,1)} %param.17) | copy-start | bytes 6291460
Sparse Core Ops, SparseCore 0:
  26.5 56.7 all-gather.1

commit v6 on v5

--- a/solution.py
+++ b/solution.py
@@ -115,21 +115,13 @@
     window = shard_rows + 2 * HALO
     rows_each = student_out.shape[0]
     stacked = jnp.concatenate((student_in, student_out[None]), axis=0)
-    seq_count = lax.axis_size("seq")
-    spread = jnp.broadcast_to(stacked[None], (seq_count,) + stacked.shape)
-    spread = lax.all_to_all(spread, "seq", split_axis=0, concat_axis=2, tiled=True)
-    gathered = lax.all_gather(spread.reshape(stacked.shape[0], -1, model_width), "dp", axis=1, tiled=True)
+    gathered = lax.all_gather(
+        lax.all_gather(stacked, "seq", axis=1, tiled=True), "dp", axis=1, tiled=True
+    )
     w_inputs = gathered[:3]
     w_output = gathered[3]
     normed = normalize(clean_frames, noise_frames, time_index, modulation)
     flat_rows = normed.reshape(dialogs * shard_rows, model_width)
-    normed_all = lax.all_to_all(
-        jnp.broadcast_to(flat_rows[None], (seq_count,) + flat_rows.shape),
-        "seq",
-        split_axis=0,
-        concat_axis=0,
-        tiled=True,
-    ).reshape(-1, model_width)
     frame_pos = jnp.arange(frames, dtype=jnp.int32)
     key_bias = jnp.where(frame_pos[None, :] < lengths[:, None], 0.0, NEGATIVE).astype(jnp.float32)
     teacher_proj = jnp.dot(flat_rows, teacher_qkv, preferred_element_type=jnp.float32).astype(
@@ -219,9 +211,12 @@
         owned_rows = owned_rows.at[:, :HALO].add(from_prev)
         owned_rows = owned_rows.at[:, shard_rows - HALO :].add(from_next)
     by_head = owned_rows.reshape(shard_rows, 2, HEADS, head_dim).transpose(0, 2, 1, 3)
-    head_grads = lax.all_to_all(by_head, "seq", split_axis=1, concat_axis=0, tiled=True)
+    head_grads = lax.all_to_all(
+        by_head.astype(jnp.bfloat16), "seq", split_axis=1, concat_axis=0, tiled=True
+    )
     head_grads = head_grads.reshape(frames, 2 * head_dim)
-    partial = split_product("rf,rg->fg", head_grads, normed_all, False)
+    normed_all = lax.all_gather(flat_rows, "seq", axis=0, tiled=True)
+    partial = jnp.dot(normed_all.T, head_grads, preferred_element_type=jnp.float32)
     dp_count = lax.axis_size("dp")
     block = rows_each * 2 * head_dim
     partial = partial.reshape(dp_count * seq_count, block)

time: 306 us -> 227 us (0.74)
  waiting for transfers between devices: 99.1 us -> 68.3 us
  local copies, waits for them, and re-layouts: 39.8 us -> 12.7 us
  blocking collectives: 76.4 us -> 54 us
    all_to_all x1, waiting for transfers between devices: 53.5 us -> 8.73 us  [shards(): lax.all_to_all(by_head.astype(jnp.bfloat16), 'seq', split_axis=1, concat_...]
    all_to_all x2 -> x0, blocking collectives: 42.1 us -> none  [the longest x1 24.2 us: shards(): lax.all_to_all(by_head, 'seq', split_axis=1, concat_axis=0, tiled=True)]
    slice x1 -> x0, local copies, waits for them, and re-layouts: 25.6 us -> none  [shards(): w_inputs[1]]
    all_gather x0 -> x1, blocking collectives: none -> 20 us  [shards(): lax.all_gather(stacked, 'seq', axis=1, tiled=True)]
    ppermute x2, waiting for transfers between devices: 12.2 us -> 22 us  [from_behind(): return lax.ppermute(block, axis, route)]
    all_gather x1 -> x2, waiting for transfers between devices: 8.76 us -> 15.2 us  [the longest x1 15.2 us: shards(): lax.all_gather(lax.all_gather(stacked, 'seq', axis=1, tiled=True), 'dp',...]
    dot_general x2 -> x1, matrix products: 6.95 us -> 3.47 us  [shards(): jnp.dot(normed_all.T, head_grads, preferred_element_type=jnp.float32)]
  transfers between devices with their start and end apart: 8 -> 9, of which waited for: 8 -> 8; matrix products, arithmetic and copies ran while one was open for 8% -> 23% of each run, Pallas kernels for 0% -> 0%
where the time goes in v6:
time: 227 us; the launch traced here: 226 us
  waiting for transfers between devices  68.3 us (30%)
  blocking collectives  54 us (24%)
  matrix products  40.7 us (18%)
  starting transfers between devices  23.3 us (10%)
  between operations  19 us (8%)
  local copies, waits for them, and re-layouts  12.7 us (6%)
  other arithmetic  7.9 us (3%)
    all_to_all x1, blocking collectives, shards(): lax.all_to_all(partial, ('dp', 'seq'), split_axis=0, concat_axis=0, tiled...  34 us
    ppermute x2, waiting for transfers between devices, from_behind(): return lax.ppermute(block, axis, route)  22 us
    all_gather x1, blocking collectives, shards(): lax.all_gather(stacked, 'seq', axis=1, tiled=True)  20 us
    all_gather x1, waiting for transfers between devices, shards(): lax.all_gather(lax.all_gather(stacked, 'seq', axis=1, tiled=True), 'dp',...  15.2 us
    all_to_all x1, waiting for transfers between devices, shards(): lax.all_to_all(teacher_proj, 'seq', split_axis=3, concat_axis=1, tiled=True)  8.89 us
    all_to_all x1, waiting for transfers between devices, shards(): lax.all_to_all(by_head.astype(jnp.bfloat16), 'seq', split_axis=1, concat_...  8.73 us
    all_to_all x1, waiting for transfers between devices, shards(): lax.all_to_all(head_out, 'seq', split_axis=1, concat_axis=1, tiled=True)  6.6 us
    sub x1, matrix products, shards(): grad_prob - jnp.sum(probs * grad_prob, axis=-1, keepdims=True)  6.49 us
  transfers between devices with their start and end apart: 9, of which 8 were waited for; matrix products, arithmetic and copies ran while one was open for 23% of the time, Pallas kernels for 0%

profile of v6, /device:TPU:1, one launch (start us, length us, event | category | flops | bytes accessed | tf_op | source)
XLA Modules:
  0.0 225.8 jit_solution(16827058306706864419)
XLA Ops:
  7.3 0.9 copy.49
  8.2 0.7 copy.50
  8.9 20.0 %all_gather.10 = bf16[4,64,1024]{2,0,1:T(4,128)(2,1)S(1)} all-gather(bf16[4,4,1024]{2,0,1:T(4,128)(2,1)S(1)} %pad_maximum_fusion.3), channel_id=1, replica_groups=mesh['dp'=16,'seq'=16] {'seq'}, dimensions={1}, use_global_device_ids=true | all-gather | bytes 557056 | tf_op jit(solution)/shard_map/all_gather | solution.py:119
  28.9 1.0 copy.51
  30.5 0.2 multiply_reduce_fusion.2
  30.8 0.1 multiply_convert_fusion
  30.9 3.9 %convolution_convert_fusion = bf16[128,3072]{1,0:T(8,128)(2,1)S(1)} fusion(bf16[1024,3072]{1,0:T(8,128)(2,1)} %param.16, bf16[1,128,1024]{2,1,0:T(8,128)(2,1)S(1)} %multiply_convert_fusion), kind=kOutput, calls=%fused_computation.10 | convolution fusion | flops 805699584 | bytes 7340032 | tf_op jit(solution)/shard_map/dot_general | solution.py:127
  34.8 1.2 copy.55
  36.0 2.1 copy.56
  38.2 4.7 %all-to-all-start = ((bf16[1,128,3,16,64]{1,4,2,0,3:T(8,128)(2,1)}), bf16[1,128,3,16,64]{1,4,2,0,3:T(8,128)(2,1)S(1)}, u32[]{:S(2)}, u32[]{:S(2)}) async-start(bf16[1,128,3,16,64]{1,4,2,0,3:T(8,128)(2,1)} %copy.56), calls=%async_computation | async-start | bytes 1572864 | tf_op jit(solution)/shard_map/all_to_all | solution.py:131
  42.9 0.7 all-gather.6.cloned.1.call-update
  44.3 0.1 pad_dynamic-slice_fusion
  44.4 8.9 %all-to-all-done = bf16[1,128,3,16,64]{1,4,2,0,3:T(8,128)(2,1)S(1)} async-done(((bf16[1,128,3,16,64]{1,4,2,0,3:T(8,128)(2,1)}), bf16[1,128,3,16,64]{1,4,2,0,3:T(8,128)(2,1)S(1)}, u32[]{:S(2)}, u32[]{:S(2)}) %all-to-all-start) | async-done | bytes 786464 | tf_op jit(solution)/shard_map/all_to_all | solution.py:131
  53.3 0.1 copy_bitcast_fusion
  53.4 2.6 %fusion.2 = (f32[2048]{0:T(1024)S(1)}, f32[2048,2048]{0,1:T(8,128)S(1)}) fusion(f32[2048]{0:T(1024)S(1)} %fusion.53, bf16[1,2048,3,1,64]{1,4,2,3,0:T(8,128)(2,1)S(1)} %copy_bitcast_fusion), kind=kOutput, calls=%fused_computation.5 | convolution fusion | flops 549451776 | bytes 17317888 | tf_op jit(solution)/shard_map/vmap(vmap())/dot_general | solution.py:45
  56.1 4.6 %fusion.3 = f32[2048]{0:T(1024)S(1)} fusion(f32[2048,2048]{0,1:T(8,128)S(1)} %get-tuple-element.15, f32[2048]{0:T(1024)S(1)} %get-tuple-element.14, f32[2048]{0:T(1024)S(1)} %fusion.53), kind=kLoop, calls=%fused_computation.6 | loop fusion | flops 16775168 | bytes 16801792 | tf_op jit(solution)/shard_map/vmap(vmap())/reduce_sum | solution.py:51
  60.6 4.1 %fusion.24 = bf16[8,8,16,128]{3,1,2,0:T(8,128)(2,1)S(1)} fusion(f32[2048,2048]{0,1:T(8,128)S(1)} %get-tuple-element.15, f32[2048]{0:T(1024)S(1)} %fusion.3, f32[2048]{0:T(1024)S(1)} %get-tuple-element.14, f32[2048]{0:T(1024)S(1)} %fusion.53, bf16[1,2048,3,1,64]{1,4,2,3,0:T(8,128)(2,1)S(1)} %copy_bitcast_fusion), kind=kOutput, calls=%fused_computation.41 | convolution fusion | flops 557973504 | bytes 17326080 | tf_op jit(solution)/shard_map/vmap(vmap())/dot_general | solution.py:52
  64.8 0.8 copy.58
  65.6 3.7 %all-to-all-start.1 = ((bf16[1,16,128,1,64]{2,4,3,0,1:T(8,128)(2,1)}), bf16[1,16,128,1,64]{2,4,3,0,1:T(8,128)(2,1)S(1)}, u32[]{:S(2)}, u32[]{:S(2)}) async-start(bf16[1,16,128,1,64]{2,4,3,0,1:T(8,128)(2,1)} %copy.58), calls=%async_computation.1 | async-start | bytes 524288 | tf_op jit(solution)/shard_map/all_to_all | solution.py:135
  69.3 0.6 convert_reduce_fusion
  69.9 0.1 or_and_fusion
  70.0 6.6 %all-to-all-done.1 = bf16[1,16,128,1,64]{2,4,3,0,1:T(8,128)(2,1)S(1)} async-done(((bf16[1,16,128,1,64]{2,4,3,0,1:T(8,128)(2,1)}), bf16[1,16,128,1,64]{2,4,3,0,1:T(8,128)(2,1)S(1)}, u32[]{:S(2)}, u32[]{:S(2)}) %all-to-all-start.1) | async-done | bytes 262176 | tf_op jit(solution)/shard_map/all_to_all | solution.py:135
  76.6 0.5 convolution_bitcast_fusion
  77.1 15.2 %all-gather.4.cloned.1.call-done = bf16[4,1024,1024]{2,1,0:T(8,128)(2,1)} async-done(((bf16[4,64,1024]{2,1,0:T(8,128)(2,1)}), bf16[4,1024,1024]{2,1,0:T(8,128)(2,1)}) %all-gather.4.cloned.1.call-update) | async-done | bytes 8388624 | tf_op jit(solution)/shard_map/all_gather | solution.py:118
  92.3 2.0 fusion.22
  94.3 2.0 fusion.23
  96.5 3.1 %collective-permute-start = (bf16[1,64,2048]{2,1,0:T(8,128)(2,1)S(1)}, bf16[1,64,2048]{2,1,0:T(8,128)(2,1)S(1)}, u32[]{:S(2)}, u32[]{:S(2)}) collective-permute-start(bf16[1,64,2048]{2,1,0:T(8,128)(2,1)S(1)} %get-tuple-element.10), channel_id=1, source_target_pairs={{0,1},{1,2},{2,3},{3,4},{4,5},{5,6},{6,7},{7,8},{8,9},{9,10},{10,1... | collective-permute-start | bytes 786440 | tf_op jit(solution)/shard_map/ppermute | solution.py:20
  99.6 1.3 collective-permute-start.1
  100.9 2.0 fusion.21
  102.9 0.2 copy.52
  103.1 1.8 collective-permute-done
  104.9 4.3 %collective-permute-done.1 = bf16[1,64,2048]{2,1,0:T(8,128)(2,1)S(1)} collective-permute-done((bf16[1,64,2048]{2,1,0:T(8,128)(2,1)S(1)}, bf16[1,64,2048]{2,1,0:T(8,128)(2,1)S(1)}, u32[]{:S(2)}, u32[]{:S(2)}) %collective-permute-start.1) | collective-permute-done | bytes 262176 | tf_op jit(solution)/shard_map/ppermute | solution.py:23
  109.2 0.1 pad_maximum_fusion.1
  109.4 0.2 copy.53
  109.7 0.2 copy.54
  109.9 2.1 fusion.61
  111.9 2.2 convolution_convert_fusion.1
  114.1 2.8 %multiply_reduce_fusion.1 = (f32[]{:T(128)}, bf16[128,1024]{1,0:T(8,128)(2,1)S(1)}) fusion(f32[128,1024]{1,0:T(8,128)S(1)} %convolution_bitcast_fusion, bf16[128,1024]{0,1:T(8,128)(2,1)S(1)} %bitcast.169, bf16[4,1024,1024]{2,1,0:T(8,128)(2,1)} %all-gather.4.cloned.1.call-done, pred[128]{0:T(512)(128)(4,1)S(1)} %get-tuple-element.3), kind=kOutput, calls=%fused_computation.59 | convolution fusion | flops 269090816 | bytes 3145860 | tf_op jit(solution)/shard_map/dot_general | solution.py:176
  116.9 2.4 %fusion.20 = bf16[128,1024]{1,0:T(8,128)(2,1)S(1)} fusion(bf16[4,1024,1024]{2,1,0:T(8,128)(2,1)} %all-gather.4.cloned.1.call-done, bf16[128,1024]{1,0:T(8,128)(2,1)S(1)} %get-tuple-element.19), kind=kOutput, calls=%fused_computation.36 | convolution fusion | flops 268566528 | bytes 2621440 | tf_op jit(solution)/shard_map/dot_general | solution.py:182
  119.3 0.2 copy.59
  119.5 6.5 %multiply_bitcast_fusion = f32[1,16,128,256]{3,2,1,0:T(8,128)S(1)} fusion(bf16[128,16,64]{0,2,1:T(8,128)(2,1)S(1)} %bitcast.164, bf16[256,16,64]{0,2,1:T(8,128)(2,1)S(1)} %bitcast.161, f32[16,128,256]{2,1,0:T(8,128)} %get-tuple-element.17, f32[16,128]{1,0:T(8,128)S(1)} %get-tuple-element.16), kind=kOutput, calls=%fused_computation.24 | convolution fusion | flops 137365760 | bytes 4988928 | tf_op jit(solution)/shard_map/sub | solution.py:189
  126.0 1.3 copy-done.2
  127.3 0.3 fusion.30
  127.6 3.1 %convolution_add_fusion = f32[16,64,256]{2,1,0:T(8,128)S(1)} fusion(f32[16,64,256]{2,1,0:T(8,128)S(1)} %fusion.30, bf16[128,16,64]{0,2,1:T(8,128)(2,1)S(1)} %bitcast.156, f32[1,16,128,256]{3,2,1,0:T(8,128)} %copy-done.2), kind=kOutput, calls=%fused_computation.32 | convolution fusion | flops 69468160 | bytes 4456448 | tf_op jit(solution)/shard_map/bhrw,brhd->bwhd/dot_general | solution.py:90
  130.7 0.1 copy-done.9
  130.8 0.8 fusion.39
  131.6 0.1 fusion.8
  131.7 0.2 fusion.57
  132.0 3.1 %collective-permute-start.2 = (bf16[1,64,2048]{1,2,0:T(8,128)(2,1)S(1)}, bf16[1,64,2048]{1,2,0:T(8,128)(2,1)S(1)}, u32[]{:S(2)}, u32[]{:S(2)}) collective-permute-start(bf16[1,64,2048]{1,2,0:T(8,128)(2,1)S(1)} %get-tuple-element.6), channel_id=1, source_target_pairs={{0,1},{1,2},{2,3},{3,4},{4,5},{5,6},{6,7},{7,8},{8,9},{9,10},{10,1... | collective-permute-start | bytes 786440 | tf_op jit(solution)/shard_map/ppermute | solution.py:31
  135.1 1.3 collective-permute-start.3
  136.4 19.9 %collective-permute-done.2 = bf16[1,64,2048]{1,2,0:T(8,128)(2,1)S(1)} collective-permute-done((bf16[1,64,2048]{1,2,0:T(8,128)(2,1)S(1)}, bf16[1,64,2048]{1,2,0:T(8,128)(2,1)S(1)}, u32[]{:S(2)}, u32[]{:S(2)}) %collective-permute-start.2) | collective-permute-done | bytes 262176 | tf_op jit(solution)/shard_map/ppermute | solution.py:31
  156.2 2.2 collective-permute-done.3
  158.4 0.5 fusion.29
  158.9 0.8 copy.60
  159.7 6.1 %all-to-all-start.2 = ((bf16[128,16,2,64]{0,3,2,1:T(8,128)(2,1)}), bf16[128,16,2,64]{0,3,2,1:T(8,128)(2,1)S(1)}, u32[]{:S(2)}, u32[]{:S(2)}) async-start(bf16[128,16,2,64]{0,3,2,1:T(8,128)(2,1)} %copy.60), calls=%async_computation.2 | async-start | bytes 1048576 | tf_op jit(solution)/shard_map/all_to_all | solution.py:214
  165.8 1.3 compare_select_fusion.1
  167.1 8.7 %all-to-all-done.2 = bf16[128,16,2,64]{0,3,2,1:T(8,128)(2,1)S(1)} async-done(((bf16[128,16,2,64]{0,3,2,1:T(8,128)(2,1)}), bf16[128,16,2,64]{0,3,2,1:T(8,128)(2,1)S(1)}, u32[]{:S(2)}, u32[]{:S(2)}) %all-to-all-start.2) | async-done | bytes 524320 | tf_op jit(solution)/shard_map/all_to_all | solution.py:214
  175.8 0.3 copy.61
  176.2 3.5 %fusion.5 = f32[1024,128]{1,0:T(8,128)S(1)} fusion(bf16[1,2048,1024]{2,1,0:T(8,128)(2,1)} %all-gather.6.cloned.1.call-done, bf16[16,8,16,128]{3,2,1,0:T(8,128)(2,1)S(1)} %bitcast.163), kind=kOutput, calls=%fused_computation.8 | convolution fusion | flops 536870912 | bytes 5242880 | tf_op jit(solution)/shard_map/dot_general | solution.py:219
  179.8 0.5 all_to_all.41
  180.3 34.0 %all_to_all.47 = f32[256,1,640]{2,1,0:T(1,128)S(1)} all-to-all(f32[256,1,640]{2,1,0:T(1,128)S(1)} %all_to_all.41), channel_id=1, replica_groups=mesh['dp'=16,'seq'=16] {'dp','seq'}, dimensions={0} | all-to-all | bytes 1310720 | tf_op jit(solution)/shard_map/all_to_all | solution.py:228
  214.4 0.6 fusion.60
  216.4 0.1 mul.117
  216.5 0.7 reshape.402
  (42 shorter events, 0.7 us)
Async XLA Ops:
  7.2 69.5 %copy-start = (bf16[1024,1024]{1,0:T(8,128)(2,1)S(1)}, bf16[1024,1024]{1,0:T(8,128)(2,1)}, u32[]{:S(2)}) copy-start(bf16[1024,1024]{1,0:T(8,128)(2,1)} %param.17) | copy-start | bytes 6291460
  7.2 23.3 %copy-start.5 = (bf16[1,128,1024]{2,1,0:T(8,128)(2,1)S(1)}, bf16[1,128,1024]{2,1,0:T(8,128)(2,1)}, u32[]{:S(2)}) copy-start(bf16[1,128,1024]{2,1,0:T(8,128)(2,1)} %param.10) | copy-start | bytes 786436
  7.2 23.3 %copy-start.6 = (bf16[1,128,1024]{2,1,0:T(8,128)(2,1)S(1)}, bf16[1,128,1024]{2,1,0:T(8,128)(2,1)}, u32[]{:S(2)}) copy-start(bf16[1,128,1024]{2,1,0:T(8,128)(2,1)} %param.11) | copy-start | bytes 786436
  7.2 23.6 %copy-start.8 = (f32[1024]{0:T(1024)S(1)}, f32[1024]{0:T(1024)}, u32[]{:S(2)}) copy-start(f32[1024]{0:T(1024)} %param.15) | copy-start | bytes 12292
  7.2 85.1 %all-gather.4.cloned.1.call-start = ((), (), s32[]{:S(2)}) async-start(), calls=%async_computation.4 | async-start | bytes 8912896 | tf_op jit(solution)/shard_map/all_gather | solution.py:118
  30.9 3.9 %copy-start.3 = (bf16[1,128,1024]{2,1,0:T(8,128)(2,1)}, bf16[1,128,1024]{2,1,0:T(8,128)(2,1)S(1)}, u32[]{:S(2)}) copy-start(bf16[1,128,1024]{2,1,0:T(8,128)(2,1)S(1)} %multiply_convert_fusion) | copy-start | bytes 786436
  36.0 8.3 %copy-start.7 = (s32[1,2048]{1,0:T(1,128)S(1)}, s32[1,2048]{1,0:T(1,128)}, u32[]{:S(2)}) copy-start(s32[1,2048]{1,0:T(1,128)} %param.13) | copy-start | bytes 24580
  38.2 15.1 %all-to-all-start = ((bf16[1,128,3,16,64]{1,4,2,0,3:T(8,128)(2,1)}), bf16[1,128,3,16,64]{1,4,2,0,3:T(8,128)(2,1)S(1)}, u32[]{:S(2)}, u32[]{:S(2)}) async-start(bf16[1,128,3,16,64]{1,4,2,0,3:T(8,128)(2,1)} %copy.56), calls=%async_computation | async-start | bytes 1572864 | tf_op jit(solution)/shard_map/all_to_all | solution.py:131
  42.8 133.3 %all-gather.6.cloned.1.call-start = ((), (), s32[]{:S(2)}) async-start(), calls=%async_computation.5 | async-start | bytes 4456448 | tf_op jit(solution)/shard_map/all_gather | solution.py:218
  64.8 27.5 %copy-start.4 = (bf16[1,128,1024]{2,1,0:T(8,128)(2,1)S(1)}, bf16[1,128,1024]{2,1,0:T(8,128)(2,1)}, u32[]{:S(2)}) copy-start(bf16[1,128,1024]{2,1,0:T(8,128)(2,1)} %copy-done.3) | copy-start | bytes 786436
  65.6 11.0 %all-to-all-start.1 = ((bf16[1,16,128,1,64]{2,4,3,0,1:T(8,128)(2,1)}), bf16[1,16,128,1,64]{2,4,3,0,1:T(8,128)(2,1)S(1)}, u32[]{:S(2)}, u32[]{:S(2)}) async-start(bf16[1,16,128,1,64]{2,4,3,0,1:T(8,128)(2,1)} %copy.58), calls=%async_computation.1 | async-start | bytes 524288 | tf_op jit(solution)/shard_map/all_to_all | solution.py:135
  96.5 8.5 %collective-permute-start = (bf16[1,64,2048]{2,1,0:T(8,128)(2,1)S(1)}, bf16[1,64,2048]{2,1,0:T(8,128)(2,1)S(1)}, u32[]{:S(2)}, u32[]{:S(2)}) collective-permute-start(bf16[1,64,2048]{2,1,0:T(8,128)(2,1)S(1)} %get-tuple-element.10), channel_id=1, source_target_pairs={{0,1},{1,2},{2,3},{3,4},{4,5},{5,6},{6,7},{7,8},{8,9},{9,10},{10,1... | collective-permute-start | bytes 786440 | tf_op jit(solution)/shard_map/ppermute | solution.py:20
  99.6 9.7 %collective-permute-start.1 = (bf16[1,64,2048]{2,1,0:T(8,128)(2,1)S(1)}, bf16[1,64,2048]{2,1,0:T(8,128)(2,1)S(1)}, u32[]{:S(2)}, u32[]{:S(2)}) collective-permute-start(bf16[1,64,2048]{2,1,0:T(8,128)(2,1)S(1)} %get-tuple-element.11), channel_id=1, source_target_pairs={{1,0},{2,1},{3,2},{4,3},{5,4},{6,5},{7,6},{8,7},{9,8},{10,9},{11,1... | collective-permute-start | bytes 786440 | tf_op jit(solution)/shard_map/ppermute | solution.py:23
  126.0 1.3 copy-start.2
  127.6 3.2 %copy-start.9 = (f32[16,128,256]{2,1,0:T(8,128)S(1)}, f32[16,128,256]{2,1,0:T(8,128)}, u32[]{:S(2)}) copy-start(f32[16,128,256]{2,1,0:T(8,128)} %get-tuple-element.17) | copy-start | bytes 6291460
  132.0 24.3 %collective-permute-start.2 = (bf16[1,64,2048]{1,2,0:T(8,128)(2,1)S(1)}, bf16[1,64,2048]{1,2,0:T(8,128)(2,1)S(1)}, u32[]{:S(2)}, u32[]{:S(2)}) collective-permute-start(bf16[1,64,2048]{1,2,0:T(8,128)(2,1)S(1)} %get-tuple-element.6), channel_id=1, source_target_pairs={{0,1},{1,2},{2,3},{3,4},{4,5},{5,6},{6,7},{7,8},{8,9},{9,10},{10,1... | collective-permute-start | bytes 786440 | tf_op jit(solution)/shard_map/ppermute | solution.py:31
  135.1 23.3 %collective-permute-start.3 = (bf16[1,64,2048]{1,2,0:T(8,128)(2,1)S(1)}, bf16[1,64,2048]{1,2,0:T(8,128)(2,1)S(1)}, u32[]{:S(2)}, u32[]{:S(2)}) collective-permute-start(bf16[1,64,2048]{1,2,0:T(8,128)(2,1)S(1)} %get-tuple-element.7), channel_id=1, source_target_pairs={{1,0},{2,1},{3,2},{4,3},{5,4},{6,5},{7,6},{8,7},{9,8},{10,9},{11,1... | collective-permute-start | bytes 786440 | tf_op jit(solution)/shard_map/ppermute | solution.py:31
  159.7 16.1 %all-to-all-start.2 = ((bf16[128,16,2,64]{0,3,2,1:T(8,128)(2,1)}), bf16[128,16,2,64]{0,3,2,1:T(8,128)(2,1)S(1)}, u32[]{:S(2)}, u32[]{:S(2)}) async-start(bf16[128,16,2,64]{0,3,2,1:T(8,128)(2,1)} %copy.60), calls=%async_computation.2 | async-start | bytes 1048576 | tf_op jit(solution)/shard_map/all_to_all | solution.py:214
  179.8 38.0 %copy-start.1 = (bf16[1024,1024]{1,0:T(8,128)(2,1)S(1)}, bf16[1024,1024]{1,0:T(8,128)(2,1)}, u32[]{:S(2)}) copy-start(bf16[1024,1024]{1,0:T(8,128)(2,1)} %param.17) | copy-start | bytes 6291460
Sparse Core Ops, SparseCore 0:
  30.0 62.2 all-gather.3
  94.7 61.6 all-gather.5

commit v7 on v6

--- a/solution.py
+++ b/solution.py
@@ -115,11 +115,9 @@
     window = shard_rows + 2 * HALO
     rows_each = student_out.shape[0]
     stacked = jnp.concatenate((student_in, student_out[None]), axis=0)
-    gathered = lax.all_gather(
-        lax.all_gather(stacked, "seq", axis=1, tiled=True), "dp", axis=1, tiled=True
-    )
-    w_inputs = gathered[:3]
-    w_output = gathered[3]
+    by_seq = lax.all_gather(stacked, "seq", axis=1, tiled=True)
+    w_inputs = lax.all_gather(by_seq[:3], "dp", axis=1, tiled=True)
+    w_output = lax.all_gather(by_seq[3], "dp", axis=0, tiled=True)
     normed = normalize(clean_frames, noise_frames, time_index, modulation)
     flat_rows = normed.reshape(dialogs * shard_rows, model_width)
     frame_pos = jnp.arange(frames, dtype=jnp.int32)

time: 227 us -> 243 us (1.070)
  waiting for transfers between devices: 68.3 us -> 75.9 us
  local copies, waits for them, and re-layouts: 12.7 us -> 16.3 us
    ppermute x2, waiting for transfers between devices: 22 us -> 14.4 us  [from_behind(): return lax.ppermute(block, axis, route)]
    all_gather x1, waiting for transfers between devices: 0.02 us -> 7.04 us  [shards(): normed_all = lax.all_gather(flat_rows, 'seq', axis=0, tiled=True)]
    all_to_all x1, waiting for transfers between devices: 8.73 us -> 15.5 us  [shards(): lax.all_to_all(by_head.astype(jnp.bfloat16), 'seq', split_axis=1, concat_...]
    all_gather x1 -> x2, waiting for transfers between devices: 15.2 us -> 18.7 us  [the longest x1 15.2 us: shards(): w_output = lax.all_gather(by_seq[3], 'dp', axis=0, tiled=True)]
    dot_general x1, matrix products: 3.09 us -> 0.29 us  [split_product(): jnp.einsum(form, lower_part, other, preferred_element_type=jnp.float32)]
  transfers between devices with their start and end apart: 9 -> 10, of which waited for: 8 -> 9; matrix products, arithmetic and copies ran while one was open for 23% -> 23% of each run, Pallas kernels for 0% -> 0%
where the time goes in v7:
time: 243 us; the launch traced here: 242 us
  waiting for transfers between devices  75.9 us (31%)
  blocking collectives  54.5 us (22%)
  matrix products  42.8 us (18%)
  starting transfers between devices  25 us (10%)
  between operations  18.6 us (8%)
  local copies, waits for them, and re-layouts  16.3 us (7%)
  other arithmetic  8.92 us (4%)
    all_to_all x1, blocking collectives, shards(): lax.all_to_all(partial, ('dp', 'seq'), split_axis=0, concat_axis=0, tiled...  34.5 us
    all_gather x1, blocking collectives, shards(): by_seq = lax.all_gather(stacked, 'seq', axis=1, tiled=True)  20 us
    all_to_all x1, waiting for transfers between devices, shards(): lax.all_to_all(by_head.astype(jnp.bfloat16), 'seq', split_axis=1, concat_...  15.5 us
    all_gather x1, waiting for transfers between devices, shards(): w_output = lax.all_gather(by_seq[3], 'dp', axis=0, tiled=True)  15.2 us
    ppermute x2, waiting for transfers between devices, from_behind(): return lax.ppermute(block, axis, route)  14.4 us
    all_to_all x1, waiting for transfers between devices, shards(): lax.all_to_all(teacher_proj, 'seq', split_axis=3, concat_axis=1, tiled=True)  8.9 us
    sub x1, matrix products, shards(): grad_prob - jnp.sum(probs * grad_prob, axis=-1, keepdims=True)  7.5 us
    all_to_all x1, starting transfers between devices, shards(): lax.all_to_all(by_head.astype(jnp.bfloat16), 'seq', split_axis=1, concat_...  7.14 us
  transfers between devices with their start and end apart: 10, of which 9 were waited for; matrix products, arithmetic and copies ran while one was open for 23% of the time, Pallas kernels for 0%

profile of v7, /device:TPU:1, one launch (start us, length us, event | category | flops | bytes accessed | tf_op | source)
XLA Modules:
  0.0 242.0 jit_solution(13347085285352139939)
XLA Ops:
  7.3 0.9 copy.49
  8.2 0.7 copy.50
  8.9 20.0 %all_gather.13 = bf16[4,64,1024]{2,0,1:T(4,128)(2,1)S(1)} all-gather(bf16[4,4,1024]{2,0,1:T(4,128)(2,1)S(1)} %pad_maximum_fusion.3), channel_id=1, replica_groups=mesh['dp'=16,'seq'=16] {'seq'}, dimensions={1}, use_global_device_ids=true | all-gather | bytes 557056 | tf_op jit(solution)/shard_map/all_gather | solution.py:118
  28.9 0.9 copy.65
  29.9 0.3 slice.86
  30.2 0.7 copy.66
  31.6 0.2 multiply_reduce_fusion.2
  31.8 0.1 multiply_convert_fusion
  31.9 3.9 %convolution_convert_fusion = bf16[128,3072]{1,0:T(8,128)(2,1)S(1)} fusion(bf16[1024,3072]{1,0:T(8,128)(2,1)} %param.16, bf16[1,128,1024]{2,1,0:T(8,128)(2,1)S(1)} %multiply_convert_fusion), kind=kOutput, calls=%fused_computation.10 | convolution fusion | flops 805699584 | bytes 7340032 | tf_op jit(solution)/shard_map/dot_general | solution.py:125
  35.8 1.2 copy.56
  37.0 2.1 copy.57
  39.2 4.7 %all-to-all-start = ((bf16[1,128,3,16,64]{1,4,2,0,3:T(8,128)(2,1)}), bf16[1,128,3,16,64]{1,4,2,0,3:T(8,128)(2,1)S(1)}, u32[]{:S(2)}, u32[]{:S(2)}) async-start(bf16[1,128,3,16,64]{1,4,2,0,3:T(8,128)(2,1)} %copy.57), calls=%async_computation | async-start | bytes 1572864 | tf_op jit(solution)/shard_map/all_to_all | solution.py:129
  43.9 0.7 all-gather.8.cloned.1.call-update
  45.4 8.9 %all-to-all-done = bf16[1,128,3,16,64]{1,4,2,0,3:T(8,128)(2,1)S(1)} async-done(((bf16[1,128,3,16,64]{1,4,2,0,3:T(8,128)(2,1)}), bf16[1,128,3,16,64]{1,4,2,0,3:T(8,128)(2,1)S(1)}, u32[]{:S(2)}, u32[]{:S(2)}) %all-to-all-start) | async-done | bytes 786464 | tf_op jit(solution)/shard_map/all_to_all | solution.py:129
  54.4 2.6 %fusion.2 = (f32[2048]{0:T(1024)S(1)}, f32[2048,2048]{0,1:T(8,128)S(1)}) fusion(f32[2048]{0:T(1024)S(1)} %fusion.61, bf16[1,2048,3,1,64]{1,4,2,3,0:T(8,128)(2,1)S(1)} %copy_bitcast_fusion), kind=kOutput, calls=%fused_computation.5 | convolution fusion | flops 549451776 | bytes 17317888 | tf_op jit(solution)/shard_map/vmap(vmap())/dot_general | solution.py:45
  57.0 4.6 %fusion.3 = f32[2048]{0:T(1024)S(1)} fusion(f32[2048,2048]{0,1:T(8,128)S(1)} %get-tuple-element.15, f32[2048]{0:T(1024)S(1)} %get-tuple-element.14, f32[2048]{0:T(1024)S(1)} %fusion.61), kind=kLoop, calls=%fused_computation.6 | loop fusion | flops 16775168 | bytes 16801792 | tf_op jit(solution)/shard_map/vmap(vmap())/reduce_sum | solution.py:51
  61.6 4.1 %fusion.32 = bf16[8,8,16,128]{3,1,2,0:T(8,128)(2,1)S(1)} fusion(f32[2048,2048]{0,1:T(8,128)S(1)} %get-tuple-element.15, f32[2048]{0:T(1024)S(1)} %fusion.3, f32[2048]{0:T(1024)S(1)} %get-tuple-element.14, f32[2048]{0:T(1024)S(1)} %fusion.61, bf16[1,2048,3,1,64]{1,4,2,3,0:T(8,128)(2,1)S(1)} %copy_bitcast_fusion), kind=kOutput, calls=%fused_computation.42 | convolution fusion | flops 557973504 | bytes 17326080 | tf_op jit(solution)/shard_map/vmap(vmap())/dot_general | solution.py:52
  65.8 0.8 copy.59
  66.5 3.7 %all-to-all-start.1 = ((bf16[1,16,128,1,64]{2,4,3,0,1:T(8,128)(2,1)}), bf16[1,16,128,1,64]{2,4,3,0,1:T(8,128)(2,1)S(1)}, u32[]{:S(2)}, u32[]{:S(2)}) async-start(bf16[1,16,128,1,64]{2,4,3,0,1:T(8,128)(2,1)} %copy.59), calls=%async_computation.1 | async-start | bytes 524288 | tf_op jit(solution)/shard_map/all_to_all | solution.py:133
  70.3 0.6 convert_reduce_fusion
  71.0 6.6 %all-to-all-done.1 = bf16[1,16,128,1,64]{2,4,3,0,1:T(8,128)(2,1)S(1)} async-done(((bf16[1,16,128,1,64]{2,4,3,0,1:T(8,128)(2,1)}), bf16[1,16,128,1,64]{2,4,3,0,1:T(8,128)(2,1)S(1)}, u32[]{:S(2)}, u32[]{:S(2)}) %all-to-all-start.1) | async-done | bytes 262176 | tf_op jit(solution)/shard_map/all_to_all | solution.py:133
  77.6 1.3 convolution_bitcast_fusion
  78.9 3.6 %all-gather.6.cloned.1.call-done = bf16[3,1024,1024]{2,1,0:T(8,128)(2,1)} async-done(((bf16[3,64,1024]{2,1,0:T(8,128)(2,1)}), bf16[3,1024,1024]{2,1,0:T(8,128)(2,1)}) %all-gather.6.cloned.1.call-update) | async-done | bytes 6291472 | tf_op jit(solution)/shard_map/all_gather | solution.py:119
  82.4 2.0 fusion.30
  84.5 2.0 fusion.31
  86.6 0.8 fusion.67
  87.3 3.8 %collective-permute-start = (bf16[1,64,2048]{2,1,0:T(8,128)(2,1)}, bf16[1,64,2048]{2,1,0:T(8,128)(2,1)}, u32[]{:S(2)}, u32[]{:S(2)}) collective-permute-start(bf16[1,64,2048]{2,1,0:T(8,128)(2,1)} %get-tuple-element.10), channel_id=1, source_target_pairs={{0,1},{1,2},{2,3},{3,4},{4,5},{5,6},{6,7},{7,8},{8,9},{9,10},{10,1... | collective-permute-start | bytes 786440 | tf_op jit(solution)/shard_map/ppermute | solution.py:20
  91.1 1.3 collective-permute-start.1
  92.4 2.0 fusion.29
  94.5 0.2 copy.52
  94.6 4.0 %collective-permute-done.1 = bf16[1,64,2048]{2,1,0:T(8,128)(2,1)} collective-permute-done((bf16[1,64,2048]{2,1,0:T(8,128)(2,1)S(1)}, bf16[1,64,2048]{2,1,0:T(8,128)(2,1)}, u32[]{:S(2)}, u32[]{:S(2)}) %collective-permute-start.1) | collective-permute-done | bytes 262176 | tf_op jit(solution)/shard_map/ppermute | solution.py:23
  98.6 1.1 pad_maximum_fusion.1
  99.9 1.0 copy.53
  100.9 0.2 copy.54
  101.1 3.1 %fusion.69 = (f32[16,128]{1,0:T(8,128)S(1)}, f32[16,128,256]{2,1,0:T(8,128)}) fusion(pred[128,256]{1,0:T(8,128)(4,1)S(1)} %or_and_fusion, bf16[128,16,64]{0,2,1:T(8,128)(2,1)S(1)} %bitcast.157, bf16[256,16,64]{0,2,1:T(8,128)(2,1)} %bitcast.165), kind=kOutput, calls=%fused_computation.106 | convolution fusion | flops 69206272 | bytes 2924544 | tf_op jit(solution)/shard_map/sub | solution.py:167
  104.2 3.0 %convolution_convert_fusion.1 = bf16[16,64,128]{2,1,0:T(8,128)(2,1)} fusion(bf16[256,16,64]{0,2,1:T(8,128)(2,1)S(1)} %bitcast.163, f32[16,128,256]{2,1,0:T(8,128)} %get-tuple-element.17, f32[16,128]{1,0:T(8,128)S(1)} %get-tuple-element.16), kind=kOutput, calls=%fused_computation.41 | convolution fusion | flops 68288512 | bytes 2891776 | tf_op jit(solution)/shard_map/bhrw,bwhd->brhd/dot_general | solution.py:170
  107.2 15.2 %all-gather.10.cloned.1.call-done = bf16[1,1024,1024]{2,1,0:T(8,128)(2,1)} async-done(((bf16[1,64,1024]{2,1,0:T(8,128)(2,1)}), bf16[1,1024,1024]{2,1,0:T(8,128)(2,1)}) %all-gather.10.cloned.1.call-update) | async-done | bytes 2097168 | tf_op jit(solution)/shard_map/all_gather | solution.py:120
  122.3 3.0 %multiply_reduce_fusion.1 = (f32[]{:T(128)}, bf16[128,1024]{1,0:T(8,128)(2,1)S(1)}) fusion(f32[128,1024]{1,0:T(8,128)S(1)} %copy-done.5, bf16[128,1024]{0,1:T(8,128)(2,1)} %bitcast.167, bf16[1,1024,1024]{2,1,0:T(8,128)(2,1)} %all-gather.10.cloned.1.call-done, pred[128]{0:T(512)(128)(4,1)S(1)} %get-tuple-element.3), kind=kOutput, calls=%fused_computation.60 | convolution fusion | flops 269090816 | bytes 3145860 | tf_op jit(solution)/shard_map/dot_general | solution.py:174
  125.3 0.8 fusion.26
  126.1 0.2 copy.60
  126.3 7.5 %multiply_bitcast_fusion = f32[1,16,128,256]{3,2,1,0:T(8,128)} fusion(bf16[128,16,64]{0,2,1:T(8,128)(2,1)S(1)} %bitcast.168, bf16[256,16,64]{0,2,1:T(8,128)(2,1)S(1)} %bitcast.164, f32[16,128,256]{2,1,0:T(8,128)} %get-tuple-element.17, f32[16,128]{1,0:T(8,128)S(1)} %get-tuple-element.16), kind=kOutput, calls=%fused_computation.27 | convolution fusion | flops 137365760 | bytes 4988928 | tf_op jit(solution)/shard_map/sub | solution.py:187
  133.8 2.1 fusion.38
  135.9 0.3 copy-done.2
  136.2 0.3 convolution_add_fusion
  136.5 1.3 copy-done.10
  137.8 0.8 fusion.47
  138.7 0.2 fusion.65
  138.9 3.0 %collective-permute-start.2 = (bf16[1,64,2048]{1,2,0:T(8,128)(2,1)S(1)}, bf16[1,64,2048]{1,2,0:T(8,128)(2,1)S(1)}, u32[]{:S(2)}, u32[]{:S(2)}) collective-permute-start(bf16[1,64,2048]{1,2,0:T(8,128)(2,1)S(1)} %get-tuple-element.6), channel_id=1, source_target_pairs={{0,1},{1,2},{2,3},{3,4},{4,5},{5,6},{6,7},{7,8},{8,9},{9,10},{10,1... | collective-permute-start | bytes 786440 | tf_op jit(solution)/shard_map/ppermute | solution.py:31
  142.0 1.3 collective-permute-start.3
  143.3 11.2 %collective-permute-done.2 = bf16[1,64,2048]{1,2,0:T(8,128)(2,1)S(1)} collective-permute-done((bf16[1,64,2048]{1,2,0:T(8,128)(2,1)S(1)}, bf16[1,64,2048]{1,2,0:T(8,128)(2,1)S(1)}, u32[]{:S(2)}, u32[]{:S(2)}) %collective-permute-start.2) | collective-permute-done | bytes 262176 | tf_op jit(solution)/shard_map/ppermute | solution.py:31
  154.5 3.2 %collective-permute-done.3 = bf16[1,64,2048]{1,2,0:T(8,128)(2,1)S(1)} collective-permute-done((bf16[1,64,2048]{1,2,0:T(8,128)(2,1)S(1)}, bf16[1,64,2048]{1,2,0:T(8,128)(2,1)S(1)}, u32[]{:S(2)}, u32[]{:S(2)}) %collective-permute-start.3) | collective-permute-done | bytes 262176 | tf_op jit(solution)/shard_map/ppermute | solution.py:31
  157.7 0.5 fusion.37
  158.2 0.8 copy.61
  159.0 7.1 %all-to-all-start.2 = ((bf16[128,16,2,64]{0,3,2,1:T(8,128)(2,1)}), bf16[128,16,2,64]{0,3,2,1:T(8,128)(2,1)S(1)}, u32[]{:S(2)}, u32[]{:S(2)}) async-start(bf16[128,16,2,64]{0,3,2,1:T(8,128)(2,1)} %copy.61), calls=%async_computation.2 | async-start | bytes 1048576 | tf_op jit(solution)/shard_map/all_to_all | solution.py:212
  166.1 1.3 compare_select_fusion.1
  167.5 15.5 %all-to-all-done.2 = bf16[128,16,2,64]{0,3,2,1:T(8,128)(2,1)S(1)} async-done(((bf16[128,16,2,64]{0,3,2,1:T(8,128)(2,1)}), bf16[128,16,2,64]{0,3,2,1:T(8,128)(2,1)S(1)}, u32[]{:S(2)}, u32[]{:S(2)}) %all-to-all-start.2) | async-done | bytes 524320 | tf_op jit(solution)/shard_map/all_to_all | solution.py:212
  183.0 0.3 copy.62
  183.3 7.0 %all-gather.8.cloned.1.call-done = bf16[1,2048,1024]{2,1,0:T(8,128)(2,1)} async-done(((bf16[1,128,1024]{2,1,0:T(8,128)(2,1)}), bf16[1,2048,1024]{2,1,0:T(8,128)(2,1)}) %all-gather.8.cloned.1.call-update) | async-done | bytes 4194320 | tf_op jit(solution)/shard_map/all_gather | solution.py:216
  190.3 4.3 %fusion.5 = f32[1024,128]{1,0:T(8,128)} fusion(bf16[1,2048,1024]{2,1,0:T(8,128)(2,1)} %all-gather.8.cloned.1.call-done, bf16[16,8,16,128]{3,2,1,0:T(8,128)(2,1)S(1)} %bitcast.166), kind=kOutput, calls=%fused_computation.8 | convolution fusion | flops 536870912 | bytes 5242880 | tf_op jit(solution)/shard_map/dot_general | solution.py:217
  194.6 1.1 reshape.400
  195.8 0.5 all_to_all.41
  196.3 34.5 %all_to_all.47 = f32[256,1,640]{2,1,0:T(1,128)S(1)} all-to-all(f32[256,1,640]{2,1,0:T(1,128)S(1)} %all_to_all.41), channel_id=1, replica_groups=mesh['dp'=16,'seq'=16] {'dp','seq'}, dimensions={0} | all-to-all | bytes 1310720 | tf_op jit(solution)/shard_map/all_to_all | solution.py:226
  230.9 0.6 fusion.68
  233.0 0.7 reshape.402
  (49 shorter events, 1.2 us)
Async XLA Ops:
  7.2 70.4 %copy-start = (bf16[1024,1024]{1,0:T(8,128)(2,1)S(1)}, bf16[1024,1024]{1,0:T(8,128)(2,1)}, u32[]{:S(2)}) copy-start(bf16[1024,1024]{1,0:T(8,128)(2,1)} %param.17) | copy-start | bytes 6291460
  7.2 24.4 %copy-start.6 = (bf16[1,128,1024]{2,1,0:T(8,128)(2,1)S(1)}, bf16[1,128,1024]{2,1,0:T(8,128)(2,1)}, u32[]{:S(2)}) copy-start(bf16[1,128,1024]{2,1,0:T(8,128)(2,1)} %param.10) | copy-start | bytes 786436
  7.2 24.4 %copy-start.7 = (bf16[1,128,1024]{2,1,0:T(8,128)(2,1)S(1)}, bf16[1,128,1024]{2,1,0:T(8,128)(2,1)}, u32[]{:S(2)}) copy-start(bf16[1,128,1024]{2,1,0:T(8,128)(2,1)} %param.11) | copy-start | bytes 786436
  7.2 24.6 %copy-start.9 = (f32[1024]{0:T(1024)S(1)}, f32[1024]{0:T(1024)}, u32[]{:S(2)}) copy-start(f32[1024]{0:T(1024)} %param.15) | copy-start | bytes 12292
  7.2 75.2 %all-gather.6.cloned.1.call-start = ((), (), s32[]{:S(2)}) async-start(), calls=%async_computation.4 | async-start | bytes 6684672 | tf_op jit(solution)/shard_map/all_gather | solution.py:119
  29.8 92.5 %all-gather.10.cloned.1.call-start = ((), (), s32[]{:S(2)}) async-start(), calls=%async_computation.6 | async-start | bytes 2228224 | tf_op jit(solution)/shard_map/all_gather | solution.py:120
  31.9 3.9 %copy-start.3 = (bf16[1,128,1024]{2,1,0:T(8,128)(2,1)}, bf16[1,128,1024]{2,1,0:T(8,128)(2,1)S(1)}, u32[]{:S(2)}) copy-start(bf16[1,128,1024]{2,1,0:T(8,128)(2,1)S(1)} %multiply_convert_fusion) | copy-start | bytes 786436
  37.0 8.3 %copy-start.8 = (s32[1,2048]{1,0:T(1,128)S(1)}, s32[1,2048]{1,0:T(1,128)}, u32[]{:S(2)}) copy-start(s32[1,2048]{1,0:T(1,128)} %param.13) | copy-start | bytes 24580
  39.2 15.1 %all-to-all-start = ((bf16[1,128,3,16,64]{1,4,2,0,3:T(8,128)(2,1)}), bf16[1,128,3,16,64]{1,4,2,0,3:T(8,128)(2,1)S(1)}, u32[]{:S(2)}, u32[]{:S(2)}) async-start(bf16[1,128,3,16,64]{1,4,2,0,3:T(8,128)(2,1)} %copy.57), calls=%async_computation | async-start | bytes 1572864 | tf_op jit(solution)/shard_map/all_to_all | solution.py:129
  43.8 146.5 %all-gather.8.cloned.1.call-start = ((), (), s32[]{:S(2)}) async-start(), calls=%async_computation.5 | async-start | bytes 4456448 | tf_op jit(solution)/shard_map/all_gather | solution.py:216
  65.8 16.7 %copy-start.4 = (bf16[1,128,1024]{2,1,0:T(8,128)(2,1)S(1)}, bf16[1,128,1024]{2,1,0:T(8,128)(2,1)}, u32[]{:S(2)}) copy-start(bf16[1,128,1024]{2,1,0:T(8,128)(2,1)} %copy-done.3) | copy-start | bytes 786436
  66.5 11.0 %all-to-all-start.1 = ((bf16[1,16,128,1,64]{2,4,3,0,1:T(8,128)(2,1)}), bf16[1,16,128,1,64]{2,4,3,0,1:T(8,128)(2,1)S(1)}, u32[]{:S(2)}, u32[]{:S(2)}) async-start(bf16[1,16,128,1,64]{2,4,3,0,1:T(8,128)(2,1)} %copy.59), calls=%async_computation.1 | async-start | bytes 524288 | tf_op jit(solution)/shard_map/all_to_all | solution.py:133
  87.3 7.3 %collective-permute-start = (bf16[1,64,2048]{2,1,0:T(8,128)(2,1)}, bf16[1,64,2048]{2,1,0:T(8,128)(2,1)}, u32[]{:S(2)}, u32[]{:S(2)}) collective-permute-start(bf16[1,64,2048]{2,1,0:T(8,128)(2,1)} %get-tuple-element.10), channel_id=1, source_target_pairs={{0,1},{1,2},{2,3},{3,4},{4,5},{5,6},{6,7},{7,8},{8,9},{9,10},{10,1... | collective-permute-start | bytes 786440 | tf_op jit(solution)/shard_map/ppermute | solution.py:20
  91.1 7.5 %collective-permute-start.1 = (bf16[1,64,2048]{2,1,0:T(8,128)(2,1)S(1)}, bf16[1,64,2048]{2,1,0:T(8,128)(2,1)}, u32[]{:S(2)}, u32[]{:S(2)}) collective-permute-start(bf16[1,64,2048]{2,1,0:T(8,128)(2,1)S(1)} %get-tuple-element.11), channel_id=1, source_target_pairs={{1,0},{2,1},{3,2},{4,3},{5,4},{6,5},{7,6},{8,7},{9,8},{10,9},{11,1... | collective-permute-start | bytes 786440 | tf_op jit(solution)/shard_map/ppermute | solution.py:23
  104.2 18.1 %copy-start.5 = (f32[128,1024]{1,0:T(8,128)S(1)}, f32[128,1024]{1,0:T(8,128)}, u32[]{:S(2)}) copy-start(f32[128,1024]{1,0:T(8,128)} %convolution_bitcast_fusion) | copy-start | bytes 1572868
  122.3 3.0 %copy-start.1 = (bf16[1,1024,1024]{2,1,0:T(8,128)(2,1)S(1)}, bf16[1,1024,1024]{2,1,0:T(8,128)(2,1)}, u32[]{:S(2)}) copy-start(bf16[1,1024,1024]{2,1,0:T(8,128)(2,1)} %all-gather.10.cloned.1.call-done) | copy-start | bytes 6291460
  133.8 2.4 copy-start.2
  136.2 1.6 copy-start.10
  138.9 15.5 %collective-permute-start.2 = (bf16[1,64,2048]{1,2,0:T(8,128)(2,1)S(1)}, bf16[1,64,2048]{1,2,0:T(8,128)(2,1)S(1)}, u32[]{:S(2)}, u32[]{:S(2)}) collective-permute-start(bf16[1,64,2048]{1,2,0:T(8,128)(2,1)S(1)} %get-tuple-element.6), channel_id=1, source_target_pairs={{0,1},{1,2},{2,3},{3,4},{4,5},{5,6},{6,7},{7,8},{8,9},{9,10},{10,1... | collective-permute-start | bytes 786440 | tf_op jit(solution)/shard_map/ppermute | solution.py:31
  142.0 15.7 %collective-permute-start.3 = (bf16[1,64,2048]{1,2,0:T(8,128)(2,1)S(1)}, bf16[1,64,2048]{1,2,0:T(8,128)(2,1)S(1)}, u32[]{:S(2)}, u32[]{:S(2)}) collective-permute-start(bf16[1,64,2048]{1,2,0:T(8,128)(2,1)S(1)} %get-tuple-element.7), channel_id=1, source_target_pairs={{1,0},{2,1},{3,2},{4,3},{5,4},{6,5},{7,6},{8,7},{9,8},{10,9},{11,1... | collective-permute-start | bytes 786440 | tf_op jit(solution)/shard_map/ppermute | solution.py:31
  159.0 24.0 %all-to-all-start.2 = ((bf16[128,16,2,64]{0,3,2,1:T(8,128)(2,1)}), bf16[128,16,2,64]{0,3,2,1:T(8,128)(2,1)S(1)}, u32[]{:S(2)}, u32[]{:S(2)}) async-start(bf16[128,16,2,64]{0,3,2,1:T(8,128)(2,1)} %copy.61), calls=%async_computation.2 | async-start | bytes 1048576 | tf_op jit(solution)/shard_map/all_to_all | solution.py:212
Sparse Core Ops, SparseCore 0:
  29.9 52.4 all-gather.5
  84.3 38.0 all-gather.9
  124.8 65.5 all-gather.7

commit v8 on v6

--- a/solution.py
+++ b/solution.py
@@ -221,14 +221,20 @@
     block = rows_each * 2 * head_dim
     partial = partial.reshape(dp_count * seq_count, block)
     lane = jnp.arange(2 * head_dim)
-    scalars = jnp.where(lane == 0, square_local, jnp.where(lane == 1, count_local, 0.0))
+    square_high = lax.reduce_precision(square_local, exponent_bits=8, mantissa_bits=7)
+    square_low = square_local - square_high
+    scalars = jnp.where(
+        lane == 0,
+        square_high,
+        jnp.where(lane == 1, square_low, jnp.where(lane == 2, count_local, 0.0)),
+    )
     partial = jnp.concatenate(
         (partial, jnp.broadcast_to(scalars, (dp_count * seq_count, 2 * head_dim))), axis=1
-    )
+    ).astype(jnp.bfloat16)
     mine = lax.all_to_all(partial, ("dp", "seq"), split_axis=0, concat_axis=0, tiled=True)
-    mine = mine.reshape(dp_count, seq_count, block + 2 * head_dim)
+    mine = mine.astype(jnp.float32).reshape(dp_count, seq_count, block + 2 * head_dim)
     totals = mine[:, :, block:].sum((0, 1))
-    square_sum, frame_count = totals[0], totals[1]
+    square_sum, frame_count = totals[0] + totals[1], totals[2]
     mean_error = square_sum / (frame_count * model_width)
     mine = mine[:, :, :block].sum(0) * lax.rsqrt(frame_count)
     mine = mine.reshape(HEADS, rows_each, 2, head_dim).transpose(2, 1, 0, 3)

time: 227 us -> 227 us (level)
  blocking collectives: 54 us -> 49.4 us
  other arithmetic: 7.9 us -> 11.1 us
  between operations: 19 us -> 22.2 us
  waiting for transfers between devices: 68.3 us -> 65.7 us
    all_to_all x1, blocking collectives: 34 us -> 29.5 us  [shards(): lax.all_to_all(partial, ('dp', 'seq'), split_axis=0, concat_axis=0, tiled...]
    concatenate x1 -> x2, other arithmetic: 0.05 us -> 3.23 us  [shards(): jnp.concatenate((partial, jnp.broadcast_to(scalars, (dp_count * seq_count...]
    all_to_all x1, waiting for transfers between devices: 8.73 us -> 6.1 us  [shards(): lax.all_to_all(by_head.astype(jnp.bfloat16), 'seq', split_axis=1, concat_...]
where the time goes in v8:
time: 227 us; the launch traced here: 226 us
  waiting for transfers between devices  65.7 us (29%)
  blocking collectives  49.4 us (22%)
  matrix products  40.7 us (18%)
  starting transfers between devices  23.3 us (10%)
  between operations  22.2 us (10%)
  local copies, waits for them, and re-layouts  13.7 us (6%)
  other arithmetic  11.1 us (5%)
    all_to_all x1, blocking collectives, shards(): lax.all_to_all(partial, ('dp', 'seq'), split_axis=0, concat_axis=0, tiled...  29.5 us
    ppermute x2, waiting for transfers between devices, from_behind(): return lax.ppermute(block, axis, route)  22 us
    all_gather x1, blocking collectives, shards(): lax.all_gather(stacked, 'seq', axis=1, tiled=True)  20 us
    all_gather x1, waiting for transfers between devices, shards(): lax.all_gather(lax.all_gather(stacked, 'seq', axis=1, tiled=True), 'dp',...  15.2 us
    all_to_all x1, waiting for transfers between devices, shards(): lax.all_to_all(teacher_proj, 'seq', split_axis=3, concat_axis=1, tiled=True)  8.89 us
    all_to_all x1, waiting for transfers between devices, shards(): lax.all_to_all(head_out, 'seq', split_axis=1, concat_axis=1, tiled=True)  6.59 us
    sub x1, matrix products, shards(): grad_prob - jnp.sum(probs * grad_prob, axis=-1, keepdims=True)  6.52 us
    all_to_all x1, waiting for transfers between devices, shards(): lax.all_to_all(by_head.astype(jnp.bfloat16), 'seq', split_axis=1, concat_...  6.1 us
  transfers between devices with their start and end apart: 9, of which 8 were waited for; matrix products, arithmetic and copies ran while one was open for 23% of the time, Pallas kernels for 0%

profile of v8, /device:TPU:1, one launch (start us, length us, event | category | flops | bytes accessed | tf_op | source)
XLA Modules:
  0.0 226.2 jit_solution(18138943645666458965)
XLA Ops:
  7.3 0.9 copy.50
  8.2 0.7 copy.51
  8.9 20.0 %all_gather.10 = bf16[4,64,1024]{2,0,1:T(4,128)(2,1)S(1)} all-gather(bf16[4,4,1024]{2,0,1:T(4,128)(2,1)S(1)} %pad_maximum_fusion.3), channel_id=1, replica_groups=mesh['dp'=16,'seq'=16] {'seq'}, dimensions={1}, use_global_device_ids=true | all-gather | bytes 557056 | tf_op jit(solution)/shard_map/all_gather | solution.py:119
  28.9 1.0 copy.52
  30.6 0.2 multiply_reduce_fusion.2
  30.8 0.1 multiply_convert_fusion
  30.9 3.9 %convolution_convert_fusion = bf16[128,3072]{1,0:T(8,128)(2,1)S(1)} fusion(bf16[1024,3072]{1,0:T(8,128)(2,1)} %param.16, bf16[1,128,1024]{2,1,0:T(8,128)(2,1)S(1)} %multiply_convert_fusion), kind=kOutput, calls=%fused_computation.10 | convolution fusion | flops 805699584 | bytes 7340032 | tf_op jit(solution)/shard_map/dot_general | solution.py:127
  34.8 1.2 copy.56
  36.0 2.1 copy.57
  38.2 4.7 %all-to-all-start = ((bf16[1,128,3,16,64]{1,4,2,0,3:T(8,128)(2,1)}), bf16[1,128,3,16,64]{1,4,2,0,3:T(8,128)(2,1)S(1)}, u32[]{:S(2)}, u32[]{:S(2)}) async-start(bf16[1,128,3,16,64]{1,4,2,0,3:T(8,128)(2,1)} %copy.57), calls=%async_computation | async-start | bytes 1572864 | tf_op jit(solution)/shard_map/all_to_all | solution.py:131
  42.9 0.7 all-gather.6.cloned.1.call-update
  44.4 8.9 %all-to-all-done = bf16[1,128,3,16,64]{1,4,2,0,3:T(8,128)(2,1)S(1)} async-done(((bf16[1,128,3,16,64]{1,4,2,0,3:T(8,128)(2,1)}), bf16[1,128,3,16,64]{1,4,2,0,3:T(8,128)(2,1)S(1)}, u32[]{:S(2)}, u32[]{:S(2)}) %all-to-all-start) | async-done | bytes 786464 | tf_op jit(solution)/shard_map/all_to_all | solution.py:131
  53.3 0.1 copy_bitcast_fusion
  53.4 2.6 %fusion.2 = (f32[2048]{0:T(1024)S(1)}, f32[2048,2048]{0,1:T(8,128)S(1)}) fusion(f32[2048]{0:T(1024)S(1)} %fusion.56, bf16[1,2048,3,1,64]{1,4,2,3,0:T(8,128)(2,1)S(1)} %copy_bitcast_fusion), kind=kOutput, calls=%fused_computation.5 | convolution fusion | flops 549451776 | bytes 17317888 | tf_op jit(solution)/shard_map/vmap(vmap())/dot_general | solution.py:45
  56.1 4.6 %fusion.3 = f32[2048]{0:T(1024)S(1)} fusion(f32[2048,2048]{0,1:T(8,128)S(1)} %get-tuple-element.16, f32[2048]{0:T(1024)S(1)} %get-tuple-element.15, f32[2048]{0:T(1024)S(1)} %fusion.56), kind=kLoop, calls=%fused_computation.6 | loop fusion | flops 16775168 | bytes 16801792 | tf_op jit(solution)/shard_map/vmap(vmap())/reduce_sum | solution.py:51
  60.6 4.1 %fusion.27 = bf16[8,8,16,128]{3,1,2,0:T(8,128)(2,1)S(1)} fusion(f32[2048,2048]{0,1:T(8,128)S(1)} %get-tuple-element.16, f32[2048]{0:T(1024)S(1)} %fusion.3, f32[2048]{0:T(1024)S(1)} %get-tuple-element.15, f32[2048]{0:T(1024)S(1)} %fusion.56, bf16[1,2048,3,1,64]{1,4,2,3,0:T(8,128)(2,1)S(1)} %copy_bitcast_fusion), kind=kOutput, calls=%fused_computation.42 | convolution fusion | flops 557973504 | bytes 17326080 | tf_op jit(solution)/shard_map/vmap(vmap())/dot_general | solution.py:52
  64.8 0.8 copy.59
  65.6 3.7 %all-to-all-start.1 = ((bf16[1,16,128,1,64]{2,4,3,0,1:T(8,128)(2,1)}), bf16[1,16,128,1,64]{2,4,3,0,1:T(8,128)(2,1)S(1)}, u32[]{:S(2)}, u32[]{:S(2)}) async-start(bf16[1,16,128,1,64]{2,4,3,0,1:T(8,128)(2,1)} %copy.59), calls=%async_computation.1 | async-start | bytes 524288 | tf_op jit(solution)/shard_map/all_to_all | solution.py:135
  69.3 0.6 convert_reduce_fusion
  69.9 0.1 or_and_fusion
  70.0 6.6 %all-to-all-done.1 = bf16[1,16,128,1,64]{2,4,3,0,1:T(8,128)(2,1)S(1)} async-done(((bf16[1,16,128,1,64]{2,4,3,0,1:T(8,128)(2,1)}), bf16[1,16,128,1,64]{2,4,3,0,1:T(8,128)(2,1)S(1)}, u32[]{:S(2)}, u32[]{:S(2)}) %all-to-all-start.1) | async-done | bytes 262176 | tf_op jit(solution)/shard_map/all_to_all | solution.py:135
  76.6 0.5 convolution_bitcast_fusion
  77.1 15.2 %all-gather.4.cloned.1.call-done = bf16[4,1024,1024]{2,1,0:T(8,128)(2,1)} async-done(((bf16[4,64,1024]{2,1,0:T(8,128)(2,1)}), bf16[4,1024,1024]{2,1,0:T(8,128)(2,1)}) %all-gather.4.cloned.1.call-update) | async-done | bytes 8388624 | tf_op jit(solution)/shard_map/all_gather | solution.py:118
  92.3 2.0 fusion.22
  94.3 2.0 fusion.23
  96.5 3.1 %collective-permute-start = (bf16[1,64,2048]{2,1,0:T(8,128)(2,1)S(1)}, bf16[1,64,2048]{2,1,0:T(8,128)(2,1)S(1)}, u32[]{:S(2)}, u32[]{:S(2)}) collective-permute-start(bf16[1,64,2048]{2,1,0:T(8,128)(2,1)S(1)} %get-tuple-element.10), channel_id=1, source_target_pairs={{0,1},{1,2},{2,3},{3,4},{4,5},{5,6},{6,7},{7,8},{8,9},{9,10},{10,1... | collective-permute-start | bytes 786440 | tf_op jit(solution)/shard_map/ppermute | solution.py:20
  99.6 1.3 collective-permute-start.1
  100.9 2.0 fusion.21
  102.9 0.2 copy.53
  103.1 1.8 collective-permute-done
  105.0 4.3 %collective-permute-done.1 = bf16[1,64,2048]{2,1,0:T(8,128)(2,1)S(1)} collective-permute-done((bf16[1,64,2048]{2,1,0:T(8,128)(2,1)S(1)}, bf16[1,64,2048]{2,1,0:T(8,128)(2,1)S(1)}, u32[]{:S(2)}, u32[]{:S(2)}) %collective-permute-start.1) | collective-permute-done | bytes 262176 | tf_op jit(solution)/shard_map/ppermute | solution.py:23
  109.4 0.2 copy.54
  109.7 0.2 copy.55
  109.9 2.1 fusion.65
  111.9 2.2 convolution_convert_fusion.1
  114.1 2.8 %multiply_reduce_fusion.1 = (f32[]{:T(128)}, bf16[128,1024]{1,0:T(8,128)(2,1)S(1)}) fusion(f32[128,1024]{1,0:T(8,128)S(1)} %convolution_bitcast_fusion, bf16[128,1024]{0,1:T(8,128)(2,1)S(1)} %bitcast.171, bf16[4,1024,1024]{2,1,0:T(8,128)(2,1)} %all-gather.4.cloned.1.call-done, pred[128]{0:T(512)(128)(4,1)S(1)} %get-tuple-element.3), kind=kOutput, calls=%fused_computation.60 | convolution fusion | flops 269090816 | bytes 3145860 | tf_op jit(solution)/shard_map/dot_general | solution.py:176
  116.9 2.4 %fusion.20 = bf16[128,1024]{1,0:T(8,128)(2,1)S(1)} fusion(bf16[4,1024,1024]{2,1,0:T(8,128)(2,1)} %all-gather.4.cloned.1.call-done, bf16[128,1024]{1,0:T(8,128)(2,1)S(1)} %get-tuple-element.20), kind=kOutput, calls=%fused_computation.36 | convolution fusion | flops 268566528 | bytes 2621440 | tf_op jit(solution)/shard_map/dot_general | solution.py:182
  119.3 0.2 copy.60
  119.5 6.5 %multiply_bitcast_fusion = f32[1,16,128,256]{3,2,1,0:T(8,128)S(1)} fusion(bf16[128,16,64]{0,2,1:T(8,128)(2,1)S(1)} %bitcast.166, bf16[256,16,64]{0,2,1:T(8,128)(2,1)S(1)} %bitcast.163, f32[16,128,256]{2,1,0:T(8,128)} %get-tuple-element.18, f32[16,128]{1,0:T(8,128)S(1)} %get-tuple-element.17), kind=kOutput, calls=%fused_computation.24 | convolution fusion | flops 137365760 | bytes 4988928 | tf_op jit(solution)/shard_map/sub | solution.py:189
  126.0 1.3 copy-done.2
  127.3 0.3 fusion.33
  127.6 3.1 %convolution_add_fusion = f32[16,64,256]{2,1,0:T(8,128)S(1)} fusion(f32[16,64,256]{2,1,0:T(8,128)S(1)} %fusion.33, bf16[128,16,64]{0,2,1:T(8,128)(2,1)S(1)} %bitcast.158, f32[1,16,128,256]{3,2,1,0:T(8,128)} %copy-done.2), kind=kOutput, calls=%fused_computation.32 | convolution fusion | flops 69468160 | bytes 4456448 | tf_op jit(solution)/shard_map/bhrw,brhd->bwhd/dot_general | solution.py:90
  130.8 0.8 fusion.42
  131.7 0.2 fusion.61
  132.0 3.1 %collective-permute-start.2 = (bf16[1,64,2048]{1,2,0:T(8,128)(2,1)S(1)}, bf16[1,64,2048]{1,2,0:T(8,128)(2,1)S(1)}, u32[]{:S(2)}, u32[]{:S(2)}) collective-permute-start(bf16[1,64,2048]{1,2,0:T(8,128)(2,1)S(1)} %get-tuple-element.6), channel_id=1, source_target_pairs={{0,1},{1,2},{2,3},{3,4},{4,5},{5,6},{6,7},{7,8},{8,9},{9,10},{10,1... | collective-permute-start | bytes 786440 | tf_op jit(solution)/shard_map/ppermute | solution.py:31
  135.1 1.3 collective-permute-start.3
  136.4 19.9 %collective-permute-done.2 = bf16[1,64,2048]{1,2,0:T(8,128)(2,1)S(1)} collective-permute-done((bf16[1,64,2048]{1,2,0:T(8,128)(2,1)S(1)}, bf16[1,64,2048]{1,2,0:T(8,128)(2,1)S(1)}, u32[]{:S(2)}, u32[]{:S(2)}) %collective-permute-start.2) | collective-permute-done | bytes 262176 | tf_op jit(solution)/shard_map/ppermute | solution.py:31
  156.3 2.1 collective-permute-done.3
  158.4 0.5 fusion.32
  158.9 0.8 copy.61
  159.7 6.1 %all-to-all-start.2 = ((bf16[128,16,2,64]{0,3,2,1:T(8,128)(2,1)}), bf16[128,16,2,64]{0,3,2,1:T(8,128)(2,1)S(1)}, u32[]{:S(2)}, u32[]{:S(2)}) async-start(bf16[128,16,2,64]{0,3,2,1:T(8,128)(2,1)} %copy.61), calls=%async_computation.2 | async-start | bytes 1048576 | tf_op jit(solution)/shard_map/all_to_all | solution.py:214
  168.4 1.3 fusion.57
  169.7 6.1 %all-to-all-done.2 = bf16[128,16,2,64]{0,3,2,1:T(8,128)(2,1)S(1)} async-done(((bf16[128,16,2,64]{0,3,2,1:T(8,128)(2,1)}), bf16[128,16,2,64]{0,3,2,1:T(8,128)(2,1)S(1)}, u32[]{:S(2)}, u32[]{:S(2)}) %all-to-all-start.2) | async-done | bytes 524320 | tf_op jit(solution)/shard_map/all_to_all | solution.py:214
  175.8 0.3 copy.62
  176.2 3.5 %fusion.24 = bf16[1024,128]{1,0:T(8,128)(2,1)S(1)} fusion(bf16[1,2048,1024]{2,1,0:T(8,128)(2,1)} %all-gather.6.cloned.1.call-done, bf16[16,8,16,128]{3,2,1,0:T(8,128)(2,1)S(1)} %bitcast.165), kind=kOutput, calls=%fused_computation.41 | convolution fusion | flops 537001984 | bytes 4980736 | tf_op jit(solution)/shard_map/dot_general | solution.py:219
  179.7 0.1 concatenate.39
  179.8 0.6 pad_maximum_fusion.2
  180.5 0.5 broadcast.240
  181.0 2.6 %reduce.11 = bf16[256,640]{1,0:T(8,128)(2,1)S(1)} reduce(bf16[256,1,640]{2,1,0:T(2,128)(2,1)S(1)} %pad_maximum_fusion.2, bf16[]{:T(256)} %broadcast.240), dimensions={1}, to_apply=%pad_maximum_fusion.2.reduce_sub_computation | reduce | bytes 655362 | tf_op jit(solution)/shard_map/concatenate | solution.py:231
  183.6 0.3 reshape.437
  183.9 29.5 %all_to_all.44 = bf16[256,2,320]{2,1,0:T(2,128)(2,1)S(1)} all-to-all(bf16[256,2,320]{2,1,0:T(2,128)(2,1)S(1)} %reshape.437), channel_id=1, replica_groups=mesh['dp'=16,'seq'=16] {'dp','seq'}, dimensions={0} | all-to-all | bytes 655360 | tf_op jit(solution)/shard_map/all_to_all | solution.py:234
  213.4 0.6 reshape.438
  214.1 0.6 fusion.64
  216.2 0.7 reshape.432
  (45 shorter events, 1.1 us)
Async XLA Ops:
  7.2 69.5 %copy-start = (bf16[1024,1024]{1,0:T(8,128)(2,1)S(1)}, bf16[1024,1024]{1,0:T(8,128)(2,1)}, u32[]{:S(2)}) copy-start(bf16[1024,1024]{1,0:T(8,128)(2,1)} %param.17) | copy-start | bytes 6291460
  7.2 23.4 %copy-start.5 = (bf16[1,128,1024]{2,1,0:T(8,128)(2,1)S(1)}, bf16[1,128,1024]{2,1,0:T(8,128)(2,1)}, u32[]{:S(2)}) copy-start(bf16[1,128,1024]{2,1,0:T(8,128)(2,1)} %param.10) | copy-start | bytes 786436
  7.2 23.4 %copy-start.6 = (bf16[1,128,1024]{2,1,0:T(8,128)(2,1)S(1)}, bf16[1,128,1024]{2,1,0:T(8,128)(2,1)}, u32[]{:S(2)}) copy-start(bf16[1,128,1024]{2,1,0:T(8,128)(2,1)} %param.11) | copy-start | bytes 786436
  7.2 23.6 %copy-start.8 = (f32[1024]{0:T(1024)S(1)}, f32[1024]{0:T(1024)}, u32[]{:S(2)}) copy-start(f32[1024]{0:T(1024)} %param.15) | copy-start | bytes 12292
  7.2 85.1 %all-gather.4.cloned.1.call-start = ((), (), s32[]{:S(2)}) async-start(), calls=%async_computation.4 | async-start | bytes 8912896 | tf_op jit(solution)/shard_map/all_gather | solution.py:118
  30.9 3.9 %copy-start.3 = (bf16[1,128,1024]{2,1,0:T(8,128)(2,1)}, bf16[1,128,1024]{2,1,0:T(8,128)(2,1)S(1)}, u32[]{:S(2)}) copy-start(bf16[1,128,1024]{2,1,0:T(8,128)(2,1)S(1)} %multiply_convert_fusion) | copy-start | bytes 786436
  36.0 8.3 %copy-start.7 = (s32[1,2048]{1,0:T(1,128)S(1)}, s32[1,2048]{1,0:T(1,128)}, u32[]{:S(2)}) copy-start(s32[1,2048]{1,0:T(1,128)} %param.13) | copy-start | bytes 24580
  38.2 15.1 %all-to-all-start = ((bf16[1,128,3,16,64]{1,4,2,0,3:T(8,128)(2,1)}), bf16[1,128,3,16,64]{1,4,2,0,3:T(8,128)(2,1)S(1)}, u32[]{:S(2)}, u32[]{:S(2)}) async-start(bf16[1,128,3,16,64]{1,4,2,0,3:T(8,128)(2,1)} %copy.57), calls=%async_computation | async-start | bytes 1572864 | tf_op jit(solution)/shard_map/all_to_all | solution.py:131
  42.9 133.3 %all-gather.6.cloned.1.call-start = ((), (), s32[]{:S(2)}) async-start(), calls=%async_computation.5 | async-start | bytes 4456448 | tf_op jit(solution)/shard_map/all_gather | solution.py:218
  64.8 27.5 %copy-start.4 = (bf16[1,128,1024]{2,1,0:T(8,128)(2,1)S(1)}, bf16[1,128,1024]{2,1,0:T(8,128)(2,1)}, u32[]{:S(2)}) copy-start(bf16[1,128,1024]{2,1,0:T(8,128)(2,1)} %copy-done.3) | copy-start | bytes 786436
  65.6 11.0 %all-to-all-start.1 = ((bf16[1,16,128,1,64]{2,4,3,0,1:T(8,128)(2,1)}), bf16[1,16,128,1,64]{2,4,3,0,1:T(8,128)(2,1)S(1)}, u32[]{:S(2)}, u32[]{:S(2)}) async-start(bf16[1,16,128,1,64]{2,4,3,0,1:T(8,128)(2,1)} %copy.59), calls=%async_computation.1 | async-start | bytes 524288 | tf_op jit(solution)/shard_map/all_to_all | solution.py:135
  96.5 8.5 %collective-permute-start = (bf16[1,64,2048]{2,1,0:T(8,128)(2,1)S(1)}, bf16[1,64,2048]{2,1,0:T(8,128)(2,1)S(1)}, u32[]{:S(2)}, u32[]{:S(2)}) collective-permute-start(bf16[1,64,2048]{2,1,0:T(8,128)(2,1)S(1)} %get-tuple-element.10), channel_id=1, source_target_pairs={{0,1},{1,2},{2,3},{3,4},{4,5},{5,6},{6,7},{7,8},{8,9},{9,10},{10,1... | collective-permute-start | bytes 786440 | tf_op jit(solution)/shard_map/ppermute | solution.py:20
  99.6 9.7 %collective-permute-start.1 = (bf16[1,64,2048]{2,1,0:T(8,128)(2,1)S(1)}, bf16[1,64,2048]{2,1,0:T(8,128)(2,1)S(1)}, u32[]{:S(2)}, u32[]{:S(2)}) collective-permute-start(bf16[1,64,2048]{2,1,0:T(8,128)(2,1)S(1)} %get-tuple-element.11), channel_id=1, source_target_pairs={{1,0},{2,1},{3,2},{4,3},{5,4},{6,5},{7,6},{8,7},{9,8},{10,9},{11,1... | collective-permute-start | bytes 786440 | tf_op jit(solution)/shard_map/ppermute | solution.py:23
  126.0 1.3 copy-start.2
  127.6 3.2 %copy-start.9 = (f32[16,128,256]{2,1,0:T(8,128)S(1)}, f32[16,128,256]{2,1,0:T(8,128)}, u32[]{:S(2)}) copy-start(f32[16,128,256]{2,1,0:T(8,128)} %get-tuple-element.18) | copy-start | bytes 6291460
  132.0 24.3 %collective-permute-start.2 = (bf16[1,64,2048]{1,2,0:T(8,128)(2,1)S(1)}, bf16[1,64,2048]{1,2,0:T(8,128)(2,1)S(1)}, u32[]{:S(2)}, u32[]{:S(2)}) collective-permute-start(bf16[1,64,2048]{1,2,0:T(8,128)(2,1)S(1)} %get-tuple-element.6), channel_id=1, source_target_pairs={{0,1},{1,2},{2,3},{3,4},{4,5},{5,6},{6,7},{7,8},{8,9},{9,10},{10,1... | collective-permute-start | bytes 786440 | tf_op jit(solution)/shard_map/ppermute | solution.py:31
  135.1 23.3 %collective-permute-start.3 = (bf16[1,64,2048]{1,2,0:T(8,128)(2,1)S(1)}, bf16[1,64,2048]{1,2,0:T(8,128)(2,1)S(1)}, u32[]{:S(2)}, u32[]{:S(2)}) collective-permute-start(bf16[1,64,2048]{1,2,0:T(8,128)(2,1)S(1)} %get-tuple-element.7), channel_id=1, source_target_pairs={{1,0},{2,1},{3,2},{4,3},{5,4},{6,5},{7,6},{8,7},{9,8},{10,9},{11,1... | collective-permute-start | bytes 786440 | tf_op jit(solution)/shard_map/ppermute | solution.py:31
  159.7 16.1 %all-to-all-start.2 = ((bf16[128,16,2,64]{0,3,2,1:T(8,128)(2,1)}), bf16[128,16,2,64]{0,3,2,1:T(8,128)(2,1)S(1)}, u32[]{:S(2)}, u32[]{:S(2)}) async-start(bf16[128,16,2,64]{0,3,2,1:T(8,128)(2,1)} %copy.61), calls=%async_computation.2 | async-start | bytes 1048576 | tf_op jit(solution)/shard_map/all_to_all | solution.py:214
  183.6 34.7 %copy-start.1 = (bf16[1024,1024]{1,0:T(8,128)(2,1)S(1)}, bf16[1024,1024]{1,0:T(8,128)(2,1)}, u32[]{:S(2)}) copy-start(bf16[1024,1024]{1,0:T(8,128)(2,1)} %param.17) | copy-start | bytes 6291460
Sparse Core Ops, SparseCore 0:
  30.0 62.2 all-gather.3
  94.7 61.6 all-gather.5

commit v9 on v6

--- a/solution.py
+++ b/solution.py
@@ -199,22 +199,22 @@
         ),
         axis=-1,
     )
-    from_next = from_behind(grad_both[:, :HALO].astype(jnp.bfloat16), "seq", -1).astype(jnp.float32)
-    from_prev = from_behind(
-        grad_both[:, HALO + shard_rows :].astype(jnp.bfloat16), "seq", 1
-    ).astype(jnp.float32)
-    owned_rows = grad_both[:, HALO : HALO + shard_rows]
+    by_head = grad_both.reshape(window, 2, HEADS, head_dim).transpose(0, 2, 1, 3)
+    windows = lax.all_to_all(
+        by_head.astype(jnp.bfloat16), "seq", split_axis=1, concat_axis=0, tiled=True
+    )
+    windows = windows.reshape(seq_count, window, 2 * head_dim).astype(jnp.float32)
+    blank = jnp.zeros((1, HALO, 2 * head_dim), jnp.float32)
+    from_prev = jnp.concatenate((blank, windows[:-1, HALO + shard_rows :]), axis=0)
+    from_next = jnp.concatenate((windows[1:, :HALO], blank), axis=0)
+    owned_rows = windows[:, HALO : HALO + shard_rows]
     if shard_rows >= 2 * HALO:
-        middle = jnp.zeros((dialogs, shard_rows - 2 * HALO, 2 * model_width), jnp.float32)
+        middle = jnp.zeros((seq_count, shard_rows - 2 * HALO, 2 * head_dim), jnp.float32)
         owned_rows = owned_rows + jnp.concatenate((from_prev, middle, from_next), axis=1)
     else:
         owned_rows = owned_rows.at[:, :HALO].add(from_prev)
         owned_rows = owned_rows.at[:, shard_rows - HALO :].add(from_next)
-    by_head = owned_rows.reshape(shard_rows, 2, HEADS, head_dim).transpose(0, 2, 1, 3)
-    head_grads = lax.all_to_all(
-        by_head.astype(jnp.bfloat16), "seq", split_axis=1, concat_axis=0, tiled=True
-    )
-    head_grads = head_grads.reshape(frames, 2 * head_dim)
+    head_grads = owned_rows.reshape(frames, 2 * head_dim).astype(jnp.bfloat16)
     normed_all = lax.all_gather(flat_rows, "seq", axis=0, tiled=True)
     partial = jnp.dot(normed_all.T, head_grads, preferred_element_type=jnp.float32)
     dp_count = lax.axis_size("dp")

time: 227 us -> 213 us (0.938)
  waiting for transfers between devices: 68.3 us -> 56.6 us
  matrix products: 40.7 us -> 37.7 us
    ppermute x2 -> x0, waiting for transfers between devices: 22 us -> none  [from_behind(): return lax.ppermute(block, axis, route)]
    all_to_all x1, waiting for transfers between devices: 8.73 us -> 21.9 us  [shards(): lax.all_to_all(by_head.astype(jnp.bfloat16), 'seq', split_axis=1, concat_...]
    all_to_all x1, starting transfers between devices: 6.06 us -> 11.3 us  [shards(): lax.all_to_all(by_head.astype(jnp.bfloat16), 'seq', split_axis=1, concat_...]
    ppermute x2 -> x0, starting transfers between devices: 4.39 us -> none  [from_behind(): return lax.ppermute(block, axis, route)]
    dot_general x1, matrix products: 3.09 us -> 0.3 us  [split_product(): jnp.einsum(form, lower_part, other, preferred_element_type=jnp.float32)]
    ppermute x1, waiting for transfers between devices: 4.3 us -> 1.95 us  [with_halo(): lax.ppermute(lax.slice_in_dim(block, 0, width, axis=dim), axis, backward)]
  transfers between devices with their start and end apart: 9 -> 7, of which waited for: 8 -> 6; matrix products, arithmetic and copies ran while one was open for 23% -> 23% of each run, Pallas kernels for 0% -> 0%
where the time goes in v9:
time: 213 us; the launch traced here: 212 us
  waiting for transfers between devices  56.6 us (27%)
  blocking collectives  52.9 us (25%)
  matrix products  37.7 us (18%)
  starting transfers between devices  25 us (12%)
  between operations  18.9 us (9%)
  local copies, waits for them, and re-layouts  12.9 us (6%)
  other arithmetic  8.25 us (4%)
    all_to_all x1, blocking collectives, shards(): lax.all_to_all(partial, ('dp', 'seq'), split_axis=0, concat_axis=0, tiled...  33 us
    all_to_all x1, waiting for transfers between devices, shards(): lax.all_to_all(by_head.astype(jnp.bfloat16), 'seq', split_axis=1, concat_...  21.9 us
    all_gather x1, blocking collectives, shards(): lax.all_gather(stacked, 'seq', axis=1, tiled=True)  20 us
    all_gather x1, waiting for transfers between devices, shards(): lax.all_gather(lax.all_gather(stacked, 'seq', axis=1, tiled=True), 'dp',...  15.2 us
    all_to_all x1, starting transfers between devices, shards(): lax.all_to_all(by_head.astype(jnp.bfloat16), 'seq', split_axis=1, concat_...  11.3 us
    all_to_all x1, waiting for transfers between devices, shards(): lax.all_to_all(teacher_proj, 'seq', split_axis=3, concat_axis=1, tiled=True)  8.91 us
    all_to_all x1, waiting for transfers between devices, shards(): lax.all_to_all(head_out, 'seq', split_axis=1, concat_axis=1, tiled=True)  6.6 us
    sub x1, matrix products, shards(): grad_prob - jnp.sum(probs * grad_prob, axis=-1, keepdims=True)  6.52 us
  transfers between devices with their start and end apart: 7, of which 6 were waited for; matrix products, arithmetic and copies ran while one was open for 23% of the time, Pallas kernels for 0%

profile of v9, /device:TPU:1, one launch (start us, length us, event | category | flops | bytes accessed | tf_op | source)
XLA Modules:
  0.0 212.3 jit_solution(12851981751122977476)
XLA Ops:
  7.3 0.9 copy.51
  8.1 0.8 copy.50
  8.9 20.0 %all_gather.10 = bf16[4,64,1024]{2,0,1:T(4,128)(2,1)S(1)} all-gather(bf16[4,4,1024]{2,0,1:T(4,128)(2,1)S(1)} %pad_maximum_fusion.3), channel_id=1, replica_groups=mesh['dp'=16,'seq'=16] {'seq'}, dimensions={1}, use_global_device_ids=true | all-gather | bytes 557056 | tf_op jit(solution)/shard_map/all_gather | solution.py:119
  28.9 1.0 copy.52
  30.6 0.2 multiply_reduce_fusion.2
  30.8 0.1 multiply_convert_fusion
  30.9 3.9 %convolution_convert_fusion = bf16[128,3072]{1,0:T(8,128)(2,1)S(1)} fusion(bf16[1024,3072]{1,0:T(8,128)(2,1)} %param.16, bf16[1,128,1024]{2,1,0:T(8,128)(2,1)S(1)} %multiply_convert_fusion), kind=kOutput, calls=%fused_computation.10 | convolution fusion | flops 805699584 | bytes 7340032 | tf_op jit(solution)/shard_map/dot_general | solution.py:127
  34.8 1.2 copy.56
  36.0 2.1 %copy.57 = bf16[1,128,3,16,64]{1,4,2,0,3:T(8,128)(2,1)} copy(bf16[1,128,3,16,64]{1,4,3,2,0:T(8,128)(2,1)} %bitcast.148) | data formatting | bytes 1572864 | tf_op jit(solution)/shard_map/reshape | solution.py:130
  38.2 4.7 %all-to-all-start = ((bf16[1,128,3,16,64]{1,4,2,0,3:T(8,128)(2,1)}), bf16[1,128,3,16,64]{1,4,2,0,3:T(8,128)(2,1)S(1)}, u32[]{:S(2)}, u32[]{:S(2)}) async-start(bf16[1,128,3,16,64]{1,4,2,0,3:T(8,128)(2,1)} %copy.57), calls=%async_computation | async-start | bytes 1572864 | tf_op jit(solution)/shard_map/all_to_all | solution.py:131
  42.9 0.7 all-gather.6.cloned.1.call-update
  44.3 0.1 pad_dynamic-slice_fusion
  44.4 8.9 %all-to-all-done = bf16[1,128,3,16,64]{1,4,2,0,3:T(8,128)(2,1)S(1)} async-done(((bf16[1,128,3,16,64]{1,4,2,0,3:T(8,128)(2,1)}), bf16[1,128,3,16,64]{1,4,2,0,3:T(8,128)(2,1)S(1)}, u32[]{:S(2)}, u32[]{:S(2)}) %all-to-all-start) | async-done | bytes 786464 | tf_op jit(solution)/shard_map/all_to_all | solution.py:131
  53.3 0.1 copy_bitcast_fusion
  53.4 2.6 %fusion.2 = (f32[2048]{0:T(1024)S(1)}, f32[2048,2048]{0,1:T(8,128)S(1)}) fusion(f32[2048]{0:T(1024)S(1)} %fusion.49, bf16[1,2048,3,1,64]{1,4,2,3,0:T(8,128)(2,1)S(1)} %copy_bitcast_fusion), kind=kOutput, calls=%fused_computation.5 | convolution fusion | flops 549451776 | bytes 17317888 | tf_op jit(solution)/shard_map/vmap(vmap())/dot_general | solution.py:45
  56.1 4.6 %fusion.3 = f32[2048]{0:T(1024)S(1)} fusion(f32[2048,2048]{0,1:T(8,128)S(1)} %get-tuple-element.15, f32[2048]{0:T(1024)S(1)} %get-tuple-element.14, f32[2048]{0:T(1024)S(1)} %fusion.49), kind=kLoop, calls=%fused_computation.6 | loop fusion | flops 16775168 | bytes 16801792 | tf_op jit(solution)/shard_map/vmap(vmap())/reduce_sum | solution.py:51
  60.6 4.1 %fusion.24 = bf16[8,8,16,128]{3,1,2,0:T(8,128)(2,1)S(1)} fusion(f32[2048,2048]{0,1:T(8,128)S(1)} %get-tuple-element.15, f32[2048]{0:T(1024)S(1)} %fusion.3, f32[2048]{0:T(1024)S(1)} %get-tuple-element.14, f32[2048]{0:T(1024)S(1)} %fusion.49, bf16[1,2048,3,1,64]{1,4,2,3,0:T(8,128)(2,1)S(1)} %copy_bitcast_fusion), kind=kOutput, calls=%fused_computation.39 | convolution fusion | flops 557973504 | bytes 17326080 | tf_op jit(solution)/shard_map/vmap(vmap())/dot_general | solution.py:52
  64.8 0.8 copy.59
  65.6 3.7 %all-to-all-start.1 = ((bf16[1,16,128,1,64]{2,4,3,0,1:T(8,128)(2,1)}), bf16[1,16,128,1,64]{2,4,3,0,1:T(8,128)(2,1)S(1)}, u32[]{:S(2)}, u32[]{:S(2)}) async-start(bf16[1,16,128,1,64]{2,4,3,0,1:T(8,128)(2,1)} %copy.59), calls=%async_computation.1 | async-start | bytes 524288 | tf_op jit(solution)/shard_map/all_to_all | solution.py:135
  69.3 0.6 convert_reduce_fusion
  69.9 0.1 or_and_fusion
  70.0 6.6 %all-to-all-done.1 = bf16[1,16,128,1,64]{2,4,3,0,1:T(8,128)(2,1)S(1)} async-done(((bf16[1,16,128,1,64]{2,4,3,0,1:T(8,128)(2,1)}), bf16[1,16,128,1,64]{2,4,3,0,1:T(8,128)(2,1)S(1)}, u32[]{:S(2)}, u32[]{:S(2)}) %all-to-all-start.1) | async-done | bytes 262176 | tf_op jit(solution)/shard_map/all_to_all | solution.py:135
  76.6 0.5 convolution_bitcast_fusion
  77.1 15.2 %all-gather.4.cloned.1.call-done = bf16[4,1024,1024]{2,1,0:T(8,128)(2,1)} async-done(((bf16[4,64,1024]{2,1,0:T(8,128)(2,1)}), bf16[4,1024,1024]{2,1,0:T(8,128)(2,1)}) %all-gather.4.cloned.1.call-update) | async-done | bytes 8388624 | tf_op jit(solution)/shard_map/all_gather | solution.py:118
  92.3 2.0 fusion.23
  94.4 2.0 fusion.22
  96.5 1.3 collective-permute-start.1
  97.8 4.0 %collective-permute-start = (bf16[1,64,2048]{2,1,0:T(8,128)(2,1)S(1)}, bf16[1,64,2048]{2,1,0:T(8,128)(2,1)S(1)}, u32[]{:S(2)}, u32[]{:S(2)}) collective-permute-start(bf16[1,64,2048]{2,1,0:T(8,128)(2,1)S(1)} %get-tuple-element.10), channel_id=1, source_target_pairs={{0,1},{1,2},{2,3},{3,4},{4,5},{5,6},{6,7},{7,8},{8,9},{9,10},{10,1... | collective-permute-start | bytes 786440 | tf_op jit(solution)/shard_map/ppermute | solution.py:20
  101.8 2.0 fusion.21
  103.9 0.2 copy.53
  104.1 2.0 collective-permute-done.1
  106.0 1.3 collective-permute-done
  107.3 0.1 pad_maximum_fusion
  107.4 0.1 fusion.54
  107.5 0.2 copy.55
  107.7 0.2 copy.54
  107.9 2.1 fusion.57
  109.9 2.2 %convolution_convert_fusion.2 = bf16[16,64,128]{2,1,0:T(8,128)(2,1)S(1)} fusion(bf16[256,16,64]{0,2,1:T(8,128)(2,1)S(1)} %bitcast.157, f32[16,128,256]{2,1,0:T(8,128)} %get-tuple-element.17, f32[16,128]{1,0:T(8,128)S(1)} %get-tuple-element.16), kind=kOutput, calls=%fused_computation.38 | convolution fusion | flops 68288512 | bytes 2891776 | tf_op jit(solution)/shard_map/bhrw,bwhd->brhd/dot_general | solution.py:172
  112.1 2.8 %multiply_reduce_fusion.1 = (f32[]{:T(128)}, bf16[128,1024]{1,0:T(8,128)(2,1)S(1)}) fusion(f32[128,1024]{1,0:T(8,128)S(1)} %convolution_bitcast_fusion, bf16[128,1024]{0,1:T(8,128)(2,1)S(1)} %bitcast.166, bf16[4,1024,1024]{2,1,0:T(8,128)(2,1)} %all-gather.4.cloned.1.call-done, pred[128]{0:T(512)(128)(4,1)S(1)} %get-tuple-element.3), kind=kOutput, calls=%fused_computation.59 | convolution fusion | flops 269090816 | bytes 3145860 | tf_op jit(solution)/shard_map/dot_general | solution.py:176
  114.9 2.4 %fusion.20 = bf16[128,1024]{1,0:T(8,128)(2,1)S(1)} fusion(bf16[4,1024,1024]{2,1,0:T(8,128)(2,1)} %all-gather.4.cloned.1.call-done, bf16[128,1024]{1,0:T(8,128)(2,1)S(1)} %get-tuple-element.19), kind=kOutput, calls=%fused_computation.34 | convolution fusion | flops 268566528 | bytes 2621440 | tf_op jit(solution)/shard_map/dot_general | solution.py:182
  117.3 0.2 copy.60
  117.5 6.5 %multiply_bitcast_fusion = f32[1,16,128,256]{3,2,1,0:T(8,128)S(1)} fusion(bf16[128,16,64]{0,2,1:T(8,128)(2,1)S(1)} %bitcast.161, bf16[256,16,64]{0,2,1:T(8,128)(2,1)S(1)} %bitcast.158, f32[16,128,256]{2,1,0:T(8,128)} %get-tuple-element.17, f32[16,128]{1,0:T(8,128)S(1)} %get-tuple-element.16), kind=kOutput, calls=%fused_computation.20 | convolution fusion | flops 137365760 | bytes 4988928 | tf_op jit(solution)/shard_map/sub | solution.py:189
  124.0 0.3 fusion.29
  124.3 0.3 fusion.17
  124.6 1.3 copy-done.8
  125.9 0.6 convolution_convert_fusion.1
  126.5 0.1 pad_maximum_fusion.1
  126.5 1.1 copy.61
  127.6 11.3 %all-to-all-start.2 = ((bf16[256,16,2,64]{0,3,2,1:T(8,128)(2,1)}), bf16[256,16,2,64]{0,3,2,1:T(8,128)(2,1)S(1)}, u32[]{:S(2)}, u32[]{:S(2)}) async-start(bf16[256,16,2,64]{0,3,2,1:T(8,128)(2,1)} %copy.61), calls=%async_computation.2 | async-start | bytes 2097152 | tf_op jit(solution)/shard_map/all_to_all | solution.py:203
  138.9 1.3 compare_select_fusion.1
  140.2 21.9 %all-to-all-done.2 = bf16[256,16,2,64]{0,3,2,1:T(8,128)(2,1)S(1)} async-done(((bf16[256,16,2,64]{0,3,2,1:T(8,128)(2,1)}), bf16[256,16,2,64]{0,3,2,1:T(8,128)(2,1)S(1)}, u32[]{:S(2)}, u32[]{:S(2)}) %all-to-all-start.2) | async-done | bytes 1048608 | tf_op jit(solution)/shard_map/all_to_all | solution.py:203
  162.1 0.3 bitcast_convert_fusion
  162.4 0.3 fusion.53
  162.7 0.6 fusion.28
  163.3 0.3 copy.62
  163.7 3.5 %fusion.5 = f32[1024,128]{1,0:T(8,128)S(1)} fusion(bf16[2048,128]{1,0:T(8,128)(2,1)S(1)} %bitcast.154, bf16[1,2048,1024]{2,1,0:T(8,128)(2,1)} %all-gather.6.cloned.1.call-done), kind=kOutput, calls=%fused_computation.8 | convolution fusion | flops 536870912 | bytes 5242880 | tf_op jit(solution)/shard_map/dot_general | solution.py:219
  167.1 0.1 reshape.407
  167.2 0.1 pad_maximum_fusion.2
  167.3 0.5 all_to_all.35
  167.7 33.0 %all_to_all.41 = f32[256,1,640]{2,1,0:T(1,128)S(1)} all-to-all(f32[256,1,640]{2,1,0:T(1,128)S(1)} %all_to_all.35), channel_id=1, replica_groups=mesh['dp'=16,'seq'=16] {'dp','seq'}, dimensions={0} | all-to-all | bytes 1310720 | tf_op jit(solution)/shard_map/all_to_all | solution.py:228
  200.8 0.1 slice_reduce_fusion.1
  200.8 0.6 fusion.56
  202.2 0.1 mul.117
  202.3 0.7 reshape.409
  (37 shorter events, 0.5 us)
Async XLA Ops:
  7.2 69.5 %copy-start = (bf16[1024,1024]{1,0:T(8,128)(2,1)S(1)}, bf16[1024,1024]{1,0:T(8,128)(2,1)}, u32[]{:S(2)}) copy-start(bf16[1024,1024]{1,0:T(8,128)(2,1)} %param.17) | copy-start | bytes 6291460
  7.2 23.4 %copy-start.4 = (bf16[1,128,1024]{2,1,0:T(8,128)(2,1)S(1)}, bf16[1,128,1024]{2,1,0:T(8,128)(2,1)}, u32[]{:S(2)}) copy-start(bf16[1,128,1024]{2,1,0:T(8,128)(2,1)} %param.10) | copy-start | bytes 786436
  7.2 23.4 %copy-start.5 = (bf16[1,128,1024]{2,1,0:T(8,128)(2,1)S(1)}, bf16[1,128,1024]{2,1,0:T(8,128)(2,1)}, u32[]{:S(2)}) copy-start(bf16[1,128,1024]{2,1,0:T(8,128)(2,1)} %param.11) | copy-start | bytes 786436
  7.2 23.6 %copy-start.7 = (f32[1024]{0:T(1024)S(1)}, f32[1024]{0:T(1024)}, u32[]{:S(2)}) copy-start(f32[1024]{0:T(1024)} %param.15) | copy-start | bytes 12292
  7.2 85.1 %all-gather.4.cloned.1.call-start = ((), (), s32[]{:S(2)}) async-start(), calls=%async_computation.4 | async-start | bytes 8912896 | tf_op jit(solution)/shard_map/all_gather | solution.py:118
  30.9 3.9 %copy-start.2 = (bf16[1,128,1024]{2,1,0:T(8,128)(2,1)}, bf16[1,128,1024]{2,1,0:T(8,128)(2,1)S(1)}, u32[]{:S(2)}) copy-start(bf16[1,128,1024]{2,1,0:T(8,128)(2,1)S(1)} %multiply_convert_fusion) | copy-start | bytes 786436
  36.0 8.3 %copy-start.6 = (s32[1,2048]{1,0:T(1,128)S(1)}, s32[1,2048]{1,0:T(1,128)}, u32[]{:S(2)}) copy-start(s32[1,2048]{1,0:T(1,128)} %param.13) | copy-start | bytes 24580
  38.2 15.1 %all-to-all-start = ((bf16[1,128,3,16,64]{1,4,2,0,3:T(8,128)(2,1)}), bf16[1,128,3,16,64]{1,4,2,0,3:T(8,128)(2,1)S(1)}, u32[]{:S(2)}, u32[]{:S(2)}) async-start(bf16[1,128,3,16,64]{1,4,2,0,3:T(8,128)(2,1)} %copy.57), calls=%async_computation | async-start | bytes 1572864 | tf_op jit(solution)/shard_map/all_to_all | solution.py:131
  42.9 120.8 %all-gather.6.cloned.1.call-start = ((), (), s32[]{:S(2)}) async-start(), calls=%async_computation.5 | async-start | bytes 4456448 | tf_op jit(solution)/shard_map/all_gather | solution.py:218
  64.8 27.6 %copy-start.3 = (bf16[1,128,1024]{2,1,0:T(8,128)(2,1)S(1)}, bf16[1,128,1024]{2,1,0:T(8,128)(2,1)}, u32[]{:S(2)}) copy-start(bf16[1,128,1024]{2,1,0:T(8,128)(2,1)} %copy-done.2) | copy-start | bytes 786436
  65.6 11.0 %all-to-all-start.1 = ((bf16[1,16,128,1,64]{2,4,3,0,1:T(8,128)(2,1)}), bf16[1,16,128,1,64]{2,4,3,0,1:T(8,128)(2,1)S(1)}, u32[]{:S(2)}, u32[]{:S(2)}) async-start(bf16[1,16,128,1,64]{2,4,3,0,1:T(8,128)(2,1)} %copy.59), calls=%async_computation.1 | async-start | bytes 524288 | tf_op jit(solution)/shard_map/all_to_all | solution.py:135
  96.5 9.5 %collective-permute-start.1 = (bf16[1,64,2048]{2,1,0:T(8,128)(2,1)S(1)}, bf16[1,64,2048]{2,1,0:T(8,128)(2,1)S(1)}, u32[]{:S(2)}, u32[]{:S(2)}) collective-permute-start(bf16[1,64,2048]{2,1,0:T(8,128)(2,1)S(1)} %get-tuple-element.11), channel_id=1, source_target_pairs={{1,0},{2,1},{3,2},{4,3},{5,4},{6,5},{7,6},{8,7},{9,8},{10,9},{11,1... | collective-permute-start | bytes 786440 | tf_op jit(solution)/shard_map/ppermute | solution.py:23
  97.8 9.4 %collective-permute-start = (bf16[1,64,2048]{2,1,0:T(8,128)(2,1)S(1)}, bf16[1,64,2048]{2,1,0:T(8,128)(2,1)S(1)}, u32[]{:S(2)}, u32[]{:S(2)}) collective-permute-start(bf16[1,64,2048]{2,1,0:T(8,128)(2,1)S(1)} %get-tuple-element.10), channel_id=1, source_target_pairs={{0,1},{1,2},{2,3},{3,4},{4,5},{5,6},{6,7},{7,8},{8,9},{9,10},{10,1... | collective-permute-start | bytes 786440 | tf_op jit(solution)/shard_map/ppermute | solution.py:20
  124.3 1.6 copy-start.8
  127.6 34.5 %all-to-all-start.2 = ((bf16[256,16,2,64]{0,3,2,1:T(8,128)(2,1)}), bf16[256,16,2,64]{0,3,2,1:T(8,128)(2,1)S(1)}, u32[]{:S(2)}, u32[]{:S(2)}) async-start(bf16[256,16,2,64]{0,3,2,1:T(8,128)(2,1)} %copy.61), calls=%async_computation.2 | async-start | bytes 2097152 | tf_op jit(solution)/shard_map/all_to_all | solution.py:203
  167.3 37.0 %copy-start.1 = (bf16[1024,1024]{1,0:T(8,128)(2,1)S(1)}, bf16[1024,1024]{1,0:T(8,128)(2,1)}, u32[]{:S(2)}) copy-start(bf16[1024,1024]{1,0:T(8,128)(2,1)} %param.17) | copy-start | bytes 6291460
Sparse Core Ops, SparseCore 0:
  30.0 62.2 all-gather.3
  94.8 64.9 all-gather.5

commit v10 on v9

--- a/solution.py
+++ b/solution.py
@@ -130,6 +130,14 @@
     teacher_proj = teacher_proj.reshape(dialogs, shard_rows, 3, HEADS, head_dim)
     by_heads = lax.all_to_all(teacher_proj, "seq", split_axis=3, concat_axis=1, tiled=True)
     head_out = jax.vmap(teacher_direct)(by_heads, key_bias)
+    normed_all = lax.all_to_all(
+        jnp.broadcast_to(flat_rows[None], (seq_count,) + flat_rows.shape),
+        "seq",
+        split_axis=0,
+        concat_axis=0,
+        tiled=True,
+    ).reshape(-1, model_width)
+    normed_all, head_out = lax.optimization_barrier((normed_all, head_out))
     heads_here = head_out.shape[2]
     head_out = head_out.reshape(dialogs, seq_count, shard_rows, heads_here, head_dim)
     by_frames = lax.all_to_all(head_out, "seq", split_axis=1, concat_axis=1, tiled=True)
@@ -215,7 +223,6 @@
         owned_rows = owned_rows.at[:, :HALO].add(from_prev)
         owned_rows = owned_rows.at[:, shard_rows - HALO :].add(from_next)
     head_grads = owned_rows.reshape(frames, 2 * head_dim).astype(jnp.bfloat16)
-    normed_all = lax.all_gather(flat_rows, "seq", axis=0, tiled=True)
     partial = jnp.dot(normed_all.T, head_grads, preferred_element_type=jnp.float32)
     dp_count = lax.axis_size("dp")
     block = rows_each * 2 * head_dim

time: 213 us -> 244 us (1.15)
  starting transfers between devices: 25 us -> 33.2 us
  waiting for transfers between devices: 56.6 us -> 64 us
  matrix products: 37.7 us -> 43.4 us
  blocking collectives: 52.9 us -> 58.1 us
  local copies, waits for them, and re-layouts: 12.9 us -> 16.4 us
    all_to_all x0 -> x1, waiting for transfers between devices: none -> 34.8 us  [shards(): lax.all_to_all(jnp.broadcast_to(flat_rows[None], (seq_count,) + flat_rows...]
    all_gather x1, waiting for transfers between devices: 15.2 us -> 0.01 us  [shards(): lax.all_gather(lax.all_gather(stacked, 'seq', axis=1, tiled=True), 'dp',...]
    all_to_all x1, waiting for transfers between devices: 21.9 us -> 12.3 us  [shards(): lax.all_to_all(by_head.astype(jnp.bfloat16), 'seq', split_axis=1, concat_...]
    all_to_all x1, starting transfers between devices: 3.71 us -> 11.7 us  [shards(): lax.all_to_all(head_out, 'seq', split_axis=1, concat_axis=1, tiled=True)]
    all_to_all x1, blocking collectives: 33 us -> 38.1 us  [shards(): lax.all_to_all(partial, ('dp', 'seq'), split_axis=0, concat_axis=0, tiled...]
    all_to_all x1, starting transfers between devices: 11.3 us -> 6.17 us  [shards(): lax.all_to_all(by_head.astype(jnp.bfloat16), 'seq', split_axis=1, concat_...]
    all_to_all x0 -> x1, starting transfers between devices: none -> 4.58 us  [shards(): lax.all_to_all(jnp.broadcast_to(flat_rows[None], (seq_count,) + flat_rows...]
    broadcast_in_dim x0 -> x1, local copies, waits for them, and re-layouts: none -> 2.49 us  [shards(): jnp.broadcast_to(flat_rows[None], (seq_count,) + flat_rows.shape)]
  transfers between devices with their start and end apart: 7 -> 7, of which waited for: 6 -> 5; matrix products, arithmetic and copies ran while one was open for 23% -> 11% of each run, Pallas kernels for 0% -> 0%
where the time goes in v10:
time: 244 us; the launch traced here: 243 us
  waiting for transfers between devices  64 us (26%)
  blocking collectives  58.1 us (24%)
  matrix products  43.4 us (18%)
  starting transfers between devices  33.2 us (14%)
  between operations  18.7 us (8%)
  local copies, waits for them, and re-layouts  16.4 us (7%)
  other arithmetic  9.24 us (4%)
    all_to_all x1, blocking collectives, shards(): lax.all_to_all(partial, ('dp', 'seq'), split_axis=0, concat_axis=0, tiled...  38.1 us
    all_to_all x1, waiting for transfers between devices, shards(): lax.all_to_all(jnp.broadcast_to(flat_rows[None], (seq_count,) + flat_rows...  34.8 us
    all_gather x1, blocking collectives, shards(): lax.all_gather(stacked, 'seq', axis=1, tiled=True)  20 us
    all_to_all x1, waiting for transfers between devices, shards(): lax.all_to_all(by_head.astype(jnp.bfloat16), 'seq', split_axis=1, concat_...  12.3 us
    all_to_all x1, starting transfers between devices, shards(): lax.all_to_all(head_out, 'seq', split_axis=1, concat_axis=1, tiled=True)  11.7 us
    all_to_all x1, waiting for transfers between devices, shards(): lax.all_to_all(teacher_proj, 'seq', split_axis=3, concat_axis=1, tiled=True)  9.66 us
    sub x1, matrix products, shards(): grad_prob - jnp.sum(probs * grad_prob, axis=-1, keepdims=True)  8.02 us
    all_to_all x1, waiting for transfers between devices, shards(): lax.all_to_all(head_out, 'seq', split_axis=1, concat_axis=1, tiled=True)  6.97 us
  transfers between devices with their start and end apart: 7, of which 5 were waited for; matrix products, arithmetic and copies ran while one was open for 11% of the time, Pallas kernels for 0%

profile of v10, /device:TPU:1, one launch (start us, length us, event | category | flops | bytes accessed | tf_op | source)
XLA Modules:
  0.0 243.0 jit_solution(2591561055919330282)
XLA Ops:
  7.3 0.9 copy.54
  8.1 0.8 copy.53
  8.9 20.0 %all_gather.6 = bf16[4,64,1024]{2,0,1:T(4,128)(2,1)S(1)} all-gather(bf16[4,4,1024]{2,0,1:T(4,128)(2,1)S(1)} %pad_maximum_fusion.3), channel_id=1, replica_groups=mesh['dp'=16,'seq'=16] {'seq'}, dimensions={1}, use_global_device_ids=true | all-gather | bytes 557056 | tf_op jit(solution)/shard_map/all_gather | solution.py:119
  28.9 0.9 copy.55
  30.5 0.2 multiply_reduce_fusion.2
  30.8 0.1 fusion.38
  30.9 3.8 %convolution_convert_fusion = bf16[128,3072]{1,0:T(8,128)(2,1)S(1)} fusion(bf16[128,1024]{1,0:T(8,128)(2,1)S(1)} %fusion.38, bf16[1024,3072]{1,0:T(8,128)(2,1)} %param.16), kind=kOutput, calls=%fused_computation.8 | convolution fusion | flops 805699584 | bytes 7340032 | tf_op jit(solution)/shard_map/dot_general | solution.py:127
  34.7 1.2 copy.50
  35.9 2.1 copy.51
  38.0 4.7 %all-to-all-start.1 = ((bf16[1,128,3,16,64]{1,4,2,0,3:T(8,128)(2,1)}), bf16[1,128,3,16,64]{1,4,2,0,3:T(8,128)(2,1)S(1)}, u32[]{:S(2)}, u32[]{:S(2)}) async-start(bf16[1,128,3,16,64]{1,4,2,0,3:T(8,128)(2,1)} %copy.51), calls=%async_computation.1 | async-start | bytes 1572864 | tf_op jit(solution)/shard_map/all_to_all | solution.py:131
  43.4 0.1 pad_dynamic-slice_fusion
  43.5 9.7 %all-to-all-done.1 = bf16[1,128,3,16,64]{1,4,2,0,3:T(8,128)(2,1)S(1)} async-done(((bf16[1,128,3,16,64]{1,4,2,0,3:T(8,128)(2,1)}), bf16[1,128,3,16,64]{1,4,2,0,3:T(8,128)(2,1)S(1)}, u32[]{:S(2)}, u32[]{:S(2)}) %all-to-all-start.1) | async-done | bytes 786464 | tf_op jit(solution)/shard_map/all_to_all | solution.py:131
  53.1 2.5 %broadcast_in_dim.50 = bf16[16,128,1024]{2,1,0:T(8,128)(2,1)} broadcast(bf16[128,1024]{1,0:T(8,128)(2,1)S(1)} %fusion.38), dimensions={1,2} | broadcast | bytes 4456448 | tf_op jit(solution)/shard_map/broadcast_in_dim | solution.py:134
  55.6 4.6 %all-to-all-start = ((bf16[16,128,1024]{2,1,0:T(8,128)(2,1)}), bf16[16,128,1024]{2,1,0:T(8,128)(2,1)}, u32[]{:S(2)}, u32[]{:S(2)}) async-start(bf16[16,128,1024]{2,1,0:T(8,128)(2,1)} %broadcast_in_dim.50), calls=%async_computation | async-start | bytes 8388608 | tf_op jit(solution)/shard_map/all_to_all | solution.py:133
  60.2 0.1 copy_bitcast_fusion
  60.3 2.6 %fusion.2 = (f32[2048]{0:T(1024)S(1)}, f32[2048,2048]{0,1:T(8,128)S(1)}) fusion(f32[2048]{0:T(1024)S(1)} %fusion.44, bf16[1,2048,3,1,64]{1,4,2,3,0:T(8,128)(2,1)S(1)} %copy_bitcast_fusion), kind=kOutput, calls=%fused_computation.5 | convolution fusion | flops 549451776 | bytes 17317888 | tf_op jit(solution)/shard_map/vmap(vmap())/dot_general | solution.py:45
  63.0 4.6 %fusion.3 = f32[2048]{0:T(1024)S(1)} fusion(f32[2048,2048]{0,1:T(8,128)S(1)} %get-tuple-element.19, f32[2048]{0:T(1024)S(1)} %get-tuple-element.18, f32[2048]{0:T(1024)S(1)} %fusion.44), kind=kLoop, calls=%fused_computation.6 | loop fusion | flops 16775168 | bytes 16801792 | tf_op jit(solution)/shard_map/vmap(vmap())/reduce_sum | solution.py:51
  67.6 4.1 %fusion.6 = bf16[1,2048,1,64]{1,3,2,0:T(8,128)(2,1)S(1)} fusion(f32[2048,2048]{0,1:T(8,128)S(1)} %get-tuple-element.19, f32[2048]{0:T(1024)S(1)} %fusion.3, f32[2048]{0:T(1024)S(1)} %get-tuple-element.18, f32[2048]{0:T(1024)S(1)} %fusion.44, bf16[1,2048,3,1,64]{1,4,2,3,0:T(8,128)(2,1)S(1)} %copy_bitcast_fusion), kind=kOutput, calls=%fused_computation.10 | convolution fusion | flops 557973504 | bytes 17326080 | tf_op jit(solution)/shard_map/vmap(vmap())/dot_general | solution.py:52
  71.7 34.8 %all-to-all-done = bf16[16,128,1024]{2,1,0:T(8,128)(2,1)} async-done(((bf16[16,128,1024]{2,1,0:T(8,128)(2,1)}), bf16[16,128,1024]{2,1,0:T(8,128)(2,1)}, u32[]{:S(2)}, u32[]{:S(2)}) %all-to-all-start) | async-done | bytes 4194336 | tf_op jit(solution)/shard_map/all_to_all | solution.py:133
  106.4 0.8 copy_bitcast_fusion.1
  107.2 11.7 %all-to-all-start.2 = ((bf16[1,16,128,1,64]{2,4,3,0,1:T(8,128)(2,1)}), bf16[1,16,128,1,64]{2,4,3,0,1:T(8,128)(2,1)S(1)}, u32[]{:S(2)}, u32[]{:S(2)}) async-start(bf16[1,16,128,1,64]{2,4,3,0,1:T(8,128)(2,1)} %copy_bitcast_fusion.1), calls=%async_computation.2 | async-start | bytes 524288 | tf_op jit(solution)/shard_map/all_to_all | solution.py:143
  118.9 0.6 convert_reduce_fusion
  119.5 0.1 or_and_fusion
  119.7 7.0 %all-to-all-done.2 = bf16[1,16,128,1,64]{2,4,3,0,1:T(8,128)(2,1)S(1)} async-done(((bf16[1,16,128,1,64]{2,4,3,0,1:T(8,128)(2,1)}), bf16[1,16,128,1,64]{2,4,3,0,1:T(8,128)(2,1)S(1)}, u32[]{:S(2)}, u32[]{:S(2)}) %all-to-all-start.2) | async-done | bytes 262176 | tf_op jit(solution)/shard_map/all_to_all | solution.py:143
  126.6 1.3 convolution_bitcast_fusion
  128.0 2.0 fusion.22
  130.0 2.0 fusion.21
  132.1 0.7 fusion.50
  132.8 1.3 collective-permute-start.1
  134.1 4.7 %collective-permute-start = (bf16[1,64,2048]{2,1,0:T(8,128)(2,1)S(1)}, bf16[1,64,2048]{2,1,0:T(8,128)(2,1)}, u32[]{:S(2)}, u32[]{:S(2)}) collective-permute-start(bf16[1,64,2048]{2,1,0:T(8,128)(2,1)S(1)} %get-tuple-element.14), channel_id=1, source_target_pairs={{0,1},{1,2},{2,3},{3,4},{4,5},{5,6},{6,7},{7,8},{8,9},{9,10},{10,1... | collective-permute-start | bytes 786440 | tf_op jit(solution)/shard_map/ppermute | solution.py:20
  138.8 2.0 fusion.20
  140.9 0.2 copy.56
  141.1 0.3 collective-permute-done
  141.4 1.1 pad_maximum_fusion
  142.5 0.1 fusion.49
  142.6 1.0 copy.58
  143.7 0.2 copy.57
  143.9 2.1 fusion.52
  146.0 2.2 convolution_convert_fusion.2
  148.2 2.7 %multiply_reduce_fusion.1 = (f32[]{:T(128)}, bf16[128,1024]{1,0:T(8,128)(2,1)S(1)}) fusion(f32[128,1024]{1,0:T(8,128)S(1)} %copy-done.5, bf16[128,1024]{0,1:T(8,128)(2,1)S(1)} %bitcast.162, bf16[4,1024,1024]{2,1,0:T(8,128)(2,1)} %all-gather.2.cloned.1.call-done, pred[128]{0:T(512)(128)(4,1)S(1)} %get-tuple-element.7), kind=kOutput, calls=%fused_computation.57 | convolution fusion | flops 269090816 | bytes 3145860 | tf_op jit(solution)/shard_map/dot_general | solution.py:184
  150.9 2.4 fusion.19
  153.3 0.9 copy.60
  154.2 2.2 convolution_convert_fusion.1
  156.5 8.0 %multiply_bitcast_fusion = f32[1,16,128,256]{3,2,1,0:T(8,128)} fusion(bf16[128,16,64]{0,2,1:T(8,128)(2,1)} %bitcast.158, bf16[256,16,64]{0,2,1:T(8,128)(2,1)S(1)} %bitcast.154, f32[16,128,256]{2,1,0:T(8,128)} %get-tuple-element.21, f32[16,128]{1,0:T(8,128)S(1)} %get-tuple-element.20), kind=kOutput, calls=%fused_computation.19 | convolution fusion | flops 137365760 | bytes 4988928 | tf_op jit(solution)/shard_map/sub | solution.py:197
  164.5 2.0 fusion.27
  166.5 0.2 copy-done.1
  166.7 0.3 fusion.16
  167.0 0.1 pad_maximum_fusion.1
  167.1 1.1 copy.61
  168.2 6.2 %all-to-all-start.3 = ((bf16[256,16,2,64]{0,3,2,1:T(8,128)(2,1)}), bf16[256,16,2,64]{0,3,2,1:T(8,128)(2,1)S(1)}, u32[]{:S(2)}, u32[]{:S(2)}) async-start(bf16[256,16,2,64]{0,3,2,1:T(8,128)(2,1)} %copy.61), calls=%async_computation.3 | async-start | bytes 2097152 | tf_op jit(solution)/shard_map/all_to_all | solution.py:211
  174.4 1.3 compare_select_fusion.1
  175.7 12.3 %all-to-all-done.3 = bf16[256,16,2,64]{0,3,2,1:T(8,128)(2,1)S(1)} async-done(((bf16[256,16,2,64]{0,3,2,1:T(8,128)(2,1)}), bf16[256,16,2,64]{0,3,2,1:T(8,128)(2,1)S(1)}, u32[]{:S(2)}, u32[]{:S(2)}) %all-to-all-start.3) | async-done | bytes 1048608 | tf_op jit(solution)/shard_map/all_to_all | solution.py:211
  188.0 0.2 bitcast_convert_fusion
  188.2 0.3 fusion.48
  188.6 0.6 fusion.26
  189.2 0.3 copy.62
  189.5 3.5 %fusion.53 = f32[1024,128]{1,0:T(8,128)S(1)} fusion(bf16[2048,1024]{1,0:T(8,128)(2,1)} %bitcast.3, bf16[2048,128]{1,0:T(8,128)(2,1)S(1)} %bitcast.151), kind=kOutput, calls=%fused_computation.101 | convolution fusion | flops 536870912 | bytes 5242880 | tf_op jit(solution)/shard_map/dot_general | solution.py:226
  192.9 0.1 reshape.412
  193.0 0.1 pad_maximum_fusion.2
  193.1 0.5 all_to_all.39
  193.5 38.1 %all_to_all.46 = f32[256,1,640]{2,1,0:T(1,128)S(1)} all-to-all(f32[256,1,640]{2,1,0:T(1,128)S(1)} %all_to_all.39), channel_id=1, replica_groups=mesh['dp'=16,'seq'=16] {'dp','seq'}, dimensions={0} | all-to-all | bytes 1310720 | tf_op jit(solution)/shard_map/all_to_all | solution.py:235
  231.8 0.6 fusion.51
  233.0 0.1 mul.117
  233.1 0.7 reshape.414
  (34 shorter events, 0.4 us)
Async XLA Ops:
  7.2 119.5 %copy-start = (bf16[1024,1024]{1,0:T(8,128)(2,1)S(1)}, bf16[1024,1024]{1,0:T(8,128)(2,1)}, u32[]{:S(2)}) copy-start(bf16[1024,1024]{1,0:T(8,128)(2,1)} %param.17) | copy-start | bytes 6291460
  7.2 23.3 %copy-start.2 = (bf16[1,128,1024]{2,1,0:T(8,128)(2,1)S(1)}, bf16[1,128,1024]{2,1,0:T(8,128)(2,1)}, u32[]{:S(2)}) copy-start(bf16[1,128,1024]{2,1,0:T(8,128)(2,1)} %param.10) | copy-start | bytes 786436
  7.2 23.3 %copy-start.3 = (bf16[1,128,1024]{2,1,0:T(8,128)(2,1)S(1)}, bf16[1,128,1024]{2,1,0:T(8,128)(2,1)}, u32[]{:S(2)}) copy-start(bf16[1,128,1024]{2,1,0:T(8,128)(2,1)} %param.11) | copy-start | bytes 786436
  7.2 23.5 %copy-start.7 = (f32[1024]{0:T(1024)S(1)}, f32[1024]{0:T(1024)}, u32[]{:S(2)}) copy-start(f32[1024]{0:T(1024)} %param.15) | copy-start | bytes 12292
  7.2 120.7 %all-gather.2.cloned.1.call-start = ((), (), s32[]{:S(2)}) async-start(), calls=%async_computation.5 | async-start | bytes 8912896 | tf_op jit(solution)/shard_map/all_gather | solution.py:118
  34.7 8.7 %copy-start.6 = (s32[1,2048]{1,0:T(1,128)S(1)}, s32[1,2048]{1,0:T(1,128)}, u32[]{:S(2)}) copy-start(s32[1,2048]{1,0:T(1,128)} %param.13) | copy-start | bytes 24580
  38.0 15.1 %all-to-all-start.1 = ((bf16[1,128,3,16,64]{1,4,2,0,3:T(8,128)(2,1)}), bf16[1,128,3,16,64]{1,4,2,0,3:T(8,128)(2,1)S(1)}, u32[]{:S(2)}, u32[]{:S(2)}) async-start(bf16[1,128,3,16,64]{1,4,2,0,3:T(8,128)(2,1)} %copy.51), calls=%async_computation.1 | async-start | bytes 1572864 | tf_op jit(solution)/shard_map/all_to_all | solution.py:131
  55.6 50.8 %all-to-all-start = ((bf16[16,128,1024]{2,1,0:T(8,128)(2,1)}), bf16[16,128,1024]{2,1,0:T(8,128)(2,1)}, u32[]{:S(2)}, u32[]{:S(2)}) async-start(bf16[16,128,1024]{2,1,0:T(8,128)(2,1)} %broadcast_in_dim.50), calls=%async_computation | async-start | bytes 8388608 | tf_op jit(solution)/shard_map/all_to_all | solution.py:133
  107.2 19.4 %all-to-all-start.2 = ((bf16[1,16,128,1,64]{2,4,3,0,1:T(8,128)(2,1)}), bf16[1,16,128,1,64]{2,4,3,0,1:T(8,128)(2,1)S(1)}, u32[]{:S(2)}, u32[]{:S(2)}) async-start(bf16[1,16,128,1,64]{2,4,3,0,1:T(8,128)(2,1)} %copy_bitcast_fusion.1), calls=%async_computation.2 | async-start | bytes 524288 | tf_op jit(solution)/shard_map/all_to_all | solution.py:143
  132.8 8.2 %collective-permute-start.1 = (bf16[1,64,2048]{2,1,0:T(8,128)(2,1)}, bf16[1,64,2048]{2,1,0:T(8,128)(2,1)}, u32[]{:S(2)}, u32[]{:S(2)}) collective-permute-start(bf16[1,64,2048]{2,1,0:T(8,128)(2,1)} %get-tuple-element.15), channel_id=1, source_target_pairs={{1,0},{2,1},{3,2},{4,3},{5,4},{6,5},{7,6},{8,7},{9,8},{10,9},{11,1... | collective-permute-start | bytes 786440 | tf_op jit(solution)/shard_map/ppermute | solution.py:23
  134.1 7.3 %collective-permute-start = (bf16[1,64,2048]{2,1,0:T(8,128)(2,1)S(1)}, bf16[1,64,2048]{2,1,0:T(8,128)(2,1)}, u32[]{:S(2)}, u32[]{:S(2)}) collective-permute-start(bf16[1,64,2048]{2,1,0:T(8,128)(2,1)S(1)} %get-tuple-element.14), channel_id=1, source_target_pairs={{0,1},{1,2},{2,3},{3,4},{4,5},{5,6},{6,7},{7,8},{8,9},{9,10},{10,1... | collective-permute-start | bytes 786440 | tf_op jit(solution)/shard_map/ppermute | solution.py:20
  143.9 2.1 copy-start.4
  146.0 2.2 copy-start.5
  164.5 2.2 copy-start.1
  168.2 19.8 %all-to-all-start.3 = ((bf16[256,16,2,64]{0,3,2,1:T(8,128)(2,1)}), bf16[256,16,2,64]{0,3,2,1:T(8,128)(2,1)S(1)}, u32[]{:S(2)}, u32[]{:S(2)}) async-start(bf16[256,16,2,64]{0,3,2,1:T(8,128)(2,1)} %copy.61), calls=%async_computation.3 | async-start | bytes 2097152 | tf_op jit(solution)/shard_map/all_to_all | solution.py:211
Sparse Core Ops, SparseCore 0:
  30.0 62.2 all-gather.1

commit v11 on v9

--- a/solution.py
+++ b/solution.py
@@ -22,6 +22,23 @@
         )
         high = lax.ppermute(lax.slice_in_dim(block, 0, width, axis=dim), axis, backward)
         block = jnp.concatenate([low, block, high], axis=dim)
+    return block
+
+
+def doubling_gather(block, axis, dim):
+    count = lax.axis_size(axis)
+    index = lax.axis_index(axis)
+    step = 1
+    while step < count:
+        pairs = [(i, i ^ step) for i in range(count)]
+        other = lax.ppermute(block, axis, pairs)
+        upper = (index & step) != 0
+        block = jnp.where(
+            upper,
+            jnp.concatenate((other, block), axis=dim),
+            jnp.concatenate((block, other), axis=dim),
+        )
+        step *= 2
     return block
 
 
@@ -115,9 +132,7 @@
     window = shard_rows + 2 * HALO
     rows_each = student_out.shape[0]
     stacked = jnp.concatenate((student_in, student_out[None]), axis=0)
-    gathered = lax.all_gather(
-        lax.all_gather(stacked, "seq", axis=1, tiled=True), "dp", axis=1, tiled=True
-    )
+    gathered = lax.all_gather(doubling_gather(stacked, "seq", 1), "dp", axis=1, tiled=True)
     w_inputs = gathered[:3]
     w_output = gathered[3]
     normed = normalize(clean_frames, noise_frames, time_index, modulation)

time: 213 us -> 215 us (level)
  blocking collectives: 52.9 us -> 33 us
  waiting for transfers between devices: 56.6 us -> 68 us
  starting transfers between devices: 25 us -> 35.5 us
  other arithmetic: 8.25 us -> 11 us
  local copies, waits for them, and re-layouts: 12.9 us -> 10.3 us
    all_gather x1 -> x0, blocking collectives: 20 us -> none  [shards(): lax.all_gather(stacked, 'seq', axis=1, tiled=True)]
    ppermute x0 -> x4, waiting for transfers between devices: none -> 11 us  [doubling_gather(): other = lax.ppermute(block, axis, pairs)]
    ppermute x0 -> x4, starting transfers between devices: none -> 9.67 us  [doubling_gather(): other = lax.ppermute(block, axis, pairs)]
  transfers between devices with their start and end apart: 7 -> 11, of which waited for: 6 -> 10; matrix products, arithmetic and copies ran while one was open for 23% -> 23% of each run, Pallas kernels for 0% -> 0%
where the time goes in v11:
time: 215 us
  waiting for transfers between devices  68 us (32%)
  matrix products  37.7 us (18%)
  starting transfers between devices  35.5 us (17%)
  blocking collectives  33 us (15%)
  between operations  19 us (9%)
  other arithmetic  11 us (5%)
  local copies, waits for them, and re-layouts  10.3 us (5%)
    all_to_all x1, blocking collectives, shards(): lax.all_to_all(partial, ('dp', 'seq'), split_axis=0, concat_axis=0, tiled...  33 us
    all_to_all x1, waiting for transfers between devices, shards(): lax.all_to_all(by_head.astype(jnp.bfloat16), 'seq', split_axis=1, concat_...  21.9 us
    all_gather x1, waiting for transfers between devices, shards(): lax.all_gather(doubling_gather(stacked, 'seq', 1), 'dp', axis=1, tiled=True)  15.9 us
    all_to_all x1, starting transfers between devices, shards(): lax.all_to_all(by_head.astype(jnp.bfloat16), 'seq', split_axis=1, concat_...  11.3 us
    ppermute x4, waiting for transfers between devices, doubling_gather(): other = lax.ppermute(block, axis, pairs)  11 us
    ppermute x4, starting transfers between devices, doubling_gather(): other = lax.ppermute(block, axis, pairs)  9.67 us
    all_to_all x1, waiting for transfers between devices, shards(): lax.all_to_all(teacher_proj, 'seq', split_axis=3, concat_axis=1, tiled=True)  8.89 us
    all_to_all x1, waiting for transfers between devices, shards(): lax.all_to_all(head_out, 'seq', split_axis=1, concat_axis=1, tiled=True)  6.78 us
  transfers between devices with their start and end apart: 11, of which 10 were waited for; matrix products, arithmetic and copies ran while one was open for 23% of the time, Pallas kernels for 0%

profile of v11, /device:TPU:1, one launch (start us, length us, event | category | flops | bytes accessed | tf_op | source)
XLA Modules:
  0.0 214.5 jit_solution(13675122534561117780)
XLA Ops:
  7.3 0.9 pad_maximum_fusion.3
  8.2 2.1 collective-permute-start
  10.3 1.3 collective-permute-done
  11.6 0.9 maximum_select_fusion.3
  12.5 3.1 %collective-permute-start.1 = (bf16[4,8,1024]{2,1,0:T(8,128)(2,1)S(1)}, bf16[4,8,1024]{2,1,0:T(8,128)(2,1)S(1)}, u32[]{:S(2)}, u32[]{:S(2)}) collective-permute-start(bf16[4,8,1024]{2,1,0:T(8,128)(2,1)S(1)} %maximum_select_fusion.3), channel_id=1, source_target_pairs={{0,2},{1,3},{2,0},{3,1},{4,6},{5,7},{6,4},{7,5},{8,10},{9,11},{10,... | collective-permute-start | bytes 196616 | tf_op jit(solution)/shard_map/ppermute | solution.py:34
  15.6 1.7 collective-permute-done.1
  17.3 1.6 collective-permute-start.2
  18.9 2.7 %collective-permute-done.2 = bf16[4,16,1024]{2,1,0:T(8,128)(2,1)S(1)} collective-permute-done((bf16[4,16,1024]{2,1,0:T(8,128)(2,1)S(1)}, bf16[4,16,1024]{2,1,0:T(8,128)(2,1)S(1)}, u32[]{:S(2)}, u32[]{:S(2)}) %collective-permute-start.2) | collective-permute-done | bytes 131104 | tf_op jit(solution)/shard_map/ppermute | solution.py:34
  21.6 2.9 %collective-permute-start.3 = (bf16[4,32,1024]{2,1,0:T(8,128)(2,1)S(1)}, bf16[4,32,1024]{2,1,0:T(8,128)(2,1)S(1)}, u32[]{:S(2)}, u32[]{:S(2)}) collective-permute-start(bf16[4,32,1024]{2,1,0:T(8,128)(2,1)S(1)} %maximum_select_fusion.1), channel_id=1, source_target_pairs={{0,8},{1,9},{2,10},{3,11},{4,12},{5,13},{6,14},{7,15},{8,0},{9,1},... | collective-permute-start | bytes 786440 | tf_op jit(solution)/shard_map/ppermute | solution.py:34
  24.4 5.3 %collective-permute-done.3 = bf16[4,32,1024]{2,1,0:T(8,128)(2,1)S(1)} collective-permute-done((bf16[4,32,1024]{2,1,0:T(8,128)(2,1)S(1)}, bf16[4,32,1024]{2,1,0:T(8,128)(2,1)S(1)}, u32[]{:S(2)}, u32[]{:S(2)}) %collective-permute-start.3) | collective-permute-done | bytes 262176 | tf_op jit(solution)/shard_map/ppermute | solution.py:34
  29.8 0.9 maximum_select_fusion
  31.4 0.2 multiply_reduce_fusion.2
  31.7 0.1 multiply_convert_fusion
  31.8 3.9 %convolution_convert_fusion = bf16[128,3072]{1,0:T(8,128)(2,1)S(1)} fusion(bf16[1024,3072]{1,0:T(8,128)(2,1)} %param.16, bf16[1,128,1024]{2,1,0:T(8,128)(2,1)S(1)} %multiply_convert_fusion), kind=kOutput, calls=%fused_computation.10 | convolution fusion | flops 805699584 | bytes 7340032 | tf_op jit(solution)/shard_map/dot_general | solution.py:142
  35.7 1.2 copy.41
  36.9 2.1 %copy.42 = bf16[1,128,3,16,64]{1,4,2,0,3:T(8,128)(2,1)} copy(bf16[1,128,3,16,64]{1,4,3,2,0:T(8,128)(2,1)} %bitcast.148) | data formatting | bytes 1572864 | tf_op jit(solution)/shard_map/reshape | solution.py:145
  39.1 5.2 %all-to-all-start = ((bf16[1,128,3,16,64]{1,4,2,0,3:T(8,128)(2,1)}), bf16[1,128,3,16,64]{1,4,2,0,3:T(8,128)(2,1)S(1)}, u32[]{:S(2)}, u32[]{:S(2)}) async-start(bf16[1,128,3,16,64]{1,4,2,0,3:T(8,128)(2,1)} %copy.42), calls=%async_computation | async-start | bytes 1572864 | tf_op jit(solution)/shard_map/all_to_all | solution.py:146
  44.3 0.2 all-gather.6.cloned.1.call-start
  44.5 0.5 all-gather.6.cloned.1.call-update
  45.9 8.9 %all-to-all-done = bf16[1,128,3,16,64]{1,4,2,0,3:T(8,128)(2,1)S(1)} async-done(((bf16[1,128,3,16,64]{1,4,2,0,3:T(8,128)(2,1)}), bf16[1,128,3,16,64]{1,4,2,0,3:T(8,128)(2,1)S(1)}, u32[]{:S(2)}, u32[]{:S(2)}) %all-to-all-start) | async-done | bytes 786464 | tf_op jit(solution)/shard_map/all_to_all | solution.py:146
  54.7 0.1 copy_bitcast_fusion
  54.9 2.6 %fusion.2 = (f32[2048]{0:T(1024)S(1)}, f32[2048,2048]{0,1:T(8,128)S(1)}) fusion(f32[2048]{0:T(1024)S(1)} %fusion.49, bf16[1,2048,3,1,64]{1,4,2,3,0:T(8,128)(2,1)S(1)} %copy_bitcast_fusion), kind=kOutput, calls=%fused_computation.5 | convolution fusion | flops 549451776 | bytes 17317888 | tf_op jit(solution)/shard_map/vmap(vmap())/dot_general | solution.py:62
  57.5 4.6 %fusion.3 = f32[2048]{0:T(1024)S(1)} fusion(f32[2048,2048]{0,1:T(8,128)S(1)} %get-tuple-element.15, f32[2048]{0:T(1024)S(1)} %get-tuple-element.14, f32[2048]{0:T(1024)S(1)} %fusion.49), kind=kLoop, calls=%fused_computation.6 | loop fusion | flops 16775168 | bytes 16801792 | tf_op jit(solution)/shard_map/vmap(vmap())/reduce_sum | solution.py:68
  62.1 4.1 %fusion.24 = bf16[8,8,16,128]{3,1,2,0:T(8,128)(2,1)S(1)} fusion(f32[2048,2048]{0,1:T(8,128)S(1)} %get-tuple-element.15, f32[2048]{0:T(1024)S(1)} %fusion.3, f32[2048]{0:T(1024)S(1)} %get-tuple-element.14, f32[2048]{0:T(1024)S(1)} %fusion.49, bf16[1,2048,3,1,64]{1,4,2,3,0:T(8,128)(2,1)S(1)} %copy_bitcast_fusion), kind=kOutput, calls=%fused_computation.39 | convolution fusion | flops 557973504 | bytes 17326080 | tf_op jit(solution)/shard_map/vmap(vmap())/dot_general | solution.py:69
  66.2 0.8 copy.44
  67.0 3.5 %all-to-all-start.1 = ((bf16[1,16,128,1,64]{2,4,3,0,1:T(8,128)(2,1)}), bf16[1,16,128,1,64]{2,4,3,0,1:T(8,128)(2,1)S(1)}, u32[]{:S(2)}, u32[]{:S(2)}) async-start(bf16[1,16,128,1,64]{2,4,3,0,1:T(8,128)(2,1)} %copy.44), calls=%async_computation.1 | async-start | bytes 524288 | tf_op jit(solution)/shard_map/all_to_all | solution.py:150
  70.5 0.6 convert_reduce_fusion
  71.1 0.1 or_and_fusion
  71.3 6.8 %all-to-all-done.1 = bf16[1,16,128,1,64]{2,4,3,0,1:T(8,128)(2,1)S(1)} async-done(((bf16[1,16,128,1,64]{2,4,3,0,1:T(8,128)(2,1)}), bf16[1,16,128,1,64]{2,4,3,0,1:T(8,128)(2,1)S(1)}, u32[]{:S(2)}, u32[]{:S(2)}) %all-to-all-start.1) | async-done | bytes 262176 | tf_op jit(solution)/shard_map/all_to_all | solution.py:150
  78.1 0.5 convolution_bitcast_fusion
  78.5 15.9 %all-gather.4.cloned.1.call-done = bf16[4,1024,1024]{2,1,0:T(8,128)(2,1)} async-done(((bf16[4,64,1024]{2,1,0:T(8,128)(2,1)}), bf16[4,1024,1024]{2,1,0:T(8,128)(2,1)}) %all-gather.4.cloned.1.call-update) | async-done | bytes 8388624 | tf_op jit(solution)/shard_map/all_gather | solution.py:135
  94.4 2.0 fusion.23
  96.5 2.0 fusion.22
  98.6 1.3 collective-permute-start.5
  99.9 4.2 %collective-permute-start.4 = (bf16[1,64,2048]{2,1,0:T(8,128)(2,1)S(1)}, bf16[1,64,2048]{2,1,0:T(8,128)(2,1)S(1)}, u32[]{:S(2)}, u32[]{:S(2)}) collective-permute-start(bf16[1,64,2048]{2,1,0:T(8,128)(2,1)S(1)} %get-tuple-element.10), channel_id=1, source_target_pairs={{0,1},{1,2},{2,3},{3,4},{4,5},{5,6},{6,7},{7,8},{8,9},{9,10},{10,1... | collective-permute-start | bytes 786440 | tf_op jit(solution)/shard_map/ppermute | solution.py:20
  104.1 2.0 fusion.21
  106.2 0.2 copy.38
  106.4 1.7 collective-permute-done.5
  108.1 1.2 collective-permute-done.4
  109.5 0.2 copy.40
  109.7 0.2 copy.39
  109.9 2.1 fusion.57
  112.0 2.2 %convolution_convert_fusion.2 = bf16[16,64,128]{2,1,0:T(8,128)(2,1)S(1)} fusion(bf16[256,16,64]{0,2,1:T(8,128)(2,1)S(1)} %bitcast.157, f32[16,128,256]{2,1,0:T(8,128)} %get-tuple-element.17, f32[16,128]{1,0:T(8,128)S(1)} %get-tuple-element.16), kind=kOutput, calls=%fused_computation.38 | convolution fusion | flops 68288512 | bytes 2891776 | tf_op jit(solution)/shard_map/bhrw,bwhd->brhd/dot_general | solution.py:187
  114.2 2.8 %multiply_reduce_fusion.1 = (f32[]{:T(128)}, bf16[128,1024]{1,0:T(8,128)(2,1)S(1)}) fusion(f32[128,1024]{1,0:T(8,128)S(1)} %convolution_bitcast_fusion, bf16[128,1024]{0,1:T(8,128)(2,1)S(1)} %bitcast.167, bf16[4,1024,1024]{2,1,0:T(8,128)(2,1)} %all-gather.4.cloned.1.call-done, pred[128]{0:T(512)(128)(4,1)S(1)} %get-tuple-element.3), kind=kOutput, calls=%fused_computation.60 | convolution fusion | flops 269090816 | bytes 3145860 | tf_op jit(solution)/shard_map/dot_general | solution.py:191
  116.9 2.4 %fusion.20 = bf16[128,1024]{1,0:T(8,128)(2,1)S(1)} fusion(bf16[4,1024,1024]{2,1,0:T(8,128)(2,1)} %all-gather.4.cloned.1.call-done, bf16[128,1024]{1,0:T(8,128)(2,1)S(1)} %get-tuple-element.19), kind=kOutput, calls=%fused_computation.34 | convolution fusion | flops 268566528 | bytes 2621440 | tf_op jit(solution)/shard_map/dot_general | solution.py:197
  119.4 0.2 copy.45
  119.5 6.5 %multiply_bitcast_fusion = f32[1,16,128,256]{3,2,1,0:T(8,128)S(1)} fusion(bf16[128,16,64]{0,2,1:T(8,128)(2,1)S(1)} %bitcast.161, bf16[256,16,64]{0,2,1:T(8,128)(2,1)S(1)} %bitcast.158, f32[16,128,256]{2,1,0:T(8,128)} %get-tuple-element.17, f32[16,128]{1,0:T(8,128)S(1)} %get-tuple-element.16), kind=kOutput, calls=%fused_computation.20 | convolution fusion | flops 137365760 | bytes 4988928 | tf_op jit(solution)/shard_map/sub | solution.py:204
  126.0 0.3 fusion.29
  126.3 0.3 fusion.17
  126.6 1.3 copy-done.8
  127.9 0.6 convolution_convert_fusion.1
  128.6 1.1 copy.46
  129.7 11.3 %all-to-all-start.2 = ((bf16[256,16,2,64]{0,3,2,1:T(8,128)(2,1)}), bf16[256,16,2,64]{0,3,2,1:T(8,128)(2,1)S(1)}, u32[]{:S(2)}, u32[]{:S(2)}) async-start(bf16[256,16,2,64]{0,3,2,1:T(8,128)(2,1)} %copy.46), calls=%async_computation.2 | async-start | bytes 2097152 | tf_op jit(solution)/shard_map/all_to_all | solution.py:218
  141.0 1.3 compare_select_fusion.1
  142.3 21.9 %all-to-all-done.2 = bf16[256,16,2,64]{0,3,2,1:T(8,128)(2,1)S(1)} async-done(((bf16[256,16,2,64]{0,3,2,1:T(8,128)(2,1)}), bf16[256,16,2,64]{0,3,2,1:T(8,128)(2,1)S(1)}, u32[]{:S(2)}, u32[]{:S(2)}) %all-to-all-start.2) | async-done | bytes 1048608 | tf_op jit(solution)/shard_map/all_to_all | solution.py:218
  164.2 0.3 bitcast_convert_fusion
  164.5 0.3 fusion.53
  164.9 0.6 fusion.28
  165.5 0.3 copy.47
  165.8 3.5 %fusion.5 = f32[1024,128]{1,0:T(8,128)S(1)} fusion(bf16[2048,128]{1,0:T(8,128)(2,1)S(1)} %bitcast.154, bf16[1,2048,1024]{2,1,0:T(8,128)(2,1)} %all-gather.6.cloned.1.call-done), kind=kOutput, calls=%fused_computation.8 | convolution fusion | flops 536870912 | bytes 5242880 | tf_op jit(solution)/shard_map/dot_general | solution.py:234
  169.4 0.5 all_to_all.35
  169.9 33.0 %all_to_all.41 = f32[256,1,640]{2,1,0:T(1,128)S(1)} all-to-all(f32[256,1,640]{2,1,0:T(1,128)S(1)} %all_to_all.35), channel_id=1, replica_groups=mesh['dp'=16,'seq'=16] {'dp','seq'}, dimensions={0} | all-to-all | bytes 1310720 | tf_op jit(solution)/shard_map/all_to_all | solution.py:243
  203.0 0.7 fusion.56
  204.5 0.7 reshape.409
  (45 shorter events, 1.1 us)
Async XLA Ops:
  7.2 70.9 %copy-start = (bf16[1024,1024]{1,0:T(8,128)(2,1)S(1)}, bf16[1024,1024]{1,0:T(8,128)(2,1)}, u32[]{:S(2)}) copy-start(bf16[1024,1024]{1,0:T(8,128)(2,1)} %param.17) | copy-start | bytes 6291460
  7.2 24.2 %copy-start.4 = (bf16[1,128,1024]{2,1,0:T(8,128)(2,1)S(1)}, bf16[1,128,1024]{2,1,0:T(8,128)(2,1)}, u32[]{:S(2)}) copy-start(bf16[1,128,1024]{2,1,0:T(8,128)(2,1)} %param.10) | copy-start | bytes 786436
  7.2 24.2 %copy-start.5 = (bf16[1,128,1024]{2,1,0:T(8,128)(2,1)S(1)}, bf16[1,128,1024]{2,1,0:T(8,128)(2,1)}, u32[]{:S(2)}) copy-start(bf16[1,128,1024]{2,1,0:T(8,128)(2,1)} %param.11) | copy-start | bytes 786436
  7.2 24.4 %copy-start.7 = (f32[1024]{0:T(1024)S(1)}, f32[1024]{0:T(1024)}, u32[]{:S(2)}) copy-start(f32[1024]{0:T(1024)} %param.15) | copy-start | bytes 12292
  7.2 87.2 %all-gather.4.cloned.1.call-start = ((), (), s32[]{:S(2)}) async-start(), calls=%async_computation.4 | async-start | bytes 8912896 | tf_op jit(solution)/shard_map/all_gather | solution.py:135
  8.2 3.4 %collective-permute-start = (bf16[4,4,1024]{2,1,0:T(4,128)(2,1)S(1)}, bf16[4,4,1024]{2,1,0:T(4,128)(2,1)S(1)}, u32[]{:S(2)}, u32[]{:S(2)}) collective-permute-start(bf16[4,4,1024]{2,1,0:T(4,128)(2,1)S(1)} %pad_maximum_fusion.3), channel_id=1, source_target_pairs={{0,1},{1,0},{2,3},{3,2},{4,5},{5,4},{6,7},{7,6},{8,9},{9,8},{10,11... | collective-permute-start | bytes 98312 | tf_op jit(solution)/shard_map/ppermute | solution.py:34
  12.5 4.7 %collective-permute-start.1 = (bf16[4,8,1024]{2,1,0:T(8,128)(2,1)S(1)}, bf16[4,8,1024]{2,1,0:T(8,128)(2,1)S(1)}, u32[]{:S(2)}, u32[]{:S(2)}) collective-permute-start(bf16[4,8,1024]{2,1,0:T(8,128)(2,1)S(1)} %maximum_select_fusion.3), channel_id=1, source_target_pairs={{0,2},{1,3},{2,0},{3,1},{4,6},{5,7},{6,4},{7,5},{8,10},{9,11},{10,... | collective-permute-start | bytes 196616 | tf_op jit(solution)/shard_map/ppermute | solution.py:34
  17.3 4.3 %collective-permute-start.2 = (bf16[4,16,1024]{2,1,0:T(8,128)(2,1)S(1)}, bf16[4,16,1024]{2,1,0:T(8,128)(2,1)S(1)}, u32[]{:S(2)}, u32[]{:S(2)}) collective-permute-start(bf16[4,16,1024]{2,1,0:T(8,128)(2,1)S(1)} %maximum_select_fusion.2), channel_id=1, source_target_pairs={{0,4},{1,5},{2,6},{3,7},{4,0},{5,1},{6,2},{7,3},{8,12},{9,13},{10,... | collective-permute-start | bytes 393224 | tf_op jit(solution)/shard_map/ppermute | solution.py:34
  21.6 8.2 %collective-permute-start.3 = (bf16[4,32,1024]{2,1,0:T(8,128)(2,1)S(1)}, bf16[4,32,1024]{2,1,0:T(8,128)(2,1)S(1)}, u32[]{:S(2)}, u32[]{:S(2)}) collective-permute-start(bf16[4,32,1024]{2,1,0:T(8,128)(2,1)S(1)} %maximum_select_fusion.1), channel_id=1, source_target_pairs={{0,8},{1,9},{2,10},{3,11},{4,12},{5,13},{6,14},{7,15},{8,0},{9,1},... | collective-permute-start | bytes 786440 | tf_op jit(solution)/shard_map/ppermute | solution.py:34
  31.8 3.9 %copy-start.2 = (bf16[1,128,1024]{2,1,0:T(8,128)(2,1)}, bf16[1,128,1024]{2,1,0:T(8,128)(2,1)S(1)}, u32[]{:S(2)}) copy-start(bf16[1,128,1024]{2,1,0:T(8,128)(2,1)S(1)} %multiply_convert_fusion) | copy-start | bytes 786436
  36.9 8.8 %copy-start.6 = (s32[1,2048]{1,0:T(1,128)S(1)}, s32[1,2048]{1,0:T(1,128)}, u32[]{:S(2)}) copy-start(s32[1,2048]{1,0:T(1,128)} %param.13) | copy-start | bytes 24580
  39.1 15.7 %all-to-all-start = ((bf16[1,128,3,16,64]{1,4,2,0,3:T(8,128)(2,1)}), bf16[1,128,3,16,64]{1,4,2,0,3:T(8,128)(2,1)S(1)}, u32[]{:S(2)}, u32[]{:S(2)}) async-start(bf16[1,128,3,16,64]{1,4,2,0,3:T(8,128)(2,1)} %copy.42), calls=%async_computation | async-start | bytes 1572864 | tf_op jit(solution)/shard_map/all_to_all | solution.py:146
  44.3 121.5 %all-gather.6.cloned.1.call-start = ((), (), s32[]{:S(2)}) async-start(), calls=%async_computation.5 | async-start | bytes 4456448 | tf_op jit(solution)/shard_map/all_gather | solution.py:233
  66.2 28.2 %copy-start.3 = (bf16[1,128,1024]{2,1,0:T(8,128)(2,1)S(1)}, bf16[1,128,1024]{2,1,0:T(8,128)(2,1)}, u32[]{:S(2)}) copy-start(bf16[1,128,1024]{2,1,0:T(8,128)(2,1)} %copy-done.2) | copy-start | bytes 786436
  67.0 11.0 %all-to-all-start.1 = ((bf16[1,16,128,1,64]{2,4,3,0,1:T(8,128)(2,1)}), bf16[1,16,128,1,64]{2,4,3,0,1:T(8,128)(2,1)S(1)}, u32[]{:S(2)}, u32[]{:S(2)}) async-start(bf16[1,16,128,1,64]{2,4,3,0,1:T(8,128)(2,1)} %copy.44), calls=%async_computation.1 | async-start | bytes 524288 | tf_op jit(solution)/shard_map/all_to_all | solution.py:150
  98.6 9.5 %collective-permute-start.5 = (bf16[1,64,2048]{2,1,0:T(8,128)(2,1)S(1)}, bf16[1,64,2048]{2,1,0:T(8,128)(2,1)S(1)}, u32[]{:S(2)}, u32[]{:S(2)}) collective-permute-start(bf16[1,64,2048]{2,1,0:T(8,128)(2,1)S(1)} %get-tuple-element.11), channel_id=1, source_target_pairs={{1,0},{2,1},{3,2},{4,3},{5,4},{6,5},{7,6},{8,7},{9,8},{10,9},{11,1... | collective-permute-start | bytes 786440 | tf_op jit(solution)/shard_map/ppermute | solution.py:23
  99.9 9.4 %collective-permute-start.4 = (bf16[1,64,2048]{2,1,0:T(8,128)(2,1)S(1)}, bf16[1,64,2048]{2,1,0:T(8,128)(2,1)S(1)}, u32[]{:S(2)}, u32[]{:S(2)}) collective-permute-start(bf16[1,64,2048]{2,1,0:T(8,128)(2,1)S(1)} %get-tuple-element.10), channel_id=1, source_target_pairs={{0,1},{1,2},{2,3},{3,4},{4,5},{5,6},{6,7},{7,8},{8,9},{9,10},{10,1... | collective-permute-start | bytes 786440 | tf_op jit(solution)/shard_map/ppermute | solution.py:20
  126.3 1.6 copy-start.8
  129.7 34.6 %all-to-all-start.2 = ((bf16[256,16,2,64]{0,3,2,1:T(8,128)(2,1)}), bf16[256,16,2,64]{0,3,2,1:T(8,128)(2,1)S(1)}, u32[]{:S(2)}, u32[]{:S(2)}) async-start(bf16[256,16,2,64]{0,3,2,1:T(8,128)(2,1)} %copy.46), calls=%async_computation.2 | async-start | bytes 2097152 | tf_op jit(solution)/shard_map/all_to_all | solution.py:218
  169.4 37.2 %copy-start.1 = (bf16[1024,1024]{1,0:T(8,128)(2,1)S(1)}, bf16[1024,1024]{1,0:T(8,128)(2,1)}, u32[]{:S(2)}) copy-start(bf16[1024,1024]{1,0:T(8,128)(2,1)} %param.17) | copy-start | bytes 6291460
Sparse Core Ops, SparseCore 0:
  30.9 63.4 all-gather.3
  96.9 65.0 all-gather.5

commit v12 on v11

--- a/solution.py
+++ b/solution.py
@@ -132,7 +132,9 @@
     window = shard_rows + 2 * HALO
     rows_each = student_out.shape[0]
     stacked = jnp.concatenate((student_in, student_out[None]), axis=0)
-    gathered = lax.all_gather(doubling_gather(stacked, "seq", 1), "dp", axis=1, tiled=True)
+    gathered = lax.all_gather(
+        lax.all_gather(stacked, "seq", axis=1, tiled=True), "dp", axis=1, tiled=True
+    )
     w_inputs = gathered[:3]
     w_output = gathered[3]
     normed = normalize(clean_frames, noise_frames, time_index, modulation)
@@ -230,7 +232,7 @@
         owned_rows = owned_rows.at[:, :HALO].add(from_prev)
         owned_rows = owned_rows.at[:, shard_rows - HALO :].add(from_next)
     head_grads = owned_rows.reshape(frames, 2 * head_dim).astype(jnp.bfloat16)
-    normed_all = lax.all_gather(flat_rows, "seq", axis=0, tiled=True)
+    normed_all = doubling_gather(flat_rows, "seq", 0)
     partial = jnp.dot(normed_all.T, head_grads, preferred_element_type=jnp.float32)
     dp_count = lax.axis_size("dp")
     block = rows_each * 2 * head_dim

time: 215 us -> 210 us (0.977)
  waiting for transfers between devices: 68 us -> 28.8 us
  blocking collectives: 33 us -> 62.1 us
  starting transfers between devices: 35.5 us -> 30 us
  matrix products: 37.7 us -> 42.1 us
  other arithmetic: 11 us -> 15.2 us
    all_gather x0 -> x1, blocking collectives: none -> 20 us  [shards(): lax.all_gather(stacked, 'seq', axis=1, tiled=True)]
    all_gather x2 -> x1, waiting for transfers between devices: 15.9 us -> 2.97 us  [shards(): lax.all_gather(lax.all_gather(stacked, 'seq', axis=1, tiled=True), 'dp',...]
    ppermute x4, waiting for transfers between devices: 11 us -> 0.01 us  [doubling_gather(): other = lax.ppermute(block, axis, pairs)]
    all_to_all x1, waiting for transfers between devices: 21.9 us -> 11.3 us  [shards(): lax.all_to_all(by_head.astype(jnp.bfloat16), 'seq', split_axis=1, concat_...]
    all_to_all x1, blocking collectives: 33 us -> 42.1 us  [shards(): lax.all_to_all(partial, ('dp', 'seq'), split_axis=0, concat_axis=0, tiled...]
    select_n x4 -> x3, other arithmetic: 1.9 us -> 6.93 us  [doubling_gather(): jnp.where(upper, jnp.concatenate((other, block), axis=dim), jnp.concatena...]
    ppermute x4, starting transfers between devices: 9.67 us -> 6 us  [doubling_gather(): other = lax.ppermute(block, axis, pairs)]
    all_to_all x1, waiting for transfers between devices: 8.89 us -> 5.81 us  [shards(): lax.all_to_all(teacher_proj, 'seq', split_axis=3, concat_axis=1, tiled=True)]
  transfers between devices with their start and end apart: 11 -> 10, of which waited for: 10 -> 5; matrix products, arithmetic and copies ran while one was open for 23% -> 29% of each run, Pallas kernels for 0% -> 0%
where the time goes in v12:
time: 210 us; the launch traced here: 209 us
  blocking collectives  62.1 us (30%)
  matrix products  42.1 us (20%)
  starting transfers between devices  30 us (14%)
  waiting for transfers between devices  28.8 us (14%)
  between operations  18.9 us (9%)
  other arithmetic  15.2 us (7%)
  local copies, waits for them, and re-layouts  12.2 us (6%)
    all_to_all x1, blocking collectives, shards(): lax.all_to_all(partial, ('dp', 'seq'), split_axis=0, concat_axis=0, tiled...  42.1 us
    all_gather x1, blocking collectives, shards(): lax.all_gather(stacked, 'seq', axis=1, tiled=True)  20 us
    all_to_all x1, waiting for transfers between devices, shards(): lax.all_to_all(by_head.astype(jnp.bfloat16), 'seq', split_axis=1, concat_...  11.3 us
    all_to_all x1, starting transfers between devices, shards(): lax.all_to_all(by_head.astype(jnp.bfloat16), 'seq', split_axis=1, concat_...  9.51 us
    all_to_all x1, waiting for transfers between devices, shards(): lax.all_to_all(head_out, 'seq', split_axis=1, concat_axis=1, tiled=True)  7.89 us
    select_n x3, other arithmetic, doubling_gather(): jnp.where(upper, jnp.concatenate((other, block), axis=dim), jnp.concatena...  6.93 us
    sub x1, matrix products, shards(): grad_prob - jnp.sum(probs * grad_prob, axis=-1, keepdims=True)  6.64 us
    ppermute x4, starting transfers between devices, doubling_gather(): other = lax.ppermute(block, axis, pairs)  6 us
  transfers between devices with their start and end apart: 10, of which 5 were waited for; matrix products, arithmetic and copies ran while one was open for 29% of the time, Pallas kernels for 0%

profile of v12, /device:TPU:1, one launch (start us, length us, event | category | flops | bytes accessed | tf_op | source)
XLA Modules:
  0.0 209.2 jit_solution(7583741783113354421)
XLA Ops:
  7.3 0.9 copy.51
  8.1 0.8 copy.50
  8.9 20.0 %all_gather.6 = bf16[4,64,1024]{2,0,1:T(4,128)(2,1)S(1)} all-gather(bf16[4,4,1024]{2,0,1:T(4,128)(2,1)S(1)} %pad_maximum_fusion.3), channel_id=1, replica_groups=mesh['dp'=16,'seq'=16] {'seq'}, dimensions={1}, use_global_device_ids=true | all-gather | bytes 557056 | tf_op jit(solution)/shard_map/all_gather | solution.py:136
  28.9 1.0 copy.52
  30.6 0.2 multiply_reduce_fusion.2
  30.8 0.1 fusion.45
  31.0 1.3 collective-permute-start
  32.2 3.8 %convolution_convert_fusion = bf16[128,3072]{1,0:T(8,128)(2,1)S(1)} fusion(bf16[128,1024]{1,0:T(8,128)(2,1)S(1)} %fusion.45, bf16[1024,3072]{1,0:T(8,128)(2,1)} %param.16), kind=kOutput, calls=%fused_computation.16 | convolution fusion | flops 805699584 | bytes 7340032 | tf_op jit(solution)/shard_map/dot_general | solution.py:144
  36.0 1.2 copy.56
  37.2 2.1 %copy.57 = bf16[1,128,3,16,64]{1,4,2,0,3:T(8,128)(2,1)} copy(bf16[1,128,3,16,64]{1,4,3,2,0:T(8,128)(2,1)} %bitcast.142) | data formatting | bytes 1572864 | tf_op jit(solution)/shard_map/reshape | solution.py:147
  39.3 4.4 %all-to-all-start = ((bf16[1,128,3,16,64]{1,4,2,0,3:T(8,128)(2,1)}), bf16[1,128,3,16,64]{1,4,2,0,3:T(8,128)(2,1)S(1)}, u32[]{:S(2)}, u32[]{:S(2)}) async-start(bf16[1,128,3,16,64]{1,4,2,0,3:T(8,128)(2,1)} %copy.57), calls=%async_computation | async-start | bytes 1572864 | tf_op jit(solution)/shard_map/all_to_all | solution.py:148
  44.4 0.1 pad_dynamic-slice_fusion
  44.5 1.0 maximum_select_fusion.4
  45.5 2.9 %collective-permute-start.1 = (bf16[256,1024]{1,0:T(8,128)(2,1)}, bf16[256,1024]{1,0:T(8,128)(2,1)}, u32[]{:S(2)}, u32[]{:S(2)}) collective-permute-start(bf16[256,1024]{1,0:T(8,128)(2,1)} %maximum_select_fusion.4), channel_id=1, source_target_pairs={{0,2},{1,3},{2,0},{3,1},{4,6},{5,7},{6,4},{7,5},{8,10},{9,11},{10,... | collective-permute-start | bytes 1572872 | tf_op jit(solution)/shard_map/ppermute | solution.py:34
  48.3 5.8 %all-to-all-done = bf16[1,128,3,16,64]{1,4,2,0,3:T(8,128)(2,1)S(1)} async-done(((bf16[1,128,3,16,64]{1,4,2,0,3:T(8,128)(2,1)}), bf16[1,128,3,16,64]{1,4,2,0,3:T(8,128)(2,1)S(1)}, u32[]{:S(2)}, u32[]{:S(2)}) %all-to-all-start) | async-done | bytes 786464 | tf_op jit(solution)/shard_map/all_to_all | solution.py:148
  54.1 0.1 copy_bitcast_fusion
  54.3 2.6 %fusion.2 = (f32[2048]{0:T(1024)S(1)}, f32[2048,2048]{0,1:T(8,128)S(1)}) fusion(f32[2048]{0:T(1024)S(1)} %fusion.51, bf16[1,2048,3,1,64]{1,4,2,3,0:T(8,128)(2,1)S(1)} %copy_bitcast_fusion), kind=kOutput, calls=%fused_computation.5 | convolution fusion | flops 549451776 | bytes 17317888 | tf_op jit(solution)/shard_map/vmap(vmap())/dot_general | solution.py:62
  56.9 4.6 %fusion.3 = f32[2048]{0:T(1024)S(1)} fusion(f32[2048,2048]{0,1:T(8,128)S(1)} %get-tuple-element.15, f32[2048]{0:T(1024)S(1)} %get-tuple-element.14, f32[2048]{0:T(1024)S(1)} %fusion.51), kind=kLoop, calls=%fused_computation.6 | loop fusion | flops 16775168 | bytes 16801792 | tf_op jit(solution)/shard_map/vmap(vmap())/reduce_sum | solution.py:68
  61.5 2.0 maximum_select_fusion.3
  63.5 1.0 collective-permute-start.2
  64.5 4.1 %fusion.29 = bf16[8,8,16,128]{3,1,2,0:T(8,128)(2,1)S(1)} fusion(f32[2048,2048]{0,1:T(8,128)S(1)} %get-tuple-element.15, f32[2048]{0:T(1024)S(1)} %fusion.3, f32[2048]{0:T(1024)S(1)} %get-tuple-element.14, f32[2048]{0:T(1024)S(1)} %fusion.51, bf16[1,2048,3,1,64]{1,4,2,3,0:T(8,128)(2,1)S(1)} %copy_bitcast_fusion), kind=kOutput, calls=%fused_computation.46 | convolution fusion | flops 557973504 | bytes 17326080 | tf_op jit(solution)/shard_map/vmap(vmap())/dot_general | solution.py:69
  68.6 0.8 copy.59
  69.4 4.5 %all-to-all-start.1 = ((bf16[1,16,128,1,64]{2,4,3,0,1:T(8,128)(2,1)}), bf16[1,16,128,1,64]{2,4,3,0,1:T(8,128)(2,1)}, u32[]{:S(2)}, u32[]{:S(2)}) async-start(bf16[1,16,128,1,64]{2,4,3,0,1:T(8,128)(2,1)} %copy.59), calls=%async_computation.1 | async-start | bytes 524288 | tf_op jit(solution)/shard_map/all_to_all | solution.py:152
  73.9 0.6 convert_reduce_fusion
  74.5 0.1 or_and_fusion
  74.6 7.9 %all-to-all-done.1 = bf16[1,16,128,1,64]{2,4,3,0,1:T(8,128)(2,1)} async-done(((bf16[1,16,128,1,64]{2,4,3,0,1:T(8,128)(2,1)}), bf16[1,16,128,1,64]{2,4,3,0,1:T(8,128)(2,1)}, u32[]{:S(2)}, u32[]{:S(2)}) %all-to-all-start.1) | async-done | bytes 262176 | tf_op jit(solution)/shard_map/all_to_all | solution.py:152
  82.5 2.3 %convolution_bitcast_fusion = f32[128,1024]{1,0:T(8,128)} fusion(bf16[16,64,1024]{2,1,0:T(8,128)(2,1)S(1)} %bitcast.138, bf16[1,16,128,1,64]{2,4,3,0,1:T(8,128)(2,1)} %all-to-all-done.1), kind=kOutput, calls=%fused_computation.38 | convolution fusion | flops 268435456 | bytes 2883584 | tf_op jit(solution)/shard_map/bsfhd,shdn->bfn/dot_general | solution.py:153
  84.8 4.0 %maximum_select_fusion.2 = bf16[1024,1024]{1,0:T(8,128)(2,1)} fusion(bf16[512,1024]{1,0:T(8,128)(2,1)S(1)} %maximum_select_fusion.3, bf16[512,1024]{1,0:T(8,128)(2,1)} %collective-permute-done.2, pred[]{:T(512)S(6)} %ne.13), kind=kLoop, calls=%fused_computation.25 | loop fusion | flops 9437184 | bytes 4194305 | tf_op jit(solution)/shard_map/jit(_where)/select_n | solution.py:36
  88.8 0.9 collective-permute-start.3
  89.6 3.0 %all-gather.2.cloned.1.call-done = bf16[4,1024,1024]{2,1,0:T(8,128)(2,1)} async-done(((bf16[4,64,1024]{2,1,0:T(8,128)(2,1)}), bf16[4,1024,1024]{2,1,0:T(8,128)(2,1)}) %all-gather.2.cloned.1.call-update) | async-done | bytes 8388624 | tf_op jit(solution)/shard_map/all_gather | solution.py:135
  92.6 2.0 fusion.28
  94.7 2.0 fusion.27
  96.8 1.3 collective-permute-start.5
  98.1 4.2 %collective-permute-start.4 = (bf16[1,64,2048]{2,1,0:T(8,128)(2,1)S(1)}, bf16[1,64,2048]{2,1,0:T(8,128)(2,1)S(1)}, u32[]{:S(2)}, u32[]{:S(2)}) collective-permute-start(bf16[1,64,2048]{2,1,0:T(8,128)(2,1)S(1)} %get-tuple-element.10), channel_id=1, source_target_pairs={{0,1},{1,2},{2,3},{3,4},{4,5},{5,6},{6,7},{7,8},{8,9},{9,10},{10,1... | collective-permute-start | bytes 786440 | tf_op jit(solution)/shard_map/ppermute | solution.py:20
  102.3 2.0 fusion.26
  104.4 0.2 copy.53
  104.5 0.8 collective-permute-done.4
  105.4 0.1 pad_maximum_fusion
  105.6 0.2 copy.55
  105.8 0.2 copy.54
  106.0 2.1 fusion.60
  108.1 2.2 %convolution_convert_fusion.2 = bf16[16,64,128]{2,1,0:T(8,128)(2,1)S(1)} fusion(bf16[256,16,64]{0,2,1:T(8,128)(2,1)S(1)} %bitcast.150, f32[16,128,256]{2,1,0:T(8,128)} %get-tuple-element.17, f32[16,128]{1,0:T(8,128)S(1)} %get-tuple-element.16), kind=kOutput, calls=%fused_computation.45 | convolution fusion | flops 68288512 | bytes 2891776 | tf_op jit(solution)/shard_map/bhrw,bwhd->brhd/dot_general | solution.py:189
  110.3 2.7 %multiply_reduce_fusion.1 = (f32[]{:T(128)}, bf16[128,1024]{1,0:T(8,128)(2,1)S(1)}) fusion(f32[128,1024]{1,0:T(8,128)S(1)} %copy-done.4, bf16[128,1024]{0,1:T(8,128)(2,1)S(1)} %bitcast.158, bf16[4,1024,1024]{2,1,0:T(8,128)(2,1)} %all-gather.2.cloned.1.call-done, pred[128]{0:T(512)(128)(4,1)S(1)} %get-tuple-element.3), kind=kOutput, calls=%fused_computation.68 | convolution fusion | flops 269090816 | bytes 3145860 | tf_op jit(solution)/shard_map/dot_general | solution.py:193
  113.0 2.4 %fusion.25 = bf16[128,1024]{1,0:T(8,128)(2,1)S(1)} fusion(bf16[4,1024,1024]{2,1,0:T(8,128)(2,1)} %all-gather.2.cloned.1.call-done, bf16[128,1024]{1,0:T(8,128)(2,1)S(1)} %get-tuple-element.19), kind=kOutput, calls=%fused_computation.41 | convolution fusion | flops 268566528 | bytes 2621440 | tf_op jit(solution)/shard_map/dot_general | solution.py:199
  115.4 0.8 copy.60
  116.3 2.2 %convolution_convert_fusion.1 = bf16[16,64,256]{2,1,0:T(8,128)(2,1)S(1)} fusion(bf16[128,16,64]{0,2,1:T(8,128)(2,1)} %bitcast.27, f32[16,128,256]{2,1,0:T(8,128)} %get-tuple-element.17, f32[16,128]{1,0:T(8,128)S(1)} %get-tuple-element.16), kind=kOutput, calls=%fused_computation.36 | convolution fusion | flops 68419584 | bytes 2891776 | tf_op jit(solution)/shard_map/bhrw,brhd->bwhd/dot_general | solution.py:209
  118.5 6.6 %multiply_bitcast_fusion = f32[1,16,128,256]{3,2,1,0:T(8,128)S(1)} fusion(bf16[128,16,64]{0,2,1:T(8,128)(2,1)} %bitcast.27, bf16[256,16,64]{0,2,1:T(8,128)(2,1)S(1)} %bitcast.151, f32[16,128,256]{2,1,0:T(8,128)} %get-tuple-element.17, f32[16,128]{1,0:T(8,128)S(1)} %get-tuple-element.16), kind=kOutput, calls=%fused_computation.27 | convolution fusion | flops 137365760 | bytes 4988928 | tf_op jit(solution)/shard_map/sub | solution.py:206
  125.2 0.3 fusion.34
  125.5 0.3 fusion.22
  125.9 1.1 copy.61
  126.9 9.5 %all-to-all-start.2 = ((bf16[256,16,2,64]{0,3,2,1:T(8,128)(2,1)}), bf16[256,16,2,64]{0,3,2,1:T(8,128)(2,1)S(1)}, u32[]{:S(2)}, u32[]{:S(2)}) async-start(bf16[256,16,2,64]{0,3,2,1:T(8,128)(2,1)} %copy.61), calls=%async_computation.2 | async-start | bytes 2097152 | tf_op jit(solution)/shard_map/all_to_all | solution.py:220
  136.5 1.3 compare_select_fusion.1
  137.8 11.3 %all-to-all-done.2 = bf16[256,16,2,64]{0,3,2,1:T(8,128)(2,1)S(1)} async-done(((bf16[256,16,2,64]{0,3,2,1:T(8,128)(2,1)}), bf16[256,16,2,64]{0,3,2,1:T(8,128)(2,1)S(1)}, u32[]{:S(2)}, u32[]{:S(2)}) %all-to-all-start.2) | async-done | bytes 1048608 | tf_op jit(solution)/shard_map/all_to_all | solution.py:220
  149.1 0.3 bitcast_convert_fusion
  149.3 0.3 fusion.56
  149.7 0.6 fusion.33
  150.3 0.3 copy.62
  150.6 4.4 %fusion.5 = f32[1024,128]{1,0:T(8,128)S(1)} fusion(bf16[2048,128]{1,0:T(8,128)(2,1)S(1)} %bitcast.152, bf16[1024,1024]{1,0:T(8,128)(2,1)} %maximum_select_fusion.2, bf16[1024,1024]{1,0:T(8,128)(2,1)} %collective-permute-done.3, pred[]{:T(512)S(6)} %ne.12), kind=kOutput, calls=%fused_computation.9 | convolution fusion | flops 555745280 | bytes 5242881 | tf_op jit(solution)/shard_map/dot_general | solution.py:236
  154.9 0.1 reshape.407
  155.1 0.5 all_to_all.35
  155.6 42.1 %all_to_all.41 = f32[256,1,640]{2,1,0:T(1,128)S(1)} all-to-all(f32[256,1,640]{2,1,0:T(1,128)S(1)} %all_to_all.35), channel_id=1, replica_groups=mesh['dp'=16,'seq'=16] {'dp','seq'}, dimensions={0} | all-to-all | bytes 1310720 | tf_op jit(solution)/shard_map/all_to_all | solution.py:245
  197.8 0.6 fusion.59
  199.1 0.1 mul.117
  199.2 0.7 reshape.409
  (41 shorter events, 0.7 us)
Async XLA Ops:
  7.2 75.4 %copy-start = (bf16[1024,1024]{1,0:T(8,128)(2,1)S(1)}, bf16[1024,1024]{1,0:T(8,128)(2,1)}, u32[]{:S(2)}) copy-start(bf16[1024,1024]{1,0:T(8,128)(2,1)} %param.17) | copy-start | bytes 6291460
  7.2 23.4 %copy-start.2 = (bf16[1,128,1024]{2,1,0:T(8,128)(2,1)S(1)}, bf16[1,128,1024]{2,1,0:T(8,128)(2,1)}, u32[]{:S(2)}) copy-start(bf16[1,128,1024]{2,1,0:T(8,128)(2,1)} %param.10) | copy-start | bytes 786436
  7.2 23.4 %copy-start.3 = (bf16[1,128,1024]{2,1,0:T(8,128)(2,1)S(1)}, bf16[1,128,1024]{2,1,0:T(8,128)(2,1)}, u32[]{:S(2)}) copy-start(bf16[1,128,1024]{2,1,0:T(8,128)(2,1)} %param.11) | copy-start | bytes 786436
  7.2 23.6 %copy-start.6 = (f32[1024]{0:T(1024)S(1)}, f32[1024]{0:T(1024)}, u32[]{:S(2)}) copy-start(f32[1024]{0:T(1024)} %param.15) | copy-start | bytes 12292
  7.2 85.4 %all-gather.2.cloned.1.call-start = ((), (), s32[]{:S(2)}) async-start(), calls=%async_computation.4 | async-start | bytes 8912896 | tf_op jit(solution)/shard_map/all_gather | solution.py:135
  31.0 13.5 %collective-permute-start = (bf16[128,1024]{1,0:T(8,128)(2,1)S(1)}, bf16[128,1024]{1,0:T(8,128)(2,1)S(1)}, u32[]{:S(2)}, u32[]{:S(2)}) collective-permute-start(bf16[128,1024]{1,0:T(8,128)(2,1)S(1)} %fusion.45), channel_id=1, source_target_pairs={{0,1},{1,0},{2,3},{3,2},{4,5},{5,4},{6,7},{7,6},{8,9},{9,8},{10,11... | collective-permute-start | bytes 786440 | tf_op jit(solution)/shard_map/ppermute | solution.py:34
  36.0 8.4 %copy-start.5 = (s32[1,2048]{1,0:T(1,128)S(1)}, s32[1,2048]{1,0:T(1,128)}, u32[]{:S(2)}) copy-start(s32[1,2048]{1,0:T(1,128)} %param.13) | copy-start | bytes 24580
  39.3 14.8 %all-to-all-start = ((bf16[1,128,3,16,64]{1,4,2,0,3:T(8,128)(2,1)}), bf16[1,128,3,16,64]{1,4,2,0,3:T(8,128)(2,1)S(1)}, u32[]{:S(2)}, u32[]{:S(2)}) async-start(bf16[1,128,3,16,64]{1,4,2,0,3:T(8,128)(2,1)} %copy.57), calls=%async_computation | async-start | bytes 1572864 | tf_op jit(solution)/shard_map/all_to_all | solution.py:148
  45.5 16.0 %collective-permute-start.1 = (bf16[256,1024]{1,0:T(8,128)(2,1)}, bf16[256,1024]{1,0:T(8,128)(2,1)}, u32[]{:S(2)}, u32[]{:S(2)}) collective-permute-start(bf16[256,1024]{1,0:T(8,128)(2,1)} %maximum_select_fusion.4), channel_id=1, source_target_pairs={{0,2},{1,3},{2,0},{3,1},{4,6},{5,7},{6,4},{7,5},{8,10},{9,11},{10,... | collective-permute-start | bytes 1572872 | tf_op jit(solution)/shard_map/ppermute | solution.py:34
  63.5 21.3 %collective-permute-start.2 = (bf16[512,1024]{1,0:T(8,128)(2,1)S(1)}, bf16[512,1024]{1,0:T(8,128)(2,1)}, u32[]{:S(2)}, u32[]{:S(2)}) collective-permute-start(bf16[512,1024]{1,0:T(8,128)(2,1)S(1)} %maximum_select_fusion.3), channel_id=1, source_target_pairs={{0,4},{1,5},{2,6},{3,7},{4,0},{5,1},{6,2},{7,3},{8,12},{9,13},{10,... | collective-permute-start | bytes 3145736 | tf_op jit(solution)/shard_map/ppermute | solution.py:34
  69.4 13.2 %all-to-all-start.1 = ((bf16[1,16,128,1,64]{2,4,3,0,1:T(8,128)(2,1)}), bf16[1,16,128,1,64]{2,4,3,0,1:T(8,128)(2,1)}, u32[]{:S(2)}, u32[]{:S(2)}) async-start(bf16[1,16,128,1,64]{2,4,3,0,1:T(8,128)(2,1)} %copy.59), calls=%async_computation.1 | async-start | bytes 524288 | tf_op jit(solution)/shard_map/all_to_all | solution.py:152
  88.8 61.8 %collective-permute-start.3 = (bf16[1024,1024]{1,0:T(8,128)(2,1)}, bf16[1024,1024]{1,0:T(8,128)(2,1)}, u32[]{:S(2)}, u32[]{:S(2)}) collective-permute-start(bf16[1024,1024]{1,0:T(8,128)(2,1)} %maximum_select_fusion.2), channel_id=1, source_target_pairs={{0,8},{1,9},{2,10},{3,11},{4,12},{5,13},{6,14},{7,15},{8,0},{9,1},... | collective-permute-start | bytes 6291464 | tf_op jit(solution)/shard_map/ppermute | solution.py:34
  96.8 7.8 %collective-permute-start.5 = (bf16[1,64,2048]{2,1,0:T(8,128)(2,1)S(1)}, bf16[1,64,2048]{2,1,0:T(8,128)(2,1)S(1)}, u32[]{:S(2)}, u32[]{:S(2)}) collective-permute-start(bf16[1,64,2048]{2,1,0:T(8,128)(2,1)S(1)} %get-tuple-element.11), channel_id=1, source_target_pairs={{1,0},{2,1},{3,2},{4,3},{5,4},{6,5},{7,6},{8,7},{9,8},{10,9},{11,1... | collective-permute-start | bytes 786440 | tf_op jit(solution)/shard_map/ppermute | solution.py:23
  98.1 7.3 %collective-permute-start.4 = (bf16[1,64,2048]{2,1,0:T(8,128)(2,1)S(1)}, bf16[1,64,2048]{2,1,0:T(8,128)(2,1)S(1)}, u32[]{:S(2)}, u32[]{:S(2)}) collective-permute-start(bf16[1,64,2048]{2,1,0:T(8,128)(2,1)S(1)} %get-tuple-element.10), channel_id=1, source_target_pairs={{0,1},{1,2},{2,3},{3,4},{4,5},{5,6},{6,7},{7,8},{8,9},{9,10},{10,1... | collective-permute-start | bytes 786440 | tf_op jit(solution)/shard_map/ppermute | solution.py:20
  108.1 2.2 %copy-start.4 = (f32[128,1024]{1,0:T(8,128)S(1)}, f32[128,1024]{1,0:T(8,128)}, u32[]{:S(2)}) copy-start(f32[128,1024]{1,0:T(8,128)} %convolution_bitcast_fusion) | copy-start | bytes 1572868
  126.9 22.1 %all-to-all-start.2 = ((bf16[256,16,2,64]{0,3,2,1:T(8,128)(2,1)}), bf16[256,16,2,64]{0,3,2,1:T(8,128)(2,1)S(1)}, u32[]{:S(2)}, u32[]{:S(2)}) async-start(bf16[256,16,2,64]{0,3,2,1:T(8,128)(2,1)} %copy.61), calls=%async_computation.2 | async-start | bytes 2097152 | tf_op jit(solution)/shard_map/all_to_all | solution.py:220
  155.1 46.1 %copy-start.1 = (bf16[1024,1024]{1,0:T(8,128)(2,1)S(1)}, bf16[1024,1024]{1,0:T(8,128)(2,1)}, u32[]{:S(2)}) copy-start(bf16[1024,1024]{1,0:T(8,128)(2,1)} %param.17) | copy-start | bytes 6291460
Sparse Core Ops, SparseCore 0:
  30.0 62.5 all-gather.1
